TPU v7x, 32 devices: a whole 2x2x4 slice. The times are simulated.
32 devices in a mesh: dp: 8 (over z, core), tensor: 4 (over y, x).
Axes of the slice: x: 2, y: 2, z: 4, core: 2. Of those that a mesh axis runs over, the one named last changes fastest.
Arguments:
- t_index: int32 [8], P('dp'), may hold values from 0 to 999
- cond_slot: int32 [8], P('dp'), may hold values from 0 to 1
- positions: int32 [8, 3, 512], P('dp'), may hold values from 0 to 63, as said below
- latent: bfloat16 [8, 512, 5120], P('dp', 'tensor'), may hold values from -6 to 6
- teacher_query: bfloat16 [2, 8, 512, 4096], P(None, 'dp', None, 'tensor'), may hold values from -6 to 6
- teacher_key: bfloat16 [2, 8, 512, 4096], P(None, 'dp', None, 'tensor'), may hold values from -6 to 6
- teacher_value: bfloat16 [2, 8, 512, 4096], P(None, 'dp', None, 'tensor'), may hold values from -6 to 6
- student_query: bfloat16 [8, 512, 4096], P('dp', 'tensor'), may hold values from -6 to 6
- student_key: bfloat16 [8, 512, 4096], P('dp', 'tensor'), may hold values from -6 to 6
- student_value: bfloat16 [8, 512, 4096], P('dp', 'tensor'), may hold values from -6 to 6
- query_tangent: bfloat16 [8, 512, 4096], P('dp', 'tensor'), may hold values from -6 to 6
- key_tangent: bfloat16 [8, 512, 4096], P('dp', 'tensor'), may hold values from -6 to 6
- value_tangent: bfloat16 [8, 512, 4096], P('dp', 'tensor'), may hold values from -6 to 6
- teacher_out: bfloat16 [4096, 5120], P('tensor', 'dp'), may hold values from -0.375 to 0.375
- student_out: bfloat16 [4096, 5120], P('tensor', 'dp'), may hold values from -0.375 to 0.375
Outputs:
- target: bfloat16 [8, 512, 5120], P('dp', 'tensor')
- gradient: float32 [4096, 5120], P('tensor', 'dp')
Inputs may be any that keep to these rules, and one draw needn't show every extreme that they name: `positions`: within each clip, tokens 64 m and 64 m + 1 have equal coordinates on all three axes.
All inputs are finite; a program needn't handle non-finite values.
Results may differ from a plain program's by a relative error of at most 0.015.
Values may be sent and summed in bfloat16 or wider, within the bound.
No kernel may reach another device: no remote copies, remote signals or barrier semaphores. Data moves between devices by JAX's collectives and lax.ppermute only.
A program may use at most 192 MiB of HBM per device.

v0:
```python
import math

import jax
import jax.numpy as jnp
from jax import lax
from jax.experimental import pallas as pl
from jax.experimental.pallas import tpu as pltpu
from jax.sharding import PartitionSpec as P

HD = 128
STEPS = 1000


sigma_data = 0.5
guidance = 5.0


def rope_angles(coords):
    half_size = HD // 2
    sixth = HD // 6
    first_pairs = half_size - 2 * sixth
    pair_index = jnp.arange(half_size)
    axis_id = (pair_index >= first_pairs).astype(jnp.int32) + (
        pair_index >= first_pairs + sixth
    ).astype(jnp.int32)
    offset = jnp.where(axis_id == 0, 0, jnp.where(axis_id == 1, first_pairs, first_pairs + sixth))
    axis_width = jnp.where(axis_id == 0, 2 * first_pairs, 2 * sixth)
    exponent = 2.0 * (pair_index - offset).astype(jnp.float32) / axis_width.astype(jnp.float32)
    frequency = jnp.exp(-exponent * math.log(10000.0))
    angles = jnp.zeros((coords.shape[1], half_size), jnp.float32)
    for which_axis in range(3):
        chosen = jnp.where(axis_id == which_axis, frequency, 0.0)
        angles = angles + coords[which_axis].astype(jnp.float32)[:, None] * chosen[None, :]
    return angles


def rotate_heads(source, angles):
    half_size = source.shape[-1] // 2
    cos_angle = jnp.cos(angles)[:, None, :]
    sin_angle = jnp.sin(angles)[:, None, :]
    front_half = source[..., :half_size]
    back_half = source[..., half_size:]
    return jnp.concatenate(
        [
            front_half * cos_angle - back_half * sin_angle,
            back_half * cos_angle + front_half * sin_angle,
        ],
        axis=-1,
    )


def split_heads(source):
    return source.reshape(source.shape[0], -1, HD)


def rotated(source, angles):
    row_count = source.shape[0]
    return (
        rotate_heads(split_heads(source).astype(jnp.float32), angles)
        .astype(jnp.bfloat16)
        .reshape(row_count, -1)
    )


def softmax_rows(scores):
    row_peak = jnp.max(scores, axis=-1, keepdims=True)
    exponent = jnp.exp(scores - row_peak)
    return exponent / jnp.sum(exponent, axis=-1, keepdims=True)


def attend_plain(queries, key_rows, value_rows):
    scores = jnp.einsum(
        "qhd,khd->hqk", queries, key_rows, preferred_element_type=jnp.float32
    ) * HD ** (-0.5)
    rounded = softmax_rows(scores).astype(jnp.bfloat16)
    return jnp.einsum("hqk,khd->qhd", rounded, value_rows, preferred_element_type=jnp.float32)


def attend_tangent(queries, key_rows, value_rows, query_dir, key_dir, value_dir):
    score_scale = HD ** (-0.5)
    scores = (
        jnp.einsum("qhd,khd->hqk", queries, key_rows, preferred_element_type=jnp.float32)
        * score_scale
    )
    weights = softmax_rows(scores)
    rounded = weights.astype(jnp.bfloat16)
    primal = jnp.einsum("hqk,khd->qhd", rounded, value_rows, preferred_element_type=jnp.float32)
    score_dir = (
        jnp.einsum("qhd,khd->hqk", query_dir, key_rows, preferred_element_type=jnp.float32)
        + jnp.einsum("qhd,khd->hqk", queries, key_dir, preferred_element_type=jnp.float32)
    ) * score_scale
    weight_dir = weights * (score_dir - jnp.sum(weights * score_dir, axis=-1, keepdims=True))
    rounded_dir = weight_dir.astype(jnp.bfloat16)
    tangent = jnp.einsum(
        "hqk,khd->qhd", rounded_dir, value_rows, preferred_element_type=jnp.float32
    ) + jnp.einsum("hqk,khd->qhd", rounded, value_dir, preferred_element_type=jnp.float32)
    return (primal, tangent)


SCORE_SCALE = HD ** (-0.5)


def rope_tables(angles):
    cos_angle = jnp.cos(angles)
    sin_angle = jnp.sin(angles)
    return (
        jnp.concatenate([cos_angle, cos_angle], axis=-1),
        jnp.concatenate([-sin_angle, sin_angle], axis=-1),
    )


def rotate_block(block, cos_ref, sin_ref):
    source = block.astype(jnp.float32)
    swapped = pltpu.roll(source, HD // 2, 1)
    return (source * cos_ref[...] + swapped * sin_ref[...]).astype(jnp.bfloat16)


def scores_of(queries, key_rows):
    return (
        lax.dot_general(
            queries, key_rows, (((1,), (1,)), ((), ())), preferred_element_type=jnp.float32
        )
        * SCORE_SCALE
    )


def softmax_block(scores):
    exponent = jnp.exp(scores - jnp.max(scores, axis=-1, keepdims=True))
    return exponent / jnp.sum(exponent, axis=-1, keepdims=True)


def teacher_kernel(scal, cos_ref, sin_ref, q0, k0, v0, q1, k1, v1, out_ref):
    def attend(q_ref, k_ref, v_ref):
        weights = softmax_block(
            scores_of(rotate_block(q_ref[...], cos_ref, sin_ref), rotate_block(k_ref[...], cos_ref, sin_ref))
        )
        return jnp.dot(weights.astype(jnp.bfloat16), v_ref[...], preferred_element_type=jnp.float32)

    first = attend(q0, k0, v0)
    second = attend(q1, k1, v1)
    pick_first = scal[1] == 0.0
    cond_out = jnp.where(pick_first, first, second)
    uncond_out = jnp.where(pick_first, second, first)
    out_ref[...] = (scal[0] * (uncond_out + guidance * (cond_out - uncond_out))).astype(jnp.bfloat16)


def student_kernel(scal, cos_ref, sin_ref, q, k, v, qt, kt, vt, term_ref, att_ref):
    queries = rotate_block(q[...], cos_ref, sin_ref)
    key_rows = rotate_block(k[...], cos_ref, sin_ref)
    query_dir = rotate_block(qt[...], cos_ref, sin_ref)
    key_dir = rotate_block(kt[...], cos_ref, sin_ref)
    weights = softmax_block(scores_of(queries, key_rows))
    rounded = weights.astype(jnp.bfloat16)
    primal = jnp.dot(rounded, v[...], preferred_element_type=jnp.float32)
    score_dir = (
        lax.dot_general(query_dir, key_rows, (((1,), (1,)), ((), ())), preferred_element_type=jnp.float32)
        + lax.dot_general(queries, key_dir, (((1,), (1,)), ((), ())), preferred_element_type=jnp.float32)
    ) * SCORE_SCALE
    weight_dir = weights * (score_dir - jnp.sum(weights * score_dir, axis=-1, keepdims=True))
    tangent = jnp.dot(weight_dir.astype(jnp.bfloat16), v[...], preferred_element_type=jnp.float32) + jnp.dot(
        rounded, vt[...], preferred_element_type=jnp.float32
    )
    term_ref[...] = (scal[0] * primal - scal[1] * tangent).astype(jnp.bfloat16)
    att_ref[...] = primal.astype(jnp.bfloat16)


def head_call(kernel, scal, tables, operands, outputs):
    seq, cols = outputs[0].shape
    heads = cols // HD
    head_block = pl.BlockSpec((seq, HD), lambda h: (0, h))
    table_block = pl.BlockSpec((seq, HD), lambda h: (0, 0))
    in_specs = [pl.BlockSpec(memory_space=pltpu.SMEM), table_block, table_block]
    for operand in operands:
        if operand.ndim == 2:
            in_specs.append(head_block)
        else:
            in_specs.append(pl.BlockSpec((None, seq, HD), lambda h, s=operand.index: (s, 0, h)))
    return pl.pallas_call(
        kernel,
        grid=(heads,),
        in_specs=in_specs,
        out_specs=[head_block] * len(outputs),
        out_shape=outputs,
        compiler_params=pltpu.CompilerParams(dimension_semantics=("arbitrary",)),
    )(scal, *tables, *[o.array for o in operands])


class Operand:
    def __init__(self, array, index=None):
        self.array = array
        self.index = index
        self.ndim = 2 if index is None else 3


def local(
    t_index,
    cond_slot,
    positions,
    latent,
    teacher_query,
    teacher_key,
    teacher_value,
    student_query,
    student_key,
    student_value,
    query_tangent,
    key_tangent,
    value_tangent,
    teacher_out,
    student_out,
):
    groups = lax.axis_size("tensor")
    seq_local = latent.shape[1]
    seq_whole = seq_local * groups
    row_start = lax.axis_index("tensor") * seq_local
    time_value = 0.2 + 1.2 * (t_index[0].astype(jnp.float32) + 0.5) / STEPS
    cos_time = jnp.cos(time_value)
    sin_time = jnp.sin(time_value)
    angles_whole = rope_angles(positions[0])
    tables = rope_tables(angles_whole)
    arrived = [
        lax.all_to_all(source[0], "tensor", split_axis=1, concat_axis=0, tiled=True)
        for source in (student_query, student_key, student_value, query_tangent, key_tangent, value_tangent)
    ]
    cols = arrived[0].shape[1]
    teacher_scal = jnp.stack(
        [cos_time * cos_time * sigma_data, cond_slot[0].astype(jnp.float32)]
    )
    t_q = teacher_query.reshape((2,) + teacher_query.shape[2:])
    t_k = teacher_key.reshape((2,) + teacher_key.shape[2:])
    t_v = teacher_value.reshape((2,) + teacher_value.shape[2:])
    (teacher_term,) = head_call(
        teacher_kernel,
        teacher_scal,
        tables,
        [Operand(t_q, 0), Operand(t_k, 0), Operand(t_v, 0), Operand(t_q, 1), Operand(t_k, 1), Operand(t_v, 1)],
        [jax.ShapeDtypeStruct((seq_whole, cols), jnp.bfloat16)],
    )
    student_scal = jnp.stack(
        [-(cos_time * cos_time) * sigma_data, cos_time * sin_time * sigma_data]
    )
    student_term, attended = head_call(
        student_kernel,
        student_scal,
        tables,
        [Operand(a) for a in arrived],
        [jax.ShapeDtypeStruct((seq_whole, cols), jnp.bfloat16)] * 2,
    )
    stacked = jnp.stack([student_out, teacher_out])
    pieces = lax.all_gather(stacked, "dp", axis=2, tiled=True)
    partial_value = jnp.dot(student_term, pieces[0], preferred_element_type=jnp.float32) + jnp.dot(
        teacher_term, pieces[1], preferred_element_type=jnp.float32
    )
    latent_weight = cos_time * sin_time
    pieces_in = lax.all_to_all(
        partial_value.astype(jnp.bfloat16).reshape(groups, seq_local, -1),
        "tensor",
        split_axis=0,
        concat_axis=0,
        tiled=True,
    )
    velocity = jnp.sum(pieces_in.astype(jnp.float32), axis=0)
    target = (velocity - latent_weight * latent[0].astype(jnp.float32)).astype(jnp.bfloat16)
    clips = lax.axis_size("dp")
    width = target.shape[1] // clips
    attended_all = lax.all_gather(attended, "dp", axis=0, tiled=False)
    columns = lax.all_to_all(
        target.reshape(seq_local, clips, width), "dp", split_axis=1, concat_axis=1, tiled=True
    )
    columns = lax.all_gather(columns, "tensor", axis=0, tiled=True)
    grad_scale = -2.0 / math.sqrt(clips * seq_whole)
    terms = jnp.einsum(
        "csi,scd->cid", attended_all, columns, preferred_element_type=jnp.float32
    )
    gradient = jnp.sum((grad_scale * terms).astype(jnp.bfloat16).astype(jnp.float32), axis=0)
    return (target[None], gradient)


def solution(mesh):
    placed = (
        P("dp"),
        P("dp"),
        P("dp", None, None),
        P("dp", "tensor", None),
        P(None, "dp", None, "tensor"),
        P(None, "dp", None, "tensor"),
        P(None, "dp", None, "tensor"),
        P("dp", "tensor", None),
        P("dp", "tensor", None),
        P("dp", "tensor", None),
        P("dp", "tensor", None),
        P("dp", "tensor", None),
        P("dp", "tensor", None),
        P("tensor", "dp"),
        P("tensor", "dp"),
    )
    return jax.shard_map(
        local,
        mesh=mesh,
        in_specs=placed,
        out_specs=(P("dp", "tensor", None), P("tensor", "dp")),
        check_vma=False,
    )
```

profile of v0, /device:TPU:0, one launch (start us, length us, event | category | flops | bytes accessed | tf_op | source)
XLA Modules:
  0.0 411.9 jit_solution(18381937901942233341)
XLA Ops:
  7.2 3.5 pad_maximum_fusion
  14.0 5.2 %all-to-all-start.2 = ((bf16[128,4,1024]{2,0,1:T(8,128)(2,1)}), bf16[128,4,1024]{2,0,1:T(8,128)(2,1)S(1)}, u32[]{:S(2)}, u32[]{:S(2)}) async-start(bf16[128,4,1024]{2,0,1:T(8,128)(2,1)} %copy.49), calls=%async_computation.2 | async-start | bytes 2097152 | tf_op jit(solution)/shard_map/all_to_all | solution.py:222
  21.2 11.5 %all-to-all-done.2 = bf16[128,4,1024]{2,0,1:T(8,128)(2,1)S(1)} async-done(((bf16[128,4,1024]{2,0,1:T(8,128)(2,1)}), bf16[128,4,1024]{2,0,1:T(8,128)(2,1)S(1)}, u32[]{:S(2)}, u32[]{:S(2)}) %all-to-all-start.2) | async-done | bytes 1048608 | tf_op jit(solution)/shard_map/all_to_all | solution.py:222
  32.8 3.5 all-to-all-start.3
  36.3 1.9 all_to_all.106
  39.5 10.0 %all-to-all-done.3 = bf16[128,4,1024]{2,0,1:T(8,128)(2,1)S(1)} async-done(((bf16[128,4,1024]{2,0,1:T(8,128)(2,1)}), bf16[128,4,1024]{2,0,1:T(8,128)(2,1)S(1)}, u32[]{:S(2)}, u32[]{:S(2)}) %all-to-all-start.3) | async-done | bytes 1048608 | tf_op jit(solution)/shard_map/all_to_all | solution.py:222
  49.5 3.5 all-to-all-start.4
  53.0 1.9 all_to_all.110
  56.3 9.9 %all-to-all-done.4 = bf16[128,4,1024]{2,0,1:T(8,128)(2,1)S(1)} async-done(((bf16[128,4,1024]{2,0,1:T(8,128)(2,1)}), bf16[128,4,1024]{2,0,1:T(8,128)(2,1)S(1)}, u32[]{:S(2)}, u32[]{:S(2)}) %all-to-all-start.4) | async-done | bytes 1048608 | tf_op jit(solution)/shard_map/all_to_all | solution.py:222
  66.2 3.5 all-to-all-start.5
  69.7 1.9 all_to_all.90
  72.8 10.0 %all-to-all-done.5 = bf16[128,4,1024]{2,0,1:T(8,128)(2,1)S(1)} async-done(((bf16[128,4,1024]{2,0,1:T(8,128)(2,1)}), bf16[128,4,1024]{2,0,1:T(8,128)(2,1)S(1)}, u32[]{:S(2)}, u32[]{:S(2)}) %all-to-all-start.5) | async-done | bytes 1048608 | tf_op jit(solution)/shard_map/all_to_all | solution.py:222
  82.8 3.5 all-to-all-start
  87.2 1.9 all_to_all.94
  90.5 9.1 %all-to-all-done = bf16[128,4,1024]{2,0,1:T(8,128)(2,1)S(1)} async-done(((bf16[128,4,1024]{2,0,1:T(8,128)(2,1)}), bf16[128,4,1024]{2,0,1:T(8,128)(2,1)S(1)}, u32[]{:S(2)}, u32[]{:S(2)}) %all-to-all-start) | async-done | bytes 1048608 | tf_op jit(solution)/shard_map/all_to_all | solution.py:222
  99.5 3.5 all-to-all-start.1
  105.8 10.4 %all-to-all-done.1 = bf16[128,4,1024]{2,0,1:T(8,128)(2,1)S(1)} async-done(((bf16[128,4,1024]{2,0,1:T(8,128)(2,1)}), bf16[128,4,1024]{2,0,1:T(8,128)(2,1)S(1)}, u32[]{:S(2)}, u32[]{:S(2)}) %all-to-all-start.1) | async-done | bytes 1048608 | tf_op jit(solution)/shard_map/all_to_all | solution.py:222
  117.2 15.9 %shard_map.158 = (bf16[512,1024]{1,0:T(8,128)(2,1)}, bf16[512,1024]{1,0:T(8,128)(2,1)}) custom-call(f32[2]{0:T(128)} %pad_maximum_fusion.3.scal, f32[512,128]{1,0:T(8,128)} %get-tuple-element.16.cos_ref, f32[512,128]{1,0:T(8,128)} %get-tuple-element.17.sin_ref, bf16[512,1024]{1,0:T(8,128)(2,1)} %bitcast.61, bf16[512,1024]{1,0:T(8,128)(2,1)} %bitcast.62, ...), custom_call_target="tpu_custom_call" | custom-call | tf_op jit(solution)/shard_map/pallas_call | solution.py:178
  134.7 15.2 %shard_map.159 = bf16[512,1024]{1,0:T(8,128)(2,1)} custom-call(f32[2]{0:T(128)} %pad_maximum_fusion.4.scal, f32[512,128]{1,0:T(8,128)} %get-tuple-element.16.cos_ref, f32[512,128]{1,0:T(8,128)} %get-tuple-element.17.sin_ref, bf16[2,512,1024]{2,1,0:T(8,128)(2,1)} %bitcast.50, bf16[2,512,1024]{2,1,0:T(8,128)(2,1)} %bitcast.52, bf16[2,512,1024]{2,1,0:T(8,128)(2,1)} %bitcast.54, ...), custom_call_target="tpu_custom_call" | custom-call | tf_op jit(solution)/shard_map/pallas_call | solution.py:178
  149.9 49.0 %all-gather.5.cloned.1.call-done = bf16[2,1024,5120]{2,1,0:T(8,128)(2,1)} async-done(((bf16[2,1024,640]{2,1,0:T(8,128)(2,1)}), bf16[2,1024,5120]{2,1,0:T(8,128)(2,1)}) %all-gather.5.cloned.1.call-update) | async-done | bytes 20971536 | tf_op jit(solution)/shard_map/all_gather | solution.py:250
  199.0 8.6 %fusion = f32[512,5120]{1,0:T(8,128)S(1)} fusion(bf16[512,1024]{1,0:T(8,128)(2,1)} %shard_map.159, bf16[2,1024,5120]{2,1,0:T(8,128)(2,1)} %all-gather.5.cloned.1.call-done), kind=kOutput, calls=%fused_computation.3 | convolution fusion | flops 5368709120 | bytes 22020096 | tf_op jit(solution)/shard_map/dot_general | solution.py:251
  207.5 10.6 %add_convert_fusion = bf16[512,5120]{1,0:T(8,128)(2,1)S(1)} fusion(f32[512,5120]{1,0:T(8,128)S(1)} %fusion, bf16[512,1024]{1,0:T(8,128)(2,1)S(1)} %copy-done.9, bf16[2,1024,5120]{2,1,0:T(8,128)(2,1)} %all-gather.5.cloned.1.call-done), kind=kOutput, calls=%fused_computation.7 | convolution fusion | flops 5373952000 | bytes 27262976 | tf_op jit(solution)/shard_map/dot_general | solution.py:251
  218.2 63.0 %all_to_all.124 = bf16[4,128,5120]{2,1,0:T(8,128)(2,1)S(1)} all-to-all(bf16[4,128,5120]{2,1,0:T(8,128)(2,1)S(1)} %bitcast.56), channel_id=1, replica_groups=mesh['dp'=8,'tensor'=4] {'tensor'}, dimensions={0} | all-to-all | bytes 10485760 | tf_op jit(solution)/shard_map/all_to_all | solution.py:255
  282.1 2.1 copy.53
  284.3 3.6 convert_multiply_fusion
  287.9 3.3 copy.54
  291.2 2.1 copy.56
  293.3 3.2 copy.55
  296.5 2.1 subtract_convert_fusion
  298.6 35.3 %all_to_all.125 = bf16[128,8,640]{2,0,1:T(8,128)(2,1)} all-to-all(bf16[128,8,640]{2,0,1:T(8,128)(2,1)S(1)} %subtract_convert_fusion), channel_id=1, replica_groups=mesh['dp'=8,'tensor'=4] {'dp'}, dimensions={1} | all-to-all | bytes 2621440 | tf_op jit(solution)/shard_map/all_to_all | solution.py:267
  334.0 58.9 %all-gather.7.cloned.1.call-done = bf16[512,8,640]{2,0,1:T(8,128)(2,1)} async-done(((bf16[128,8,640]{2,0,1:T(8,128)(2,1)}), bf16[512,8,640]{2,0,1:T(8,128)(2,1)}) %all-gather.7.cloned.1.call-update) | async-done | bytes 5242896 | tf_op jit(solution)/shard_map/all_gather | solution.py:270
  392.9 12.4 %convert_reduce_fusion = f32[1024,640]{1,0:T(8,128)} fusion(bf16[8,512,1024]{2,1,0:T(8,128)(2,1)} %bitcast.68, bf16[512,8,640]{2,0,1:T(8,128)(2,1)} %all-gather.7.cloned.1.call-done), kind=kOutput, calls=%fused_computation | convolution fusion | flops 5389025280 | bytes 16252928 | tf_op jit(solution)/shard_map/csi,scd->cid/dot_general | solution.py:272
  (44 shorter events, 16.5 us)
Async XLA Ops:
  7.2 191.8 %all-gather.5.cloned.1.call-start = ((), (), s32[]{:S(2)}) async-start(), calls=%async_computation.8 | async-start | bytes 23592960 | tf_op jit(solution)/shard_map/all_gather | solution.py:250
  10.7 1.2 copy-start.6
  11.9 7.2 %copy-start.7 = (bf16[1,128,4096]{2,1,0:T(8,128)(2,1)S(1)}, bf16[1,128,4096]{2,1,0:T(8,128)(2,1)}, u32[]{:S(2)}) copy-start(bf16[1,128,4096]{2,1,0:T(8,128)(2,1)} %param.25) | copy-start | bytes 3145732
  14.0 18.8 %all-to-all-start.2 = ((bf16[128,4,1024]{2,0,1:T(8,128)(2,1)}), bf16[128,4,1024]{2,0,1:T(8,128)(2,1)S(1)}, u32[]{:S(2)}, u32[]{:S(2)}) async-start(bf16[128,4,1024]{2,0,1:T(8,128)(2,1)} %copy.49), calls=%async_computation.2 | async-start | bytes 2097152 | tf_op jit(solution)/shard_map/all_to_all | solution.py:222
  32.8 6.7 %copy-start = (bf16[128,4,1024]{2,0,1:T(8,128)(2,1)}, bf16[128,4,1024]{2,0,1:T(8,128)(2,1)S(1)}, u32[]{:S(2)}) copy-start(bf16[128,4,1024]{2,0,1:T(8,128)(2,1)S(1)} %all-to-all-done.2) | copy-start | bytes 3145732
  32.8 16.7 %all-to-all-start.3 = ((bf16[128,4,1024]{2,0,1:T(8,128)(2,1)}), bf16[128,4,1024]{2,0,1:T(8,128)(2,1)S(1)}, u32[]{:S(2)}, u32[]{:S(2)}) async-start(bf16[128,4,1024]{2,0,1:T(8,128)(2,1)} %copy.50), calls=%async_computation.3 | async-start | bytes 2097152 | tf_op jit(solution)/shard_map/all_to_all | solution.py:222
  49.5 6.8 %copy-start.1 = (bf16[128,4,1024]{2,0,1:T(8,128)(2,1)}, bf16[128,4,1024]{2,0,1:T(8,128)(2,1)S(1)}, u32[]{:S(2)}) copy-start(bf16[128,4,1024]{2,0,1:T(8,128)(2,1)S(1)} %all-to-all-done.3) | copy-start | bytes 3145732
  49.5 16.7 %all-to-all-start.4 = ((bf16[128,4,1024]{2,0,1:T(8,128)(2,1)}), bf16[128,4,1024]{2,0,1:T(8,128)(2,1)S(1)}, u32[]{:S(2)}, u32[]{:S(2)}) async-start(bf16[128,4,1024]{2,0,1:T(8,128)(2,1)} %copy.51), calls=%async_computation.4 | async-start | bytes 2097152 | tf_op jit(solution)/shard_map/all_to_all | solution.py:222
  66.2 6.7 %copy-start.2 = (bf16[128,4,1024]{2,0,1:T(8,128)(2,1)}, bf16[128,4,1024]{2,0,1:T(8,128)(2,1)S(1)}, u32[]{:S(2)}) copy-start(bf16[128,4,1024]{2,0,1:T(8,128)(2,1)S(1)} %all-to-all-done.4) | copy-start | bytes 3145732
  66.2 16.7 %all-to-all-start.5 = ((bf16[128,4,1024]{2,0,1:T(8,128)(2,1)}), bf16[128,4,1024]{2,0,1:T(8,128)(2,1)S(1)}, u32[]{:S(2)}, u32[]{:S(2)}) async-start(bf16[128,4,1024]{2,0,1:T(8,128)(2,1)} %copy.52), calls=%async_computation.5 | async-start | bytes 2097152 | tf_op jit(solution)/shard_map/all_to_all | solution.py:222
  82.8 7.6 %copy-start.3 = (bf16[128,4,1024]{2,0,1:T(8,128)(2,1)}, bf16[128,4,1024]{2,0,1:T(8,128)(2,1)S(1)}, u32[]{:S(2)}) copy-start(bf16[128,4,1024]{2,0,1:T(8,128)(2,1)S(1)} %all-to-all-done.5) | copy-start | bytes 3145732
  82.8 16.7 %all-to-all-start = ((bf16[128,4,1024]{2,0,1:T(8,128)(2,1)}), bf16[128,4,1024]{2,0,1:T(8,128)(2,1)S(1)}, u32[]{:S(2)}, u32[]{:S(2)}) async-start(bf16[128,4,1024]{2,0,1:T(8,128)(2,1)} %copy.47), calls=%async_computation | async-start | bytes 2097152 | tf_op jit(solution)/shard_map/all_to_all | solution.py:222
  89.0 14.7 %copy-start.8 = (s32[1,3,512]{2,0,1:T(1,128)S(1)}, s32[1,3,512]{2,0,1:T(1,128)}, u32[]{:S(2)}) copy-start(s32[1,3,512]{2,0,1:T(1,128)} %param.17) | copy-start | bytes 18436
  99.5 16.7 %copy-start.4 = (bf16[128,4,1024]{2,0,1:T(8,128)(2,1)}, bf16[128,4,1024]{2,0,1:T(8,128)(2,1)S(1)}, u32[]{:S(2)}) copy-start(bf16[128,4,1024]{2,0,1:T(8,128)(2,1)S(1)} %all-to-all-done) | copy-start | bytes 3145732
  99.5 16.7 %all-to-all-start.1 = ((bf16[128,4,1024]{2,0,1:T(8,128)(2,1)}), bf16[128,4,1024]{2,0,1:T(8,128)(2,1)S(1)}, u32[]{:S(2)}, u32[]{:S(2)}) async-start(bf16[128,4,1024]{2,0,1:T(8,128)(2,1)} %copy.48), calls=%async_computation.1 | async-start | bytes 2097152 | tf_op jit(solution)/shard_map/all_to_all | solution.py:222
  103.0 231.0 %all-gather.9.cloned.1.call-start = ((), (), s32[]{:S(2)}) async-start(), calls=%async_computation.10 | async-start | bytes 9437184 | tf_op jit(solution)/shard_map/all_gather | solution.py:266
  116.2 1.1 copy-start.5
  133.2 259.8 %all-gather.7.cloned.1.call-start = ((), (), s32[]{:S(2)}) async-start(), calls=%async_computation.9 | async-start | bytes 6553600 | tf_op jit(solution)/shard_map/all_gather | solution.py:270
  149.9 57.6 %copy-start.9 = (bf16[512,1024]{1,0:T(8,128)(2,1)S(1)}, bf16[512,1024]{1,0:T(8,128)(2,1)}, u32[]{:S(2)}) copy-start(bf16[512,1024]{1,0:T(8,128)(2,1)} %get-tuple-element.4) | copy-start | bytes 3145732
Sparse Core Ops, SparseCore 0:
  10.8 188.0 all-gather.4
  200.6 80.2 all-gather.8
  334.1 58.7 all-gather.6
where the time goes:
time: 413 us; the launch traced here: 412 us
  waiting for transfers between devices  169 us (41%)
  blocking collectives  98.4 us (24%)
  matrix products  31.6 us (8%)
  Pallas kernels  31.1 us (8%)
  local copies, waits for them, and re-layouts  29.9 us (7%)
  starting transfers between devices  23 us (6%)
  between operations  15.4 us (4%)
  other arithmetic  13.5 us (3%)
    all_to_all x1, blocking collectives, local(): lax.all_to_all(partial_value.astype(jnp.bfloat16).reshape(groups, seq_loc...  63 us
    all_to_all x6, waiting for transfers between devices, local(): lax.all_to_all(source[0], 'tensor', split_axis=1, concat_axis=0, tiled=True)  60.9 us
    all_gather x1, waiting for transfers between devices, local(): columns = lax.all_gather(columns, 'tensor', axis=0, tiled=True)  58.9 us
    all_gather x1, waiting for transfers between devices, local(): pieces = lax.all_gather(stacked, 'dp', axis=2, tiled=True)  49 us
    all_to_all x1, blocking collectives, local(): lax.all_to_all(target.reshape(seq_local, clips, width), 'dp', split_axis=...  35.3 us
    pallas_call x2, Pallas kernels, head_call(): pl.pallas_call(kernel, grid=(heads,), in_specs=in_specs, out_specs=[head_...  31.1 us
    all_to_all x6, starting transfers between devices, local(): lax.all_to_all(source[0], 'tensor', split_axis=1, concat_axis=0, tiled=True)  22.7 us
    all_to_all x12, local copies, waits for them, and re-layouts, local(): lax.all_to_all(source[0], 'tensor', split_axis=1, concat_axis=0, tiled=True)  16.9 us
  transfers between devices with their start and end apart: 9, of which 8 were waited for; matrix products, arithmetic and copies ran while one was open for 12% of the time, Pallas kernels for 8%

commit v1 on v0

--- a/solution.py
+++ b/solution.py
@@ -218,11 +218,7 @@
     sin_time = jnp.sin(time_value)
     angles_whole = rope_angles(positions[0])
     tables = rope_tables(angles_whole)
-    arrived = [
-        lax.all_to_all(source[0], "tensor", split_axis=1, concat_axis=0, tiled=True)
-        for source in (student_query, student_key, student_value, query_tangent, key_tangent, value_tangent)
-    ]
-    cols = arrived[0].shape[1]
+    cols = teacher_query.shape[3]
     teacher_scal = jnp.stack(
         [cos_time * cos_time * sigma_data, cond_slot[0].astype(jnp.float32)]
     )
@@ -236,6 +232,16 @@
         [Operand(t_q, 0), Operand(t_k, 0), Operand(t_v, 0), Operand(t_q, 1), Operand(t_k, 1), Operand(t_v, 1)],
         [jax.ShapeDtypeStruct((seq_whole, cols), jnp.bfloat16)],
     )
+    teacher_term, sources = lax.optimization_barrier(
+        (teacher_term, (student_query, student_key, student_value, query_tangent, key_tangent, value_tangent))
+    )
+    teacher_all = lax.all_gather(teacher_term, "dp", axis=0, tiled=False)
+    arrived = [
+        lax.all_to_all(source[0], "tensor", split_axis=1, concat_axis=0, tiled=True)
+        for source in sources[:-1]
+    ]
+    teacher_all, last = lax.optimization_barrier((teacher_all, sources[-1]))
+    arrived.append(lax.all_to_all(last[0], "tensor", split_axis=1, concat_axis=0, tiled=True))
     student_scal = jnp.stack(
         [-(cos_time * cos_time) * sigma_data, cos_time * sin_time * sigma_data]
     )
@@ -246,31 +252,38 @@
         [Operand(a) for a in arrived],
         [jax.ShapeDtypeStruct((seq_whole, cols), jnp.bfloat16)] * 2,
     )
-    stacked = jnp.stack([student_out, teacher_out])
-    pieces = lax.all_gather(stacked, "dp", axis=2, tiled=True)
-    partial_value = jnp.dot(student_term, pieces[0], preferred_element_type=jnp.float32) + jnp.dot(
-        teacher_term, pieces[1], preferred_element_type=jnp.float32
-    )
-    latent_weight = cos_time * sin_time
+    clips = lax.axis_size("dp")
+    width = latent.shape[2] // clips
+    times_all = lax.all_gather(t_index, "dp", axis=0, tiled=True)
+    time_all = 0.2 + 1.2 * (times_all.astype(jnp.float32) + 0.5) / STEPS
+    latent_weight = (jnp.cos(time_all) * jnp.sin(time_all))[:, None, None]
+    latent_cols = lax.all_to_all(
+        latent[0].reshape(seq_local, clips, width), "dp", split_axis=1, concat_axis=1, tiled=True
+    )
+    student_all = lax.all_gather(student_term, "dp", axis=0, tiled=False)
+    attended, student_all = lax.optimization_barrier((attended, student_all))
+    attended_all = lax.all_gather(attended, "dp", axis=0, tiled=False)
+    partial_value = jnp.einsum(
+        "csi,id->csd", student_all, student_out, preferred_element_type=jnp.float32
+    ) + jnp.einsum("csi,id->csd", teacher_all, teacher_out, preferred_element_type=jnp.float32)
     pieces_in = lax.all_to_all(
-        partial_value.astype(jnp.bfloat16).reshape(groups, seq_local, -1),
+        partial_value.astype(jnp.bfloat16).reshape(clips, groups, seq_local, width),
         "tensor",
-        split_axis=0,
-        concat_axis=0,
+        split_axis=1,
+        concat_axis=1,
         tiled=True,
     )
-    velocity = jnp.sum(pieces_in.astype(jnp.float32), axis=0)
-    target = (velocity - latent_weight * latent[0].astype(jnp.float32)).astype(jnp.bfloat16)
-    clips = lax.axis_size("dp")
-    width = target.shape[1] // clips
-    attended_all = lax.all_gather(attended, "dp", axis=0, tiled=False)
-    columns = lax.all_to_all(
-        target.reshape(seq_local, clips, width), "dp", split_axis=1, concat_axis=1, tiled=True
-    )
-    columns = lax.all_gather(columns, "tensor", axis=0, tiled=True)
+    velocity = jnp.sum(pieces_in.astype(jnp.float32), axis=1)
+    columns = (
+        velocity - latent_weight * jnp.transpose(latent_cols, (1, 0, 2)).astype(jnp.float32)
+    ).astype(jnp.bfloat16)
+    target = lax.all_to_all(columns, "dp", split_axis=0, concat_axis=0, tiled=True)
+    target = jnp.transpose(target, (1, 0, 2)).reshape(seq_local, clips * width)
+    columns, attended_all = lax.optimization_barrier((columns, attended_all))
+    columns = lax.all_gather(columns, "tensor", axis=1, tiled=True)
     grad_scale = -2.0 / math.sqrt(clips * seq_whole)
     terms = jnp.einsum(
-        "csi,scd->cid", attended_all, columns, preferred_element_type=jnp.float32
+        "csi,csd->cid", attended_all, columns, preferred_element_type=jnp.float32
     )
     gradient = jnp.sum((grad_scale * terms).astype(jnp.bfloat16).astype(jnp.float32), axis=0)
     return (target[None], gradient)

time: 413 us -> 444 us (1.075)
  waiting for transfers between devices: 169 us -> 224 us
  blocking collectives: 98.4 us -> 66.6 us
  starting transfers between devices: 23 us -> 34.1 us
    all_to_all x0 -> x3, waiting for transfers between devices: none -> 69.4 us  [the longest x1 57.1 us: local(): lax.all_to_all(partial_value.astype(jnp.bfloat16).reshape(clips, groups,...]
    all_to_all x2 -> x1, blocking collectives: 98.4 us -> 35.7 us  [local(): lax.all_to_all(columns, 'dp', split_axis=0, concat_axis=0, tiled=True)]
    unnamed x0 -> x1, blocking collectives: none -> 30.9 us
    all_to_all x6 -> x5, waiting for transfers between devices: 60.9 us -> 42.4 us  [local(): lax.all_to_all(source[0], 'tensor', split_axis=1, concat_axis=0, tiled=True)]
    all_to_all x0 -> x3, starting transfers between devices: none -> 12.3 us  [the longest x1 5.19 us: local(): lax.all_to_all(partial_value.astype(jnp.bfloat16).reshape(clips, groups,...]
    mul x2 -> x0, local copies, waits for them, and re-layouts: 5.41 us -> none  [local(): latent_weight * latent[0].astype(jnp.float32)]
    reduce_sum x2 -> x0, local copies, waits for them, and re-layouts: 5.33 us -> none  [local(): velocity = jnp.sum(pieces_in.astype(jnp.float32), axis=0)]
    all_gather x2 -> x3, waiting for transfers between devices: 108 us -> 112 us  [the longest x1 82.3 us: local(): student_all = lax.all_gather(student_term, 'dp', axis=0, tiled=False)]
  transfers between devices with their start and end apart: 9 -> 12, of which waited for: 8 -> 10; matrix products, arithmetic and copies ran while one was open for 12% -> 10% of each run, Pallas kernels for 8% -> 0%
where the time goes in v1:
time: 444 us; the launch traced here: 443 us
  waiting for transfers between devices  224 us (50%)
  blocking collectives  66.6 us (15%)
  starting transfers between devices  34.1 us (8%)
  matrix products  31.6 us (7%)
  Pallas kernels  31.2 us (7%)
  local copies, waits for them, and re-layouts  27.4 us (6%)
  between operations  15.5 us (3%)
  other arithmetic  12.5 us (3%)
    all_gather x1, waiting for transfers between devices, local(): student_all = lax.all_gather(student_term, 'dp', axis=0, tiled=False)  82.3 us
    all_to_all x1, waiting for transfers between devices, local(): lax.all_to_all(partial_value.astype(jnp.bfloat16).reshape(clips, groups,...  57.1 us
    all_to_all x5, waiting for transfers between devices, local(): lax.all_to_all(source[0], 'tensor', split_axis=1, concat_axis=0, tiled=True)  42.4 us
    all_to_all x1, blocking collectives, local(): lax.all_to_all(columns, 'dp', split_axis=0, concat_axis=0, tiled=True)  35.7 us
    pallas_call x2, Pallas kernels, head_call(): pl.pallas_call(kernel, grid=(heads,), in_specs=in_specs, out_specs=[head_...  31.2 us
    unnamed x1, blocking collectives  30.9 us
    all_gather x1, waiting for transfers between devices, local(): columns = lax.all_gather(columns, 'tensor', axis=1, tiled=True)  21.6 us
    all_to_all x5, starting transfers between devices, local(): lax.all_to_all(source[0], 'tensor', split_axis=1, concat_axis=0, tiled=True)  21.5 us
  transfers between devices with their start and end apart: 12, of which 10 were waited for; matrix products, arithmetic and copies ran while one was open for 10% of the time, Pallas kernels for 0%

profile of v1, /device:TPU:0, one launch (start us, length us, event | category | flops | bytes accessed | tf_op | source)
XLA Modules:
  0.0 442.8 jit_solution(16789273342027082997)
XLA Ops:
  12.1 15.3 %shard_map.158 = bf16[512,1024]{1,0:T(8,128)(2,1)} custom-call(f32[2]{0:T(128)} %pad_maximum_fusion.3.scal, f32[512,128]{1,0:T(8,128)} %get-tuple-element.44.cos_ref, f32[512,128]{1,0:T(8,128)} %get-tuple-element.45.sin_ref, bf16[2,512,1024]{2,1,0:T(8,128)(2,1)} %bitcast.46, bf16[2,512,1024]{2,1,0:T(8,128)(2,1)} %bitcast.48, bf16[2,512,1024]{2,1,0:T(8,128)(2,1)} %bitcast.50, ...), custom_call_target="tpu_custom_call" | custom-call | tf_op jit(solution)/shard_map/pallas_call | solution.py:178
  29.5 5.2 %all-to-all-start.2 = ((bf16[128,4,1024]{2,0,1:T(8,128)(2,1)}), bf16[128,4,1024]{2,0,1:T(8,128)(2,1)S(1)}, u32[]{:S(2)}, u32[]{:S(2)}) async-start(bf16[128,4,1024]{2,0,1:T(8,128)(2,1)} %copy.50), calls=%async_computation.2 | async-start | bytes 2097152 | tf_op jit(solution)/shard_map/all_to_all | solution.py:240
  34.7 1.8 all_to_all.105
  37.8 10.5 %all-to-all-done.2 = bf16[128,4,1024]{2,0,1:T(8,128)(2,1)S(1)} async-done(((bf16[128,4,1024]{2,0,1:T(8,128)(2,1)}), bf16[128,4,1024]{2,0,1:T(8,128)(2,1)S(1)}, u32[]{:S(2)}, u32[]{:S(2)}) %all-to-all-start.2) | async-done | bytes 1048608 | tf_op jit(solution)/shard_map/all_to_all | solution.py:240
  48.3 4.3 all-to-all-start.3
  52.6 1.9 all_to_all.109
  55.8 10.1 %all-to-all-done.3 = bf16[128,4,1024]{2,0,1:T(8,128)(2,1)} async-done(((bf16[128,4,1024]{2,0,1:T(8,128)(2,1)}), bf16[128,4,1024]{2,0,1:T(8,128)(2,1)}, u32[]{:S(2)}, u32[]{:S(2)}) %all-to-all-start.3) | async-done | bytes 1048608 | tf_op jit(solution)/shard_map/all_to_all | solution.py:240
  65.9 4.3 all-to-all-start.4
  70.1 1.9 all_to_all.93
  73.3 10.0 %all-to-all-done.4 = bf16[128,4,1024]{2,0,1:T(8,128)(2,1)} async-done(((bf16[128,4,1024]{2,0,1:T(8,128)(2,1)}), bf16[128,4,1024]{2,0,1:T(8,128)(2,1)}, u32[]{:S(2)}, u32[]{:S(2)}) %all-to-all-start.4) | async-done | bytes 1048608 | tf_op jit(solution)/shard_map/all_to_all | solution.py:240
  83.3 3.5 all-to-all-start
  86.8 1.9 all_to_all.97
  89.9 9.9 %all-to-all-done = bf16[128,4,1024]{2,0,1:T(8,128)(2,1)S(1)} async-done(((bf16[128,4,1024]{2,0,1:T(8,128)(2,1)}), bf16[128,4,1024]{2,0,1:T(8,128)(2,1)S(1)}, u32[]{:S(2)}, u32[]{:S(2)}) %all-to-all-start) | async-done | bytes 1048608 | tf_op jit(solution)/shard_map/all_to_all | solution.py:240
  99.9 4.2 all-to-all-start.1
  104.1 8.2 %all-gather.10.cloned.1.call-done = bf16[4096,1024]{1,0:T(8,128)(2,1)} async-done(((bf16[512,1024]{1,0:T(8,128)(2,1)}), bf16[4096,1024]{1,0:T(8,128)(2,1)}) %all-gather.10.cloned.1.call-update) | async-done | bytes 8388624 | tf_op jit(solution)/shard_map/all_gather | solution.py:238
  115.5 1.9 all-to-all-done.1
  117.4 3.5 all-to-all-start.5
  121.7 12.2 %all-to-all-done.5 = bf16[128,4,1024]{2,0,1:T(8,128)(2,1)S(1)} async-done(((bf16[128,4,1024]{2,0,1:T(8,128)(2,1)}), bf16[128,4,1024]{2,0,1:T(8,128)(2,1)S(1)}, u32[]{:S(2)}, u32[]{:S(2)}) %all-to-all-start.5) | async-done | bytes 1048608 | tf_op jit(solution)/shard_map/all_to_all | solution.py:244
  134.9 15.9 %shard_map.159 = (bf16[512,1024]{1,0:T(8,128)(2,1)}, bf16[512,1024]{1,0:T(8,128)(2,1)}) custom-call(f32[2]{0:T(128)} %pad_maximum_fusion.2.scal, f32[512,128]{1,0:T(8,128)} %get-tuple-element.44.cos_ref, f32[512,128]{1,0:T(8,128)} %get-tuple-element.45.sin_ref, bf16[512,1024]{1,0:T(8,128)(2,1)} %bitcast.57, bf16[512,1024]{1,0:T(8,128)(2,1)} %bitcast.9.k, ...), custom_call_target="tpu_custom_call" | custom-call | tf_op jit(solution)/shard_map/pallas_call | solution.py:178
  151.1 82.3 %all-gather.12.cloned.1.call-done = bf16[4096,1024]{1,0:T(8,128)(2,1)} async-done(((bf16[512,1024]{1,0:T(8,128)(2,1)}), bf16[4096,1024]{1,0:T(8,128)(2,1)}) %all-gather.12.cloned.1.call-update) | async-done | bytes 8388624 | tf_op jit(solution)/shard_map/all_gather | solution.py:263
  233.4 9.4 %fusion.2 = f32[8,512,640]{2,1,0:T(8,128)S(1)} fusion(bf16[8,512,1024]{2,1,0:T(8,128)(2,1)} %bitcast.64, bf16[1024,640]{1,0:T(8,128)(2,1)S(1)} %copy-done), kind=kOutput, calls=%fused_computation.7 | convolution fusion | flops 5368709120 | bytes 20185088 | tf_op jit(solution)/shard_map/csi,id->csd/dot_general | solution.py:266
  242.8 9.8 %add_convert_fusion = bf16[8,512,640]{2,1,0:T(8,128)(2,1)S(1)} fusion(f32[8,512,640]{2,1,0:T(8,128)S(1)} %fusion.2, bf16[8,512,1024]{2,1,0:T(8,128)(2,1)} %bitcast.62, bf16[1024,640]{1,0:T(8,128)(2,1)S(1)} %copy-done.7), kind=kOutput, calls=%fused_computation.3 | convolution fusion | flops 5373952000 | bytes 25427968 | tf_op jit(solution)/shard_map/csi,id->csd/dot_general | solution.py:268
  252.6 2.8 copy.54
  255.4 5.2 %all-to-all-start.6 = ((bf16[8,4,128,640]{3,2,0,1:T(8,128)(2,1)}), bf16[8,4,128,640]{3,2,0,1:T(8,128)(2,1)}, u32[]{:S(2)}, u32[]{:S(2)}) async-start(bf16[8,4,128,640]{3,2,0,1:T(8,128)(2,1)} %copy.54), calls=%async_computation.6 | async-start | bytes 10485760 | tf_op jit(solution)/shard_map/all_to_all | solution.py:269
  262.8 57.1 %all-to-all-done.6 = bf16[8,4,128,640]{3,2,0,1:T(8,128)(2,1)} async-done(((bf16[8,4,128,640]{3,2,0,1:T(8,128)(2,1)}), bf16[8,4,128,640]{3,2,0,1:T(8,128)(2,1)}, u32[]{:S(2)}, u32[]{:S(2)}) %all-to-all-start.6) | async-done | bytes 5242912 | tf_op jit(solution)/shard_map/all_to_all | solution.py:269
  320.0 3.6 all-to-all-start.7
  325.0 30.9 %all-reduce = s32[8]{0:T(128)S(1)} all-reduce(s32[8]{0:T(128)S(1)} %dynamic-update-slice), channel_id=1, replica_groups=mesh['dp'=8,'tensor'=4] {'dp'}, use_global_device_ids=true, to_apply=%add | all-reduce | flops 8 | bytes 64
  355.9 5.1 %convert_reduce_fusion.1 = f32[8,128,640]{2,1,0:T(8,128)} fusion(bf16[8,4,128,640]{3,2,0,1:T(8,128)(2,1)} %all-to-all-done.6), kind=kLoop, calls=%fused_computation.2 | loop fusion | flops 4587520 | bytes 7864320 | tf_op jit(solution)/shard_map/reduce_sum | solution.py:276
  361.0 3.2 fusion
  364.3 35.7 %all_to_all.129 = bf16[8,128,640]{2,1,0:T(8,128)(2,1)S(1)} all-to-all(bf16[8,128,640]{2,1,0:T(8,128)(2,1)} %fusion), channel_id=1, replica_groups=mesh['dp'=8,'tensor'=4] {'dp'}, dimensions={0} | all-to-all | bytes 2621440 | tf_op jit(solution)/shard_map/all_to_all | solution.py:280
  402.2 21.6 %all-gather.8.cloned.1.call-done = bf16[8,512,640]{2,1,0:T(8,128)(2,1)} async-done(((bf16[8,128,640]{2,1,0:T(8,128)(2,1)}), bf16[8,512,640]{2,1,0:T(8,128)(2,1)}) %all-gather.8.cloned.1.call-update) | async-done | bytes 5242896 | tf_op jit(solution)/shard_map/all_gather | solution.py:283
  423.8 12.5 %convert_reduce_fusion = f32[1024,640]{1,0:T(8,128)} fusion(bf16[8,512,1024]{2,1,0:T(8,128)(2,1)} %bitcast.63, bf16[8,512,640]{2,1,0:T(8,128)(2,1)} %all-gather.8.cloned.1.call-done), kind=kOutput, calls=%fused_computation | convolution fusion | flops 5389025280 | bytes 16252928 | tf_op jit(solution)/shard_map/csi,csd->cid/dot_general | solution.py:285
  (52 shorter events, 21.8 us)
Async XLA Ops:
  7.2 226.2 %copy-start = (bf16[1024,640]{1,0:T(8,128)(2,1)S(1)}, bf16[1024,640]{1,0:T(8,128)(2,1)}, u32[]{:S(2)}) copy-start(bf16[1024,640]{1,0:T(8,128)(2,1)} %param.29) | copy-start | bytes 3932164
  7.2 105.2 %all-gather.10.cloned.1.call-start = ((), (), s32[]{:S(2)}) async-start(), calls=%async_computation.10 | async-start | bytes 9437184 | tf_op jit(solution)/shard_map/all_gather | solution.py:238
  12.1 15.3 %copy-start.6 = (bf16[1,128,4096]{2,1,0:T(8,128)(2,1)S(1)}, bf16[1,128,4096]{2,1,0:T(8,128)(2,1)}, u32[]{:S(2)}) copy-start(bf16[1,128,4096]{2,1,0:T(8,128)(2,1)} %param.24) | copy-start | bytes 3145732
  29.5 18.8 %all-to-all-start.2 = ((bf16[128,4,1024]{2,0,1:T(8,128)(2,1)}), bf16[128,4,1024]{2,0,1:T(8,128)(2,1)S(1)}, u32[]{:S(2)}, u32[]{:S(2)}) async-start(bf16[128,4,1024]{2,0,1:T(8,128)(2,1)} %copy.50), calls=%async_computation.2 | async-start | bytes 2097152 | tf_op jit(solution)/shard_map/all_to_all | solution.py:240
  48.3 23.7 %copy-start.2 = (bf16[128,4,1024]{2,0,1:T(8,128)(2,1)}, bf16[128,4,1024]{2,0,1:T(8,128)(2,1)S(1)}, u32[]{:S(2)}) copy-start(bf16[128,4,1024]{2,0,1:T(8,128)(2,1)S(1)} %all-to-all-done.2) | copy-start | bytes 3145732
  48.3 17.5 %all-to-all-start.3 = ((bf16[128,4,1024]{2,0,1:T(8,128)(2,1)}), bf16[128,4,1024]{2,0,1:T(8,128)(2,1)}, u32[]{:S(2)}, u32[]{:S(2)}) async-start(bf16[128,4,1024]{2,0,1:T(8,128)(2,1)} %copy.51), calls=%async_computation.3 | async-start | bytes 2097152 | tf_op jit(solution)/shard_map/all_to_all | solution.py:240
  65.9 17.4 %all-to-all-start.4 = ((bf16[128,4,1024]{2,0,1:T(8,128)(2,1)}), bf16[128,4,1024]{2,0,1:T(8,128)(2,1)}, u32[]{:S(2)}, u32[]{:S(2)}) async-start(bf16[128,4,1024]{2,0,1:T(8,128)(2,1)} %copy.52), calls=%async_computation.4 | async-start | bytes 2097152 | tf_op jit(solution)/shard_map/all_to_all | solution.py:240
  83.3 16.6 %all-to-all-start = ((bf16[128,4,1024]{2,0,1:T(8,128)(2,1)}), bf16[128,4,1024]{2,0,1:T(8,128)(2,1)S(1)}, u32[]{:S(2)}, u32[]{:S(2)}) async-start(bf16[128,4,1024]{2,0,1:T(8,128)(2,1)} %copy.48), calls=%async_computation | async-start | bytes 2097152 | tf_op jit(solution)/shard_map/all_to_all | solution.py:240
  99.9 34.1 %copy-start.3 = (bf16[128,4,1024]{2,0,1:T(8,128)(2,1)}, bf16[128,4,1024]{2,0,1:T(8,128)(2,1)S(1)}, u32[]{:S(2)}) copy-start(bf16[128,4,1024]{2,0,1:T(8,128)(2,1)S(1)} %all-to-all-done) | copy-start | bytes 3145732
  99.9 17.5 %all-to-all-start.1 = ((bf16[128,4,1024]{2,0,1:T(8,128)(2,1)}), bf16[128,4,1024]{2,0,1:T(8,128)(2,1)}, u32[]{:S(2)}, u32[]{:S(2)}) async-start(bf16[128,4,1024]{2,0,1:T(8,128)(2,1)} %copy.49), calls=%async_computation.1 | async-start | bytes 2097152 | tf_op jit(solution)/shard_map/all_to_all | solution.py:240
  117.4 16.6 %all-to-all-start.5 = ((bf16[128,4,1024]{2,0,1:T(8,128)(2,1)}), bf16[128,4,1024]{2,0,1:T(8,128)(2,1)S(1)}, u32[]{:S(2)}, u32[]{:S(2)}) async-start(bf16[128,4,1024]{2,0,1:T(8,128)(2,1)} %copy.53), calls=%async_computation.5 | async-start | bytes 2097152 | tf_op jit(solution)/shard_map/all_to_all | solution.py:244
  120.9 112.4 %all-gather.12.cloned.1.call-start = ((), (), s32[]{:S(2)}) async-start(), calls=%async_computation.11 | async-start | bytes 9437184 | tf_op jit(solution)/shard_map/all_gather | solution.py:263
  134.0 1.0 copy-start.4
  150.8 213.4 %all-gather.14.cloned.1.call-start = ((), (), s32[]{:S(2)}) async-start(), calls=%async_computation.12 | async-start | bytes 9437184 | tf_op jit(solution)/shard_map/all_gather | solution.py:265
  233.4 9.4 %copy-start.7 = (bf16[1024,640]{1,0:T(8,128)(2,1)S(1)}, bf16[1024,640]{1,0:T(8,128)(2,1)}, u32[]{:S(2)}) copy-start(bf16[1024,640]{1,0:T(8,128)(2,1)} %param.28) | copy-start | bytes 3932164
  255.4 5.2 %copy-start.5 = (bf16[1,128,5120]{2,1,0:T(8,128)(2,1)S(1)}, bf16[1,128,5120]{2,1,0:T(8,128)(2,1)}, u32[]{:S(2)}) copy-start(bf16[1,128,5120]{2,1,0:T(8,128)(2,1)} %param.18) | copy-start | bytes 3932164
  255.4 64.6 %all-to-all-start.6 = ((bf16[8,4,128,640]{3,2,0,1:T(8,128)(2,1)}), bf16[8,4,128,640]{3,2,0,1:T(8,128)(2,1)}, u32[]{:S(2)}, u32[]{:S(2)}) async-start(bf16[8,4,128,640]{3,2,0,1:T(8,128)(2,1)} %copy.54), calls=%async_computation.6 | async-start | bytes 10485760 | tf_op jit(solution)/shard_map/all_to_all | solution.py:269
  260.6 63.0 %copy-start.8 = (u32[32]{0:T(128)S(1)}, u32[32]{0:T(128)}, u32[]{:S(2)}) copy-start(u32[32]{0:T(128)} %constant.64) | copy-start | bytes 388
  320.0 41.0 %all-to-all-start.7 = ((bf16[128,8,640]{2,0,1:T(8,128)(2,1)}), bf16[128,8,640]{2,0,1:T(8,128)(2,1)S(1)}, u32[]{:S(2)}, u32[]{:S(2)}) async-start(bf16[128,8,640]{2,0,1:T(8,128)(2,1)} %copy.56), calls=%async_computation.7 | async-start | bytes 2621440 | tf_op jit(solution)/shard_map/all_to_all | solution.py:260
  323.6 100.2 %all-gather.8.cloned.1.call-start = ((), (), s32[]{:S(2)}) async-start(), calls=%async_computation.9 | async-start | bytes 6553600 | tf_op jit(solution)/shard_map/all_gather | solution.py:283
  423.8 12.5 %copy-start.1 = (bf16[1024,640]{1,0:T(8,128)(2,1)S(1)}, bf16[1024,640]{1,0:T(8,128)(2,1)}, u32[]{:S(2)}) copy-start(bf16[1024,640]{1,0:T(8,128)(2,1)} %param.29) | copy-start | bytes 3932164
Sparse Core Ops, SparseCore 0:
  27.5 84.7 all-gather.9
  151.0 82.3 all-gather.11
  235.0 80.5 all-gather.13
  364.4 59.3 all-gather.7

commit v2 on v1

--- a/solution.py
+++ b/solution.py
@@ -232,15 +232,21 @@
         [Operand(t_q, 0), Operand(t_k, 0), Operand(t_v, 0), Operand(t_q, 1), Operand(t_k, 1), Operand(t_v, 1)],
         [jax.ShapeDtypeStruct((seq_whole, cols), jnp.bfloat16)],
     )
-    teacher_term, sources = lax.optimization_barrier(
-        (teacher_term, (student_query, student_key, student_value, query_tangent, key_tangent, value_tangent))
+    clips = lax.axis_size("dp")
+    width = latent.shape[2] // clips
+    times_all = lax.all_gather(t_index, "dp", axis=0, tiled=True)
+    teacher_term, sources, times_all = lax.optimization_barrier(
+        (teacher_term, (student_query, student_key, student_value, query_tangent, key_tangent, value_tangent), times_all)
     )
     teacher_all = lax.all_gather(teacher_term, "dp", axis=0, tiled=False)
+    latent_cols = lax.all_to_all(
+        latent[0].reshape(seq_local, clips, width), "dp", split_axis=1, concat_axis=1, tiled=True
+    )
     arrived = [
         lax.all_to_all(source[0], "tensor", split_axis=1, concat_axis=0, tiled=True)
         for source in sources[:-1]
     ]
-    teacher_all, last = lax.optimization_barrier((teacher_all, sources[-1]))
+    teacher_all, last, latent_cols = lax.optimization_barrier((teacher_all, sources[-1], latent_cols))
     arrived.append(lax.all_to_all(last[0], "tensor", split_axis=1, concat_axis=0, tiled=True))
     student_scal = jnp.stack(
         [-(cos_time * cos_time) * sigma_data, cos_time * sin_time * sigma_data]
@@ -252,20 +258,17 @@
         [Operand(a) for a in arrived],
         [jax.ShapeDtypeStruct((seq_whole, cols), jnp.bfloat16)] * 2,
     )
-    clips = lax.axis_size("dp")
-    width = latent.shape[2] // clips
-    times_all = lax.all_gather(t_index, "dp", axis=0, tiled=True)
     time_all = 0.2 + 1.2 * (times_all.astype(jnp.float32) + 0.5) / STEPS
     latent_weight = (jnp.cos(time_all) * jnp.sin(time_all))[:, None, None]
-    latent_cols = lax.all_to_all(
-        latent[0].reshape(seq_local, clips, width), "dp", split_axis=1, concat_axis=1, tiled=True
+    teacher_partial = jnp.einsum(
+        "csi,id->csd", teacher_all, teacher_out, preferred_element_type=jnp.float32
     )
     student_all = lax.all_gather(student_term, "dp", axis=0, tiled=False)
-    attended, student_all = lax.optimization_barrier((attended, student_all))
+    attended, student_all, teacher_partial = lax.optimization_barrier((attended, student_all, teacher_partial))
     attended_all = lax.all_gather(attended, "dp", axis=0, tiled=False)
     partial_value = jnp.einsum(
         "csi,id->csd", student_all, student_out, preferred_element_type=jnp.float32
-    ) + jnp.einsum("csi,id->csd", teacher_all, teacher_out, preferred_element_type=jnp.float32)
+    ) + teacher_partial
     pieces_in = lax.all_to_all(
         partial_value.astype(jnp.bfloat16).reshape(clips, groups, seq_local, width),
         "tensor",

time: 444 us -> 443 us (level)
  blocking collectives: 66.6 us -> 46.3 us
  waiting for transfers between devices: 224 us -> 239 us
  local copies, waits for them, and re-layouts: 27.4 us -> 32.3 us
    unnamed x1 -> x0, blocking collectives: 30.9 us -> none
    all_to_all x1, waiting for transfers between devices: 0.01 us -> 28.2 us  [local(): lax.all_to_all(latent[0].reshape(seq_local, clips, width), 'dp', split_ax...]
    all_gather x1, waiting for transfers between devices: 82.3 us -> 67.9 us  [local(): student_all = lax.all_gather(student_term, 'dp', axis=0, tiled=False)]
    optimization_barrier x0 -> x1, blocking collectives: none -> 10.6 us  [local(): lax.optimization_barrier((teacher_term, (student_query, student_key, stud...]
    all_gather x1, waiting for transfers between devices: 8.22 us -> 0.02 us  [local(): teacher_all = lax.all_gather(teacher_term, 'dp', axis=0, tiled=False)]
    all_to_all x5, waiting for transfers between devices: 42.4 us -> 47.8 us  [local(): lax.all_to_all(source[0], 'tensor', split_axis=1, concat_axis=0, tiled=True)]
  transfers between devices with their start and end apart: 12 -> 12, of which waited for: 10 -> 10; matrix products, arithmetic and copies ran while one was open for 10% -> 11% of each run, Pallas kernels for 0% -> 0%
where the time goes in v2:
time: 443 us; the launch traced here: 442 us
  waiting for transfers between devices  239 us (54%)
  blocking collectives  46.3 us (10%)
  matrix products  34.9 us (8%)
  starting transfers between devices  33.9 us (8%)
  local copies, waits for them, and re-layouts  32.3 us (7%)
  Pallas kernels  31.1 us (7%)
  between operations  15.5 us (3%)
  other arithmetic  9.42 us (2%)
    all_gather x1, waiting for transfers between devices, local(): student_all = lax.all_gather(student_term, 'dp', axis=0, tiled=False)  67.9 us
    all_to_all x1, waiting for transfers between devices, local(): lax.all_to_all(partial_value.astype(jnp.bfloat16).reshape(clips, groups,...  59.2 us
    all_to_all x5, waiting for transfers between devices, local(): lax.all_to_all(source[0], 'tensor', split_axis=1, concat_axis=0, tiled=True)  47.8 us
    all_to_all x1, blocking collectives, local(): lax.all_to_all(columns, 'dp', split_axis=0, concat_axis=0, tiled=True)  35.7 us
    pallas_call x2, Pallas kernels, head_call(): pl.pallas_call(kernel, grid=(heads,), in_specs=in_specs, out_specs=[head_...  31.1 us
    all_to_all x1, waiting for transfers between devices, local(): lax.all_to_all(latent[0].reshape(seq_local, clips, width), 'dp', split_ax...  28.2 us
    all_gather x1, waiting for transfers between devices, local(): columns = lax.all_gather(columns, 'tensor', axis=1, tiled=True)  23 us
    all_to_all x5, starting transfers between devices, local(): lax.all_to_all(source[0], 'tensor', split_axis=1, concat_axis=0, tiled=True)  20.7 us
  transfers between devices with their start and end apart: 12, of which 10 were waited for; matrix products, arithmetic and copies ran while one was open for 11% of the time, Pallas kernels for 0%

profile of v2, /device:TPU:0, one launch (start us, length us, event | category | flops | bytes accessed | tf_op | source)
XLA Modules:
  0.0 442.1 jit_solution(12009621096127758188)
XLA Ops:
  10.8 10.6 %all-reduce = s32[8]{0:T(128)S(1)} all-reduce(s32[8]{0:T(128)S(1)} %dynamic-update-slice), channel_id=1, replica_groups=mesh['dp'=8,'tensor'=4] {'dp'}, use_global_device_ids=true, to_apply=%add | all-reduce | flops 8 | bytes 64 | tf_op jit(solution)/shard_map/optimization_barrier | solution.py:238
  24.8 15.3 %shard_map.158 = bf16[512,1024]{1,0:T(8,128)(2,1)} custom-call(f32[2]{0:T(128)} %pad_maximum_fusion.3.scal, f32[512,128]{1,0:T(8,128)} %get-tuple-element.50.cos_ref, f32[512,128]{1,0:T(8,128)} %get-tuple-element.51.sin_ref, bf16[2,512,1024]{2,1,0:T(8,128)(2,1)} %bitcast.46, bf16[2,512,1024]{2,1,0:T(8,128)(2,1)} %bitcast.48, bf16[2,512,1024]{2,1,0:T(8,128)(2,1)} %bitcast.50, ...), custom_call_target="tpu_custom_call" | custom-call | tf_op jit(solution)/shard_map/pallas_call | solution.py:178
  42.2 3.7 all-to-all-start
  45.9 1.9 all_to_all.97
  49.2 8.9 %all-to-all-done = bf16[128,4,1024]{2,0,1:T(8,128)(2,1)S(1)} async-done(((bf16[128,4,1024]{2,0,1:T(8,128)(2,1)}), bf16[128,4,1024]{2,0,1:T(8,128)(2,1)S(1)}, u32[]{:S(2)}, u32[]{:S(2)}) %all-to-all-start) | async-done | bytes 1048608 | tf_op jit(solution)/shard_map/all_to_all | solution.py:246
  58.1 4.2 all-to-all-start.1
  65.5 10.1 %all-to-all-done.1 = bf16[128,4,1024]{2,0,1:T(8,128)(2,1)} async-done(((bf16[128,4,1024]{2,0,1:T(8,128)(2,1)}), bf16[128,4,1024]{2,0,1:T(8,128)(2,1)}, u32[]{:S(2)}, u32[]{:S(2)}) %all-to-all-start.1) | async-done | bytes 1048608 | tf_op jit(solution)/shard_map/all_to_all | solution.py:246
  75.6 4.3 all-to-all-start.2
  83.0 9.9 %all-to-all-done.2 = bf16[128,4,1024]{2,0,1:T(8,128)(2,1)} async-done(((bf16[128,4,1024]{2,0,1:T(8,128)(2,1)}), bf16[128,4,1024]{2,0,1:T(8,128)(2,1)}, u32[]{:S(2)}, u32[]{:S(2)}) %all-to-all-start.2) | async-done | bytes 1048608 | tf_op jit(solution)/shard_map/all_to_all | solution.py:246
  93.0 4.3 all-to-all-start.3
  100.5 9.9 %all-to-all-done.3 = bf16[128,4,1024]{2,0,1:T(8,128)(2,1)} async-done(((bf16[128,4,1024]{2,0,1:T(8,128)(2,1)}), bf16[128,4,1024]{2,0,1:T(8,128)(2,1)}, u32[]{:S(2)}, u32[]{:S(2)}) %all-to-all-start.3) | async-done | bytes 1048608 | tf_op jit(solution)/shard_map/all_to_all | solution.py:246
  110.4 3.6 all-to-all-start.5
  113.9 2.6 all_to_all.109
  116.6 2.6 copy.52
  119.1 28.2 %all-to-all-done.5 = bf16[128,8,640]{2,0,1:T(8,128)(2,1)S(1)} async-done(((bf16[128,8,640]{2,0,1:T(8,128)(2,1)}), bf16[128,8,640]{2,0,1:T(8,128)(2,1)S(1)}, u32[]{:S(2)}, u32[]{:S(2)}) %all-to-all-start.5) | async-done | bytes 1310752 | tf_op jit(solution)/shard_map/all_to_all | solution.py:242
  147.3 4.2 all-to-all-start.4
  151.6 2.6 all_to_all.114
  154.2 2.5 copy.55
  156.7 8.9 %all-to-all-done.4 = bf16[128,4,1024]{2,0,1:T(8,128)(2,1)} async-done(((bf16[128,4,1024]{2,0,1:T(8,128)(2,1)}), bf16[128,4,1024]{2,0,1:T(8,128)(2,1)}, u32[]{:S(2)}, u32[]{:S(2)}) %all-to-all-start.4) | async-done | bytes 1048608 | tf_op jit(solution)/shard_map/all_to_all | solution.py:246
  165.6 4.2 all-to-all-start.6
  170.7 12.5 %all-to-all-done.6 = bf16[128,4,1024]{2,0,1:T(8,128)(2,1)} async-done(((bf16[128,4,1024]{2,0,1:T(8,128)(2,1)}), bf16[128,4,1024]{2,0,1:T(8,128)(2,1)}, u32[]{:S(2)}, u32[]{:S(2)}) %all-to-all-start.6) | async-done | bytes 1048608 | tf_op jit(solution)/shard_map/all_to_all | solution.py:250
  183.1 15.9 %shard_map.159 = (bf16[512,1024]{1,0:T(8,128)(2,1)}, bf16[512,1024]{1,0:T(8,128)(2,1)}) custom-call(f32[2]{0:T(128)} %pad_maximum_fusion.2.scal, f32[512,128]{1,0:T(8,128)} %get-tuple-element.50.cos_ref, f32[512,128]{1,0:T(8,128)} %get-tuple-element.51.sin_ref, bf16[512,1024]{1,0:T(8,128)(2,1)} %bitcast.56, bf16[512,1024]{1,0:T(8,128)(2,1)} %bitcast.10.k, ...), custom_call_target="tpu_custom_call" | custom-call | tf_op jit(solution)/shard_map/pallas_call | solution.py:178
  199.3 11.4 %fusion.2 = f32[8,512,640]{2,1,0:T(8,128)} fusion(bf16[8,512,1024]{2,1,0:T(8,128)(2,1)} %bitcast.60, bf16[1024,640]{1,0:T(8,128)(2,1)S(1)} %copy-done), kind=kOutput, calls=%fused_computation.7 | convolution fusion | flops 5368709120 | bytes 20185088 | tf_op jit(solution)/shard_map/csi,id->csd/dot_general | solution.py:263
  210.7 67.9 %all-gather.12.cloned.1.call-done = bf16[4096,1024]{1,0:T(8,128)(2,1)} async-done(((bf16[512,1024]{1,0:T(8,128)(2,1)}), bf16[4096,1024]{1,0:T(8,128)(2,1)}) %all-gather.12.cloned.1.call-update) | async-done | bytes 8388624 | tf_op jit(solution)/shard_map/all_gather | solution.py:266
  278.6 11.0 %add_convert_fusion = bf16[8,512,640]{2,1,0:T(8,128)(2,1)S(1)} fusion(f32[8,512,640]{2,1,0:T(8,128)} %fusion.2, bf16[8,512,1024]{2,1,0:T(8,128)(2,1)} %bitcast.62, bf16[1024,640]{1,0:T(8,128)(2,1)} %param.29), kind=kOutput, calls=%fused_computation.3 | convolution fusion | flops 5373952000 | bytes 25427968 | tf_op jit(solution)/shard_map/csi,id->csd/dot_general | solution.py:269
  289.7 2.8 copy.56
  292.5 5.1 %all-to-all-start.7 = ((bf16[8,4,128,640]{3,2,0,1:T(8,128)(2,1)}), bf16[8,4,128,640]{3,2,0,1:T(8,128)(2,1)}, u32[]{:S(2)}, u32[]{:S(2)}) async-start(bf16[8,4,128,640]{3,2,0,1:T(8,128)(2,1)} %copy.56), calls=%async_computation.7 | async-start | bytes 10485760 | tf_op jit(solution)/shard_map/all_to_all | solution.py:272
  297.7 59.2 %all-to-all-done.7 = bf16[8,4,128,640]{3,2,0,1:T(8,128)(2,1)} async-done(((bf16[8,4,128,640]{3,2,0,1:T(8,128)(2,1)}), bf16[8,4,128,640]{3,2,0,1:T(8,128)(2,1)}, u32[]{:S(2)}, u32[]{:S(2)}) %all-to-all-start.7) | async-done | bytes 5242912 | tf_op jit(solution)/shard_map/all_to_all | solution.py:272
  356.9 3.7 convert_reduce_fusion.1
  362.2 35.7 %all_to_all.129 = bf16[8,128,640]{2,1,0:T(8,128)(2,1)S(1)} all-to-all(bf16[8,128,640]{2,1,0:T(8,128)(2,1)} %fusion), channel_id=1, replica_groups=mesh['dp'=8,'tensor'=4] {'dp'}, dimensions={0} | all-to-all | bytes 2621440 | tf_op jit(solution)/shard_map/all_to_all | solution.py:283
  400.1 23.0 %all-gather.8.cloned.1.call-done = bf16[8,512,640]{2,1,0:T(8,128)(2,1)} async-done(((bf16[8,128,640]{2,1,0:T(8,128)(2,1)}), bf16[8,512,640]{2,1,0:T(8,128)(2,1)}) %all-gather.8.cloned.1.call-update) | async-done | bytes 5242896 | tf_op jit(solution)/shard_map/all_gather | solution.py:286
  423.1 12.5 %convert_reduce_fusion = f32[1024,640]{1,0:T(8,128)} fusion(bf16[8,512,1024]{2,1,0:T(8,128)(2,1)} %bitcast.61, bf16[8,512,640]{2,1,0:T(8,128)(2,1)} %all-gather.8.cloned.1.call-done), kind=kOutput, calls=%fused_computation | convolution fusion | flops 5389025280 | bytes 16252928 | tf_op jit(solution)/shard_map/csi,csd->cid/dot_general | solution.py:288
  (42 shorter events, 23.4 us)
Async XLA Ops:
  7.2 192.1 %copy-start = (bf16[1024,640]{1,0:T(8,128)(2,1)S(1)}, bf16[1024,640]{1,0:T(8,128)(2,1)}, u32[]{:S(2)}) copy-start(bf16[1024,640]{1,0:T(8,128)(2,1)} %param.28) | copy-start | bytes 3932164
  7.2 144.4 %all-gather.10.cloned.1.call-start = ((), (), s32[]{:S(2)}) async-start(), calls=%async_computation.10 | async-start | bytes 9437184 | tf_op jit(solution)/shard_map/all_gather | solution.py:241
  24.8 15.3 %copy-start.3 = (bf16[1,128,4096]{2,1,0:T(8,128)(2,1)S(1)}, bf16[1,128,4096]{2,1,0:T(8,128)(2,1)}, u32[]{:S(2)}) copy-start(bf16[1,128,4096]{2,1,0:T(8,128)(2,1)} %param.22) | copy-start | bytes 3145732
  42.2 15.9 %all-to-all-start = ((bf16[128,4,1024]{2,0,1:T(8,128)(2,1)}), bf16[128,4,1024]{2,0,1:T(8,128)(2,1)S(1)}, u32[]{:S(2)}, u32[]{:S(2)}) async-start(bf16[128,4,1024]{2,0,1:T(8,128)(2,1)} %copy.48), calls=%async_computation | async-start | bytes 2097152 | tf_op jit(solution)/shard_map/all_to_all | solution.py:246
  58.1 23.6 %copy-start.2 = (bf16[128,4,1024]{2,0,1:T(8,128)(2,1)}, bf16[128,4,1024]{2,0,1:T(8,128)(2,1)S(1)}, u32[]{:S(2)}) copy-start(bf16[128,4,1024]{2,0,1:T(8,128)(2,1)S(1)} %all-to-all-done) | copy-start | bytes 3145732
  58.1 17.5 %all-to-all-start.1 = ((bf16[128,4,1024]{2,0,1:T(8,128)(2,1)}), bf16[128,4,1024]{2,0,1:T(8,128)(2,1)}, u32[]{:S(2)}, u32[]{:S(2)}) async-start(bf16[128,4,1024]{2,0,1:T(8,128)(2,1)} %copy.49), calls=%async_computation.1 | async-start | bytes 2097152 | tf_op jit(solution)/shard_map/all_to_all | solution.py:246
  75.6 17.4 %all-to-all-start.2 = ((bf16[128,4,1024]{2,0,1:T(8,128)(2,1)}), bf16[128,4,1024]{2,0,1:T(8,128)(2,1)}, u32[]{:S(2)}, u32[]{:S(2)}) async-start(bf16[128,4,1024]{2,0,1:T(8,128)(2,1)} %copy.50), calls=%async_computation.2 | async-start | bytes 2097152 | tf_op jit(solution)/shard_map/all_to_all | solution.py:246
  93.0 17.4 %all-to-all-start.3 = ((bf16[128,4,1024]{2,0,1:T(8,128)(2,1)}), bf16[128,4,1024]{2,0,1:T(8,128)(2,1)}, u32[]{:S(2)}, u32[]{:S(2)}) async-start(bf16[128,4,1024]{2,0,1:T(8,128)(2,1)} %copy.51), calls=%async_computation.3 | async-start | bytes 2097152 | tf_op jit(solution)/shard_map/all_to_all | solution.py:246
  110.4 36.9 %all-to-all-start.5 = ((bf16[128,8,640]{2,0,1:T(8,128)(2,1)}), bf16[128,8,640]{2,0,1:T(8,128)(2,1)S(1)}, u32[]{:S(2)}, u32[]{:S(2)}) async-start(bf16[128,8,640]{2,0,1:T(8,128)(2,1)} %copy.54), calls=%async_computation.5 | async-start | bytes 2621440 | tf_op jit(solution)/shard_map/all_to_all | solution.py:242
  147.3 18.3 %all-to-all-start.4 = ((bf16[128,4,1024]{2,0,1:T(8,128)(2,1)}), bf16[128,4,1024]{2,0,1:T(8,128)(2,1)}, u32[]{:S(2)}, u32[]{:S(2)}) async-start(bf16[128,4,1024]{2,0,1:T(8,128)(2,1)} %copy.52), calls=%async_computation.4 | async-start | bytes 2097152 | tf_op jit(solution)/shard_map/all_to_all | solution.py:246
  165.6 17.5 %all-to-all-start.6 = ((bf16[128,4,1024]{2,0,1:T(8,128)(2,1)}), bf16[128,4,1024]{2,0,1:T(8,128)(2,1)}, u32[]{:S(2)}, u32[]{:S(2)}) async-start(bf16[128,4,1024]{2,0,1:T(8,128)(2,1)} %copy.55), calls=%async_computation.6 | async-start | bytes 2097152 | tf_op jit(solution)/shard_map/all_to_all | solution.py:250
  169.9 108.7 %all-gather.12.cloned.1.call-start = ((), (), s32[]{:S(2)}) async-start(), calls=%async_computation.11 | async-start | bytes 9437184 | tf_op jit(solution)/shard_map/all_gather | solution.py:266
  199.0 163.1 %all-gather.14.cloned.1.call-start = ((), (), s32[]{:S(2)}) async-start(), calls=%async_computation.12 | async-start | bytes 9437184 | tf_op jit(solution)/shard_map/all_gather | solution.py:268
  292.5 64.4 %all-to-all-start.7 = ((bf16[8,4,128,640]{3,2,0,1:T(8,128)(2,1)}), bf16[8,4,128,640]{3,2,0,1:T(8,128)(2,1)}, u32[]{:S(2)}, u32[]{:S(2)}) async-start(bf16[8,4,128,640]{3,2,0,1:T(8,128)(2,1)} %copy.56), calls=%async_computation.7 | async-start | bytes 10485760 | tf_op jit(solution)/shard_map/all_to_all | solution.py:272
  297.6 125.5 %all-gather.8.cloned.1.call-start = ((), (), s32[]{:S(2)}) async-start(), calls=%async_computation.9 | async-start | bytes 6553600 | tf_op jit(solution)/shard_map/all_gather | solution.py:286
  423.1 12.5 %copy-start.1 = (bf16[1024,640]{1,0:T(8,128)(2,1)S(1)}, bf16[1024,640]{1,0:T(8,128)(2,1)}, u32[]{:S(2)}) copy-start(bf16[1024,640]{1,0:T(8,128)(2,1)} %param.28) | copy-start | bytes 3932164
Sparse Core Ops, SparseCore 0:
  40.2 82.9 all-gather.9
  199.1 79.4 all-gather.11
  280.2 80.5 all-gather.13
  363.1 59.9 all-gather.7

commit v3 on v0

--- a/solution.py
+++ b/solution.py
@@ -264,15 +264,20 @@
     clips = lax.axis_size("dp")
     width = target.shape[1] // clips
     attended_all = lax.all_gather(attended, "dp", axis=0, tiled=False)
-    columns = lax.all_to_all(
-        target.reshape(seq_local, clips, width), "dp", split_axis=1, concat_axis=1, tiled=True
-    )
-    columns = lax.all_gather(columns, "tensor", axis=0, tiled=True)
     grad_scale = -2.0 / math.sqrt(clips * seq_whole)
-    terms = jnp.einsum(
-        "csi,scd->cid", attended_all, columns, preferred_element_type=jnp.float32
-    )
-    gradient = jnp.sum((grad_scale * terms).astype(jnp.bfloat16).astype(jnp.float32), axis=0)
+    half = width // 2
+    split_target = target.reshape(seq_local, clips, width)
+    pieces = []
+    for part in range(2):
+        columns = lax.all_to_all(
+            split_target[:, :, part * half : (part + 1) * half], "dp", split_axis=1, concat_axis=1, tiled=True
+        )
+        columns = lax.all_gather(columns, "tensor", axis=0, tiled=True)
+        terms = jnp.einsum(
+            "csi,scd->cid", attended_all, columns, preferred_element_type=jnp.float32
+        )
+        pieces.append(jnp.sum((grad_scale * terms).astype(jnp.bfloat16).astype(jnp.float32), axis=0))
+    gradient = jnp.concatenate(pieces, axis=1)
     return (target[None], gradient)
 
 

time: 413 us -> 410 us (level)
  waiting for transfers between devices: 169 us -> 159 us
  blocking collectives: 98.4 us -> 106 us
    all_gather x1 -> x2, waiting for transfers between devices: 58.9 us -> 48.6 us  [local(): columns = lax.all_gather(columns, 'tensor', axis=0, tiled=True)]
    all_to_all x1 -> x2, blocking collectives: 35.3 us -> 42.5 us  [local(): lax.all_to_all(split_target[:, :, part * half:(part + 1) * half], 'dp', s...]
    dot_general x1 -> x2, matrix products: 12.4 us -> 15.6 us  [local(): jnp.einsum('csi,scd->cid', attended_all, columns, preferred_element_type=...]
  transfers between devices with their start and end apart: 9 -> 10, of which waited for: 8 -> 9; matrix products, arithmetic and copies ran while one was open for 12% -> 12% of each run, Pallas kernels for 8% -> 8%
where the time goes in v3:
time: 410 us; the launch traced here: 409 us
  waiting for transfers between devices  159 us (39%)
  blocking collectives  106 us (26%)
  matrix products  34.8 us (8%)
  Pallas kernels  31.2 us (8%)
  local copies, waits for them, and re-layouts  26.8 us (7%)
  starting transfers between devices  23.1 us (6%)
  between operations  15.4 us (4%)
  other arithmetic  13.5 us (3%)
    all_to_all x1, blocking collectives, local(): lax.all_to_all(partial_value.astype(jnp.bfloat16).reshape(groups, seq_loc...  63 us
    all_to_all x6, waiting for transfers between devices, local(): lax.all_to_all(source[0], 'tensor', split_axis=1, concat_axis=0, tiled=True)  61 us
    all_gather x1, waiting for transfers between devices, local(): pieces = lax.all_gather(stacked, 'dp', axis=2, tiled=True)  49.1 us
    all_gather x2, waiting for transfers between devices, local(): columns = lax.all_gather(columns, 'tensor', axis=0, tiled=True)  48.6 us
    all_to_all x2, blocking collectives, local(): lax.all_to_all(split_target[:, :, part * half:(part + 1) * half], 'dp', s...  42.5 us
    pallas_call x2, Pallas kernels, head_call(): pl.pallas_call(kernel, grid=(heads,), in_specs=in_specs, out_specs=[head_...  31.2 us
    all_to_all x6, starting transfers between devices, local(): lax.all_to_all(source[0], 'tensor', split_axis=1, concat_axis=0, tiled=True)  22.7 us
    all_to_all x12, local copies, waits for them, and re-layouts, local(): lax.all_to_all(source[0], 'tensor', split_axis=1, concat_axis=0, tiled=True)  16.9 us
  transfers between devices with their start and end apart: 10, of which 9 were waited for; matrix products, arithmetic and copies ran while one was open for 12% of the time, Pallas kernels for 8%

profile of v3, /device:TPU:0, one launch (start us, length us, event | category | flops | bytes accessed | tf_op | source)
XLA Modules:
  0.0 409.1 jit_solution(11361844241075438768)
XLA Ops:
  7.2 3.5 pad_maximum_fusion
  14.0 5.2 %all-to-all-start.2 = ((bf16[128,4,1024]{2,0,1:T(8,128)(2,1)}), bf16[128,4,1024]{2,0,1:T(8,128)(2,1)S(1)}, u32[]{:S(2)}, u32[]{:S(2)}) async-start(bf16[128,4,1024]{2,0,1:T(8,128)(2,1)} %copy.37), calls=%async_computation.2 | async-start | bytes 2097152 | tf_op jit(solution)/shard_map/all_to_all | solution.py:222
  21.3 11.5 %all-to-all-done.2 = bf16[128,4,1024]{2,0,1:T(8,128)(2,1)S(1)} async-done(((bf16[128,4,1024]{2,0,1:T(8,128)(2,1)}), bf16[128,4,1024]{2,0,1:T(8,128)(2,1)S(1)}, u32[]{:S(2)}, u32[]{:S(2)}) %all-to-all-start.2) | async-done | bytes 1048608 | tf_op jit(solution)/shard_map/all_to_all | solution.py:222
  32.8 3.5 all-to-all-start.3
  36.3 1.9 all_to_all.109
  39.5 10.0 %all-to-all-done.3 = bf16[128,4,1024]{2,0,1:T(8,128)(2,1)S(1)} async-done(((bf16[128,4,1024]{2,0,1:T(8,128)(2,1)}), bf16[128,4,1024]{2,0,1:T(8,128)(2,1)S(1)}, u32[]{:S(2)}, u32[]{:S(2)}) %all-to-all-start.3) | async-done | bytes 1048608 | tf_op jit(solution)/shard_map/all_to_all | solution.py:222
  49.5 3.5 all-to-all-start.4
  53.0 1.9 all_to_all.113
  56.3 9.9 %all-to-all-done.4 = bf16[128,4,1024]{2,0,1:T(8,128)(2,1)S(1)} async-done(((bf16[128,4,1024]{2,0,1:T(8,128)(2,1)}), bf16[128,4,1024]{2,0,1:T(8,128)(2,1)S(1)}, u32[]{:S(2)}, u32[]{:S(2)}) %all-to-all-start.4) | async-done | bytes 1048608 | tf_op jit(solution)/shard_map/all_to_all | solution.py:222
  66.2 3.5 all-to-all-start.5
  72.8 10.0 %all-to-all-done.5 = bf16[128,4,1024]{2,0,1:T(8,128)(2,1)S(1)} async-done(((bf16[128,4,1024]{2,0,1:T(8,128)(2,1)}), bf16[128,4,1024]{2,0,1:T(8,128)(2,1)S(1)}, u32[]{:S(2)}, u32[]{:S(2)}) %all-to-all-start.5) | async-done | bytes 1048608 | tf_op jit(solution)/shard_map/all_to_all | solution.py:222
  82.8 3.5 all-to-all-start
  90.4 9.1 %all-to-all-done = bf16[128,4,1024]{2,0,1:T(8,128)(2,1)S(1)} async-done(((bf16[128,4,1024]{2,0,1:T(8,128)(2,1)}), bf16[128,4,1024]{2,0,1:T(8,128)(2,1)S(1)}, u32[]{:S(2)}, u32[]{:S(2)}) %all-to-all-start) | async-done | bytes 1048608 | tf_op jit(solution)/shard_map/all_to_all | solution.py:222
  99.5 3.5 all-to-all-start.1
  105.8 10.4 %all-to-all-done.1 = bf16[128,4,1024]{2,0,1:T(8,128)(2,1)S(1)} async-done(((bf16[128,4,1024]{2,0,1:T(8,128)(2,1)}), bf16[128,4,1024]{2,0,1:T(8,128)(2,1)S(1)}, u32[]{:S(2)}, u32[]{:S(2)}) %all-to-all-start.1) | async-done | bytes 1048608 | tf_op jit(solution)/shard_map/all_to_all | solution.py:222
  117.2 15.9 %shard_map.158 = (bf16[512,1024]{1,0:T(8,128)(2,1)}, bf16[512,1024]{1,0:T(8,128)(2,1)}) custom-call(f32[2]{0:T(128)} %pad_maximum_fusion.4.scal, f32[512,128]{1,0:T(8,128)} %get-tuple-element.20.cos_ref, f32[512,128]{1,0:T(8,128)} %get-tuple-element.21.sin_ref, bf16[512,1024]{1,0:T(8,128)(2,1)} %bitcast.63, bf16[512,1024]{1,0:T(8,128)(2,1)} %bitcast.64, ...), custom_call_target="tpu_custom_call" | custom-call | tf_op jit(solution)/shard_map/pallas_call | solution.py:178
  134.6 15.2 %shard_map.159 = bf16[512,1024]{1,0:T(8,128)(2,1)} custom-call(f32[2]{0:T(128)} %pad_maximum_fusion.5.scal, f32[512,128]{1,0:T(8,128)} %get-tuple-element.20.cos_ref, f32[512,128]{1,0:T(8,128)} %get-tuple-element.21.sin_ref, bf16[2,512,1024]{2,1,0:T(8,128)(2,1)} %bitcast.52, bf16[2,512,1024]{2,1,0:T(8,128)(2,1)} %bitcast.54, bf16[2,512,1024]{2,1,0:T(8,128)(2,1)} %bitcast.56, ...), custom_call_target="tpu_custom_call" | custom-call | tf_op jit(solution)/shard_map/pallas_call | solution.py:178
  149.9 49.1 %all-gather.6.cloned.1.call-done = bf16[2,1024,5120]{2,1,0:T(8,128)(2,1)} async-done(((bf16[2,1024,640]{2,1,0:T(8,128)(2,1)}), bf16[2,1024,5120]{2,1,0:T(8,128)(2,1)}) %all-gather.6.cloned.1.call-update) | async-done | bytes 20971536 | tf_op jit(solution)/shard_map/all_gather | solution.py:250
  199.0 8.6 %fusion = f32[512,5120]{1,0:T(8,128)S(1)} fusion(bf16[512,1024]{1,0:T(8,128)(2,1)} %shard_map.159, bf16[2,1024,5120]{2,1,0:T(8,128)(2,1)} %all-gather.6.cloned.1.call-done), kind=kOutput, calls=%fused_computation.1 | convolution fusion | flops 5368709120 | bytes 22020096 | tf_op jit(solution)/shard_map/dot_general | solution.py:251
  207.5 10.6 %add_convert_fusion = bf16[512,5120]{1,0:T(8,128)(2,1)S(1)} fusion(f32[512,5120]{1,0:T(8,128)S(1)} %fusion, bf16[512,1024]{1,0:T(8,128)(2,1)S(1)} %copy-done.11, bf16[2,1024,5120]{2,1,0:T(8,128)(2,1)} %all-gather.6.cloned.1.call-done), kind=kOutput, calls=%fused_computation.9 | convolution fusion | flops 5373952000 | bytes 27262976 | tf_op jit(solution)/shard_map/dot_general | solution.py:251
  218.2 63.0 %all_to_all.129 = bf16[4,128,5120]{2,1,0:T(8,128)(2,1)S(1)} all-to-all(bf16[4,128,5120]{2,1,0:T(8,128)(2,1)S(1)} %bitcast.58), channel_id=1, replica_groups=mesh['dp'=8,'tensor'=4] {'tensor'}, dimensions={0} | all-to-all | bytes 10485760 | tf_op jit(solution)/shard_map/all_to_all | solution.py:255
  282.1 2.1 copy.41
  284.2 3.6 convert_multiply_fusion
  287.9 3.4 copy.42
  291.3 2.0 subtract_convert_fusion
  293.4 21.3 %all_to_all.130 = bf16[128,8,320]{0,2,1:T(8,128)(2,1)} all-to-all(bf16[128,8,320]{0,2,1:T(8,128)(2,1)S(1)} %get-tuple-element.10), channel_id=1, replica_groups=mesh['dp'=8,'tensor'=4] {'dp'}, dimensions={1} | all-to-all | bytes 1310720 | tf_op jit(solution)/shard_map/all_to_all | solution.py:272
  314.7 21.3 %all_to_all.131 = bf16[128,8,320]{0,2,1:T(8,128)(2,1)} all-to-all(bf16[128,8,320]{0,2,1:T(8,128)(2,1)S(1)} %get-tuple-element.11), channel_id=1, replica_groups=mesh['dp'=8,'tensor'=4] {'dp'}, dimensions={1} | all-to-all | bytes 1310720 | tf_op jit(solution)/shard_map/all_to_all | solution.py:272
  336.0 15.7 %all-gather.8.cloned.1.call-done = bf16[512,8,320]{0,2,1:T(8,128)(2,1)} async-done(((bf16[128,8,320]{0,2,1:T(8,128)(2,1)}), bf16[512,8,320]{0,2,1:T(8,128)(2,1)}) %all-gather.8.cloned.1.call-update) | async-done | bytes 2621456 | tf_op jit(solution)/shard_map/all_gather | solution.py:275
  351.7 8.3 %convert_reduce_fusion.1 = f32[1024,320]{0,1:T(8,128)} fusion(bf16[512,8,320]{0,2,1:T(8,128)(2,1)} %all-gather.8.cloned.1.call-done, bf16[8,512,1024]{2,1,0:T(8,128)(2,1)} %bitcast.70), kind=kOutput, calls=%fused_computation.6 | convolution fusion | flops 2694512640 | bytes 12320768 | tf_op jit(solution)/shard_map/csi,scd->cid/dot_general | solution.py:276
  360.0 32.9 %all-gather.10.cloned.1.call-done = bf16[512,8,320]{0,2,1:T(8,128)(2,1)} async-done(((bf16[128,8,320]{0,2,1:T(8,128)(2,1)}), bf16[512,8,320]{0,2,1:T(8,128)(2,1)}) %all-gather.10.cloned.1.call-update) | async-done | bytes 2621456 | tf_op jit(solution)/shard_map/all_gather | solution.py:275
  392.9 7.3 %convert_reduce_fusion = f32[1024,320]{0,1:T(8,128)S(1)} fusion(bf16[512,8,320]{0,2,1:T(8,128)(2,1)} %all-gather.10.cloned.1.call-done, bf16[8,512,1024]{2,1,0:T(8,128)(2,1)} %bitcast.71), kind=kOutput, calls=%fused_computation.4 | convolution fusion | flops 2694512640 | bytes 12320768 | tf_op jit(solution)/shard_map/csi,scd->cid/dot_general | solution.py:276
  400.5 2.1 copy.43
  (54 shorter events, 20.3 us)
Async XLA Ops:
  7.2 191.8 %all-gather.6.cloned.1.call-start = ((), (), s32[]{:S(2)}) async-start(), calls=%async_computation.9 | async-start | bytes 23592960 | tf_op jit(solution)/shard_map/all_gather | solution.py:250
  10.7 1.2 copy-start.8
  11.9 7.2 %copy-start.9 = (bf16[1,128,4096]{2,1,0:T(8,128)(2,1)S(1)}, bf16[1,128,4096]{2,1,0:T(8,128)(2,1)}, u32[]{:S(2)}) copy-start(bf16[1,128,4096]{2,1,0:T(8,128)(2,1)} %param.25) | copy-start | bytes 3145732
  14.0 18.8 %all-to-all-start.2 = ((bf16[128,4,1024]{2,0,1:T(8,128)(2,1)}), bf16[128,4,1024]{2,0,1:T(8,128)(2,1)S(1)}, u32[]{:S(2)}, u32[]{:S(2)}) async-start(bf16[128,4,1024]{2,0,1:T(8,128)(2,1)} %copy.37), calls=%async_computation.2 | async-start | bytes 2097152 | tf_op jit(solution)/shard_map/all_to_all | solution.py:222
  32.8 6.7 %copy-start.1 = (bf16[128,4,1024]{2,0,1:T(8,128)(2,1)}, bf16[128,4,1024]{2,0,1:T(8,128)(2,1)S(1)}, u32[]{:S(2)}) copy-start(bf16[128,4,1024]{2,0,1:T(8,128)(2,1)S(1)} %all-to-all-done.2) | copy-start | bytes 3145732
  32.8 16.7 %all-to-all-start.3 = ((bf16[128,4,1024]{2,0,1:T(8,128)(2,1)}), bf16[128,4,1024]{2,0,1:T(8,128)(2,1)S(1)}, u32[]{:S(2)}, u32[]{:S(2)}) async-start(bf16[128,4,1024]{2,0,1:T(8,128)(2,1)} %copy.38), calls=%async_computation.3 | async-start | bytes 2097152 | tf_op jit(solution)/shard_map/all_to_all | solution.py:222
  49.5 6.8 %copy-start.2 = (bf16[128,4,1024]{2,0,1:T(8,128)(2,1)}, bf16[128,4,1024]{2,0,1:T(8,128)(2,1)S(1)}, u32[]{:S(2)}) copy-start(bf16[128,4,1024]{2,0,1:T(8,128)(2,1)S(1)} %all-to-all-done.3) | copy-start | bytes 3145732
  49.5 16.7 %all-to-all-start.4 = ((bf16[128,4,1024]{2,0,1:T(8,128)(2,1)}), bf16[128,4,1024]{2,0,1:T(8,128)(2,1)S(1)}, u32[]{:S(2)}, u32[]{:S(2)}) async-start(bf16[128,4,1024]{2,0,1:T(8,128)(2,1)} %copy.39), calls=%async_computation.4 | async-start | bytes 2097152 | tf_op jit(solution)/shard_map/all_to_all | solution.py:222
  66.2 6.7 %copy-start.3 = (bf16[128,4,1024]{2,0,1:T(8,128)(2,1)}, bf16[128,4,1024]{2,0,1:T(8,128)(2,1)S(1)}, u32[]{:S(2)}) copy-start(bf16[128,4,1024]{2,0,1:T(8,128)(2,1)S(1)} %all-to-all-done.4) | copy-start | bytes 3145732
  66.2 16.7 %all-to-all-start.5 = ((bf16[128,4,1024]{2,0,1:T(8,128)(2,1)}), bf16[128,4,1024]{2,0,1:T(8,128)(2,1)S(1)}, u32[]{:S(2)}, u32[]{:S(2)}) async-start(bf16[128,4,1024]{2,0,1:T(8,128)(2,1)} %copy.40), calls=%async_computation.5 | async-start | bytes 2097152 | tf_op jit(solution)/shard_map/all_to_all | solution.py:222
  82.8 7.6 %copy-start.4 = (bf16[128,4,1024]{2,0,1:T(8,128)(2,1)}, bf16[128,4,1024]{2,0,1:T(8,128)(2,1)S(1)}, u32[]{:S(2)}) copy-start(bf16[128,4,1024]{2,0,1:T(8,128)(2,1)S(1)} %all-to-all-done.5) | copy-start | bytes 3145732
  82.8 16.7 %all-to-all-start = ((bf16[128,4,1024]{2,0,1:T(8,128)(2,1)}), bf16[128,4,1024]{2,0,1:T(8,128)(2,1)S(1)}, u32[]{:S(2)}, u32[]{:S(2)}) async-start(bf16[128,4,1024]{2,0,1:T(8,128)(2,1)} %copy.35), calls=%async_computation | async-start | bytes 2097152 | tf_op jit(solution)/shard_map/all_to_all | solution.py:222
  89.0 14.7 %copy-start.10 = (s32[1,3,512]{2,0,1:T(1,128)S(1)}, s32[1,3,512]{2,0,1:T(1,128)}, u32[]{:S(2)}) copy-start(s32[1,3,512]{2,0,1:T(1,128)} %param.17) | copy-start | bytes 18436
  99.5 16.7 %copy-start.5 = (bf16[128,4,1024]{2,0,1:T(8,128)(2,1)}, bf16[128,4,1024]{2,0,1:T(8,128)(2,1)S(1)}, u32[]{:S(2)}) copy-start(bf16[128,4,1024]{2,0,1:T(8,128)(2,1)S(1)} %all-to-all-done) | copy-start | bytes 3145732
  99.5 16.7 %all-to-all-start.1 = ((bf16[128,4,1024]{2,0,1:T(8,128)(2,1)}), bf16[128,4,1024]{2,0,1:T(8,128)(2,1)S(1)}, u32[]{:S(2)}, u32[]{:S(2)}) async-start(bf16[128,4,1024]{2,0,1:T(8,128)(2,1)} %copy.36), calls=%async_computation.1 | async-start | bytes 2097152 | tf_op jit(solution)/shard_map/all_to_all | solution.py:222
  103.0 233.0 %all-gather.12.cloned.1.call-start = ((), (), s32[]{:S(2)}) async-start(), calls=%async_computation.12 | async-start | bytes 9437184 | tf_op jit(solution)/shard_map/all_gather | solution.py:266
  116.2 1.0 copy-start.6
  133.2 218.5 %all-gather.8.cloned.1.call-start = ((), (), s32[]{:S(2)}) async-start(), calls=%async_computation.10 | async-start | bytes 3276800 | tf_op jit(solution)/shard_map/all_gather | solution.py:275
  149.9 57.7 %copy-start.11 = (bf16[512,1024]{1,0:T(8,128)(2,1)S(1)}, bf16[512,1024]{1,0:T(8,128)(2,1)}, u32[]{:S(2)}) copy-start(bf16[512,1024]{1,0:T(8,128)(2,1)} %get-tuple-element.4) | copy-start | bytes 3145732
  287.9 3.4 copy-start
  314.7 78.2 %all-gather.10.cloned.1.call-start = ((), (), s32[]{:S(2)}) async-start(), calls=%async_computation.11 | async-start | bytes 3276800 | tf_op jit(solution)/shard_map/all_gather | solution.py:275
  392.9 7.3 %copy-start.7 = (f32[1024,320]{0,1:T(8,128)S(1)}, f32[1024,320]{0,1:T(8,128)}, u32[]{:S(2)}) copy-start(f32[1024,320]{0,1:T(8,128)} %convert_reduce_fusion.1) | copy-start | bytes 3932164
Sparse Core Ops, SparseCore 0:
  10.8 188.0 all-gather.5
  200.6 80.2 all-gather.11
  314.8 36.8 all-gather.7
  353.4 39.4 all-gather.9

commit v4 on v3

--- a/solution.py
+++ b/solution.py
@@ -246,11 +246,11 @@
         [Operand(a) for a in arrived],
         [jax.ShapeDtypeStruct((seq_whole, cols), jnp.bfloat16)] * 2,
     )
-    stacked = jnp.stack([student_out, teacher_out])
-    pieces = lax.all_gather(stacked, "dp", axis=2, tiled=True)
-    partial_value = jnp.dot(student_term, pieces[0], preferred_element_type=jnp.float32) + jnp.dot(
-        teacher_term, pieces[1], preferred_element_type=jnp.float32
-    )
+    teacher_whole = lax.all_gather(teacher_out, "dp", axis=1, tiled=True)
+    student_whole = lax.all_gather(student_out, "dp", axis=1, tiled=True)
+    teacher_partial = jnp.dot(teacher_term, teacher_whole, preferred_element_type=jnp.float32)
+    teacher_partial, student_whole = lax.optimization_barrier((teacher_partial, student_whole))
+    partial_value = jnp.dot(student_term, student_whole, preferred_element_type=jnp.float32) + teacher_partial
     latent_weight = cos_time * sin_time
     pieces_in = lax.all_to_all(
         partial_value.astype(jnp.bfloat16).reshape(groups, seq_local, -1),

time: 410 us -> 414 us (level)
  waiting for transfers between devices: 159 us -> 165 us
    all_gather x1 -> x2, waiting for transfers between devices: 49.1 us -> 53.5 us  [the longest x1 53.5 us: local(): student_whole = lax.all_gather(student_out, 'dp', axis=1, tiled=True)]
  transfers between devices with their start and end apart: 10 -> 11, of which waited for: 9 -> 9; matrix products, arithmetic and copies ran while one was open for 12% -> 13% of each run, Pallas kernels for 8% -> 8%
where the time goes in v4:
time: 414 us; the launch traced here: 413 us
  waiting for transfers between devices  165 us (40%)
  blocking collectives  105 us (25%)
  matrix products  38.1 us (9%)
  Pallas kernels  31.1 us (8%)
  local copies, waits for them, and re-layouts  25.4 us (6%)
  starting transfers between devices  23.1 us (6%)
  between operations  15.5 us (4%)
  other arithmetic  10.1 us (2%)
    all_to_all x1, blocking collectives, local(): lax.all_to_all(partial_value.astype(jnp.bfloat16).reshape(groups, seq_loc...  62.9 us
    all_to_all x6, waiting for transfers between devices, local(): lax.all_to_all(source[0], 'tensor', split_axis=1, concat_axis=0, tiled=True)  61.1 us
    all_gather x1, waiting for transfers between devices, local(): student_whole = lax.all_gather(student_out, 'dp', axis=1, tiled=True)  53.5 us
    all_gather x2, waiting for transfers between devices, local(): columns = lax.all_gather(columns, 'tensor', axis=0, tiled=True)  48.6 us
    all_to_all x2, blocking collectives, local(): lax.all_to_all(split_target[:, :, part * half:(part + 1) * half], 'dp', s...  42.5 us
    pallas_call x2, Pallas kernels, head_call(): pl.pallas_call(kernel, grid=(heads,), in_specs=in_specs, out_specs=[head_...  31.1 us
    all_to_all x6, starting transfers between devices, local(): lax.all_to_all(source[0], 'tensor', split_axis=1, concat_axis=0, tiled=True)  22.8 us
    all_to_all x12, local copies, waits for them, and re-layouts, local(): lax.all_to_all(source[0], 'tensor', split_axis=1, concat_axis=0, tiled=True)  16.7 us
  transfers between devices with their start and end apart: 11, of which 9 were waited for; matrix products, arithmetic and copies ran while one was open for 13% of the time, Pallas kernels for 8%

profile of v4, /device:TPU:0, one launch (start us, length us, event | category | flops | bytes accessed | tf_op | source)
XLA Modules:
  0.0 413.4 jit_solution(2941023161411380610)
XLA Ops:
  10.8 5.2 %all-to-all-start.2 = ((bf16[128,4,1024]{2,0,1:T(8,128)(2,1)}), bf16[128,4,1024]{2,0,1:T(8,128)(2,1)S(1)}, u32[]{:S(2)}, u32[]{:S(2)}) async-start(bf16[128,4,1024]{2,0,1:T(8,128)(2,1)} %copy.37), calls=%async_computation.2 | async-start | bytes 2097152 | tf_op jit(solution)/shard_map/all_to_all | solution.py:222
  18.0 11.6 %all-to-all-done.2 = bf16[128,4,1024]{2,0,1:T(8,128)(2,1)S(1)} async-done(((bf16[128,4,1024]{2,0,1:T(8,128)(2,1)}), bf16[128,4,1024]{2,0,1:T(8,128)(2,1)S(1)}, u32[]{:S(2)}, u32[]{:S(2)}) %all-to-all-start.2) | async-done | bytes 1048608 | tf_op jit(solution)/shard_map/all_to_all | solution.py:222
  29.6 3.5 all-to-all-start.3
  33.1 1.9 all_to_all.109
  36.2 10.0 %all-to-all-done.3 = bf16[128,4,1024]{2,0,1:T(8,128)(2,1)S(1)} async-done(((bf16[128,4,1024]{2,0,1:T(8,128)(2,1)}), bf16[128,4,1024]{2,0,1:T(8,128)(2,1)S(1)}, u32[]{:S(2)}, u32[]{:S(2)}) %all-to-all-start.3) | async-done | bytes 1048608 | tf_op jit(solution)/shard_map/all_to_all | solution.py:222
  46.3 3.5 all-to-all-start.4
  49.8 1.9 all_to_all.113
  53.0 10.0 %all-to-all-done.4 = bf16[128,4,1024]{2,0,1:T(8,128)(2,1)S(1)} async-done(((bf16[128,4,1024]{2,0,1:T(8,128)(2,1)}), bf16[128,4,1024]{2,0,1:T(8,128)(2,1)S(1)}, u32[]{:S(2)}, u32[]{:S(2)}) %all-to-all-start.4) | async-done | bytes 1048608 | tf_op jit(solution)/shard_map/all_to_all | solution.py:222
  62.9 3.5 all-to-all-start.5
  66.5 1.9 all_to_all.93
  69.6 10.0 %all-to-all-done.5 = bf16[128,4,1024]{2,0,1:T(8,128)(2,1)S(1)} async-done(((bf16[128,4,1024]{2,0,1:T(8,128)(2,1)}), bf16[128,4,1024]{2,0,1:T(8,128)(2,1)S(1)}, u32[]{:S(2)}, u32[]{:S(2)}) %all-to-all-start.5) | async-done | bytes 1048608 | tf_op jit(solution)/shard_map/all_to_all | solution.py:222
  79.6 3.5 all-to-all-start
  87.2 9.1 %all-to-all-done = bf16[128,4,1024]{2,0,1:T(8,128)(2,1)S(1)} async-done(((bf16[128,4,1024]{2,0,1:T(8,128)(2,1)}), bf16[128,4,1024]{2,0,1:T(8,128)(2,1)S(1)}, u32[]{:S(2)}, u32[]{:S(2)}) %all-to-all-start) | async-done | bytes 1048608 | tf_op jit(solution)/shard_map/all_to_all | solution.py:222
  96.3 3.5 all-to-all-start.1
  102.6 10.4 %all-to-all-done.1 = bf16[128,4,1024]{2,0,1:T(8,128)(2,1)S(1)} async-done(((bf16[128,4,1024]{2,0,1:T(8,128)(2,1)}), bf16[128,4,1024]{2,0,1:T(8,128)(2,1)S(1)}, u32[]{:S(2)}, u32[]{:S(2)}) %all-to-all-start.1) | async-done | bytes 1048608 | tf_op jit(solution)/shard_map/all_to_all | solution.py:222
  114.0 15.9 %shard_map.158 = (bf16[512,1024]{1,0:T(8,128)(2,1)}, bf16[512,1024]{1,0:T(8,128)(2,1)}) custom-call(f32[2]{0:T(128)} %pad_maximum_fusion.3.scal, f32[512,128]{1,0:T(8,128)} %get-tuple-element.24.cos_ref, f32[512,128]{1,0:T(8,128)} %get-tuple-element.25.sin_ref, bf16[512,1024]{1,0:T(8,128)(2,1)} %bitcast.55, bf16[512,1024]{1,0:T(8,128)(2,1)} %bitcast.56, ...), custom_call_target="tpu_custom_call" | custom-call | tf_op jit(solution)/shard_map/pallas_call | solution.py:178
  131.3 15.2 %shard_map.159 = bf16[512,1024]{1,0:T(8,128)(2,1)} custom-call(f32[2]{0:T(128)} %pad_maximum_fusion.4.scal, f32[512,128]{1,0:T(8,128)} %get-tuple-element.24.cos_ref, f32[512,128]{1,0:T(8,128)} %get-tuple-element.25.sin_ref, bf16[2,512,1024]{2,1,0:T(8,128)(2,1)} %bitcast.44, bf16[2,512,1024]{2,1,0:T(8,128)(2,1)} %bitcast.46, bf16[2,512,1024]{2,1,0:T(8,128)(2,1)} %bitcast.48, ...), custom_call_target="tpu_custom_call" | custom-call | tf_op jit(solution)/shard_map/pallas_call | solution.py:178
  146.6 11.0 %fusion.10 = f32[512,5120]{1,0:T(8,128)} fusion(bf16[512,1024]{1,0:T(8,128)(2,1)} %shard_map.159, bf16[1024,5120]{1,0:T(8,128)(2,1)} %all-gather.7.cloned.1.call-done), kind=kOutput, calls=%fused_computation.36 | convolution fusion | flops 5368709120 | bytes 22020096 | tf_op jit(solution)/shard_map/dot_general | solution.py:251
  157.6 53.5 %all-gather.9.cloned.1.call-done = bf16[1024,5120]{1,0:T(8,128)(2,1)} async-done(((bf16[1024,640]{1,0:T(8,128)(2,1)}), bf16[1024,5120]{1,0:T(8,128)(2,1)}) %all-gather.9.cloned.1.call-update) | async-done | bytes 10485776 | tf_op jit(solution)/shard_map/all_gather | solution.py:250
  211.1 11.5 %add_convert_fusion = bf16[512,5120]{1,0:T(8,128)(2,1)S(1)} fusion(f32[512,5120]{1,0:T(8,128)} %fusion.10, bf16[512,1024]{1,0:T(8,128)(2,1)S(1)} %copy-done.11, bf16[1024,5120]{1,0:T(8,128)(2,1)} %all-gather.9.cloned.1.call-done), kind=kOutput, calls=%fused_computation.5 | convolution fusion | flops 5373952000 | bytes 27262976 | tf_op jit(solution)/shard_map/dot_general | solution.py:253
  222.6 62.9 %all_to_all.129 = bf16[4,128,5120]{2,1,0:T(8,128)(2,1)S(1)} all-to-all(bf16[4,128,5120]{2,1,0:T(8,128)(2,1)S(1)} %bitcast.50), channel_id=1, replica_groups=mesh['dp'=8,'tensor'=4] {'tensor'}, dimensions={0} | all-to-all | bytes 10485760 | tf_op jit(solution)/shard_map/all_to_all | solution.py:255
  286.4 2.1 copy.41
  288.5 3.6 convert_multiply_fusion
  292.2 3.4 copy.42
  295.6 2.0 subtract_convert_fusion
  297.7 21.3 %all_to_all.130 = bf16[128,8,320]{0,2,1:T(8,128)(2,1)} all-to-all(bf16[128,8,320]{0,2,1:T(8,128)(2,1)S(1)} %get-tuple-element.14), channel_id=1, replica_groups=mesh['dp'=8,'tensor'=4] {'dp'}, dimensions={1} | all-to-all | bytes 1310720 | tf_op jit(solution)/shard_map/all_to_all | solution.py:272
  319.0 21.3 %all_to_all.131 = bf16[128,8,320]{0,2,1:T(8,128)(2,1)} all-to-all(bf16[128,8,320]{0,2,1:T(8,128)(2,1)S(1)} %get-tuple-element.15), channel_id=1, replica_groups=mesh['dp'=8,'tensor'=4] {'dp'}, dimensions={1} | all-to-all | bytes 1310720 | tf_op jit(solution)/shard_map/all_to_all | solution.py:272
  340.3 15.7 %all-gather.11.cloned.1.call-done = bf16[512,8,320]{0,2,1:T(8,128)(2,1)} async-done(((bf16[128,8,320]{0,2,1:T(8,128)(2,1)}), bf16[512,8,320]{0,2,1:T(8,128)(2,1)}) %all-gather.11.cloned.1.call-update) | async-done | bytes 2621456 | tf_op jit(solution)/shard_map/all_gather | solution.py:275
  356.0 8.3 %convert_reduce_fusion.1 = f32[1024,320]{0,1:T(8,128)} fusion(bf16[512,8,320]{0,2,1:T(8,128)(2,1)} %all-gather.11.cloned.1.call-done, bf16[8,512,1024]{2,1,0:T(8,128)(2,1)} %bitcast.60), kind=kOutput, calls=%fused_computation.2 | convolution fusion | flops 2694512640 | bytes 12320768 | tf_op jit(solution)/shard_map/csi,scd->cid/dot_general | solution.py:276
  364.4 32.9 %all-gather.13.cloned.1.call-done = bf16[512,8,320]{0,2,1:T(8,128)(2,1)} async-done(((bf16[128,8,320]{0,2,1:T(8,128)(2,1)}), bf16[512,8,320]{0,2,1:T(8,128)(2,1)}) %all-gather.13.cloned.1.call-update) | async-done | bytes 2621456 | tf_op jit(solution)/shard_map/all_gather | solution.py:275
  397.2 7.3 %convert_reduce_fusion = f32[1024,320]{0,1:T(8,128)S(1)} fusion(bf16[512,8,320]{0,2,1:T(8,128)(2,1)} %all-gather.13.cloned.1.call-done, bf16[8,512,1024]{2,1,0:T(8,128)(2,1)} %bitcast.61), kind=kOutput, calls=%fused_computation | convolution fusion | flops 2694512640 | bytes 12320768 | tf_op jit(solution)/shard_map/csi,scd->cid/dot_general | solution.py:276
  404.8 2.1 copy.43
  (56 shorter events, 18.5 us)
Async XLA Ops:
  7.2 1.5 copy-start.8
  7.2 139.4 %all-gather.7.cloned.1.call-start = ((), (), s32[]{:S(2)}) async-start(), calls=%async_computation.9 | async-start | bytes 11796480 | tf_op jit(solution)/shard_map/all_gather | solution.py:249
  7.9 203.2 %all-gather.9.cloned.1.call-start = ((), (), s32[]{:S(2)}) async-start(), calls=%async_computation.10 | async-start | bytes 11796480 | tf_op jit(solution)/shard_map/all_gather | solution.py:250
  8.7 7.3 %copy-start.9 = (bf16[1,128,4096]{2,1,0:T(8,128)(2,1)S(1)}, bf16[1,128,4096]{2,1,0:T(8,128)(2,1)}, u32[]{:S(2)}) copy-start(bf16[1,128,4096]{2,1,0:T(8,128)(2,1)} %param.25) | copy-start | bytes 3145732
  10.8 18.8 %all-to-all-start.2 = ((bf16[128,4,1024]{2,0,1:T(8,128)(2,1)}), bf16[128,4,1024]{2,0,1:T(8,128)(2,1)S(1)}, u32[]{:S(2)}, u32[]{:S(2)}) async-start(bf16[128,4,1024]{2,0,1:T(8,128)(2,1)} %copy.37), calls=%async_computation.2 | async-start | bytes 2097152 | tf_op jit(solution)/shard_map/all_to_all | solution.py:222
  29.6 6.7 %copy-start.1 = (bf16[128,4,1024]{2,0,1:T(8,128)(2,1)}, bf16[128,4,1024]{2,0,1:T(8,128)(2,1)S(1)}, u32[]{:S(2)}) copy-start(bf16[128,4,1024]{2,0,1:T(8,128)(2,1)S(1)} %all-to-all-done.2) | copy-start | bytes 3145732
  29.6 16.7 %all-to-all-start.3 = ((bf16[128,4,1024]{2,0,1:T(8,128)(2,1)}), bf16[128,4,1024]{2,0,1:T(8,128)(2,1)S(1)}, u32[]{:S(2)}, u32[]{:S(2)}) async-start(bf16[128,4,1024]{2,0,1:T(8,128)(2,1)} %copy.38), calls=%async_computation.3 | async-start | bytes 2097152 | tf_op jit(solution)/shard_map/all_to_all | solution.py:222
  46.3 6.7 %copy-start.2 = (bf16[128,4,1024]{2,0,1:T(8,128)(2,1)}, bf16[128,4,1024]{2,0,1:T(8,128)(2,1)S(1)}, u32[]{:S(2)}) copy-start(bf16[128,4,1024]{2,0,1:T(8,128)(2,1)S(1)} %all-to-all-done.3) | copy-start | bytes 3145732
  46.3 16.7 %all-to-all-start.4 = ((bf16[128,4,1024]{2,0,1:T(8,128)(2,1)}), bf16[128,4,1024]{2,0,1:T(8,128)(2,1)S(1)}, u32[]{:S(2)}, u32[]{:S(2)}) async-start(bf16[128,4,1024]{2,0,1:T(8,128)(2,1)} %copy.39), calls=%async_computation.4 | async-start | bytes 2097152 | tf_op jit(solution)/shard_map/all_to_all | solution.py:222
  62.9 6.7 %copy-start.3 = (bf16[128,4,1024]{2,0,1:T(8,128)(2,1)}, bf16[128,4,1024]{2,0,1:T(8,128)(2,1)S(1)}, u32[]{:S(2)}) copy-start(bf16[128,4,1024]{2,0,1:T(8,128)(2,1)S(1)} %all-to-all-done.4) | copy-start | bytes 3145732
  62.9 16.7 %all-to-all-start.5 = ((bf16[128,4,1024]{2,0,1:T(8,128)(2,1)}), bf16[128,4,1024]{2,0,1:T(8,128)(2,1)S(1)}, u32[]{:S(2)}, u32[]{:S(2)}) async-start(bf16[128,4,1024]{2,0,1:T(8,128)(2,1)} %copy.40), calls=%async_computation.5 | async-start | bytes 2097152 | tf_op jit(solution)/shard_map/all_to_all | solution.py:222
  79.6 7.5 %copy-start.4 = (bf16[128,4,1024]{2,0,1:T(8,128)(2,1)}, bf16[128,4,1024]{2,0,1:T(8,128)(2,1)S(1)}, u32[]{:S(2)}) copy-start(bf16[128,4,1024]{2,0,1:T(8,128)(2,1)S(1)} %all-to-all-done.5) | copy-start | bytes 3145732
  79.6 16.7 %all-to-all-start = ((bf16[128,4,1024]{2,0,1:T(8,128)(2,1)}), bf16[128,4,1024]{2,0,1:T(8,128)(2,1)S(1)}, u32[]{:S(2)}, u32[]{:S(2)}) async-start(bf16[128,4,1024]{2,0,1:T(8,128)(2,1)} %copy.35), calls=%async_computation | async-start | bytes 2097152 | tf_op jit(solution)/shard_map/all_to_all | solution.py:222
  85.8 14.7 %copy-start.10 = (s32[1,3,512]{2,0,1:T(1,128)S(1)}, s32[1,3,512]{2,0,1:T(1,128)}, u32[]{:S(2)}) copy-start(s32[1,3,512]{2,0,1:T(1,128)} %param.17) | copy-start | bytes 18436
  96.3 16.7 %copy-start.5 = (bf16[128,4,1024]{2,0,1:T(8,128)(2,1)}, bf16[128,4,1024]{2,0,1:T(8,128)(2,1)S(1)}, u32[]{:S(2)}) copy-start(bf16[128,4,1024]{2,0,1:T(8,128)(2,1)S(1)} %all-to-all-done) | copy-start | bytes 3145732
  96.3 16.7 %all-to-all-start.1 = ((bf16[128,4,1024]{2,0,1:T(8,128)(2,1)}), bf16[128,4,1024]{2,0,1:T(8,128)(2,1)S(1)}, u32[]{:S(2)}, u32[]{:S(2)}) async-start(bf16[128,4,1024]{2,0,1:T(8,128)(2,1)} %copy.36), calls=%async_computation.1 | async-start | bytes 2097152 | tf_op jit(solution)/shard_map/all_to_all | solution.py:222
  99.8 240.5 %all-gather.15.cloned.1.call-start = ((), (), s32[]{:S(2)}) async-start(), calls=%async_computation.13 | async-start | bytes 9437184 | tf_op jit(solution)/shard_map/all_gather | solution.py:266
  113.0 1.0 copy-start.6
  129.9 226.2 %all-gather.11.cloned.1.call-start = ((), (), s32[]{:S(2)}) async-start(), calls=%async_computation.11 | async-start | bytes 3276800 | tf_op jit(solution)/shard_map/all_gather | solution.py:275
  146.6 64.5 %copy-start.11 = (bf16[512,1024]{1,0:T(8,128)(2,1)S(1)}, bf16[512,1024]{1,0:T(8,128)(2,1)}, u32[]{:S(2)}) copy-start(bf16[512,1024]{1,0:T(8,128)(2,1)} %get-tuple-element.6) | copy-start | bytes 3145732
  292.2 3.4 copy-start
  319.0 78.3 %all-gather.13.cloned.1.call-start = ((), (), s32[]{:S(2)}) async-start(), calls=%async_computation.12 | async-start | bytes 3276800 | tf_op jit(solution)/shard_map/all_gather | solution.py:275
  397.2 7.3 %copy-start.7 = (f32[1024,320]{0,1:T(8,128)S(1)}, f32[1024,320]{0,1:T(8,128)}, u32[]{:S(2)}) copy-start(f32[1024,320]{0,1:T(8,128)} %convert_reduce_fusion.1) | copy-start | bytes 3932164
Sparse Core Ops, SparseCore 0:
  9.6 102.0 all-gather.6
  113.3 97.7 all-gather.8
  212.7 80.4 all-gather.14
  319.1 36.8 all-gather.10
  357.7 39.4 all-gather.12

commit v5 on v3

--- a/solution.py
+++ b/solution.py
@@ -268,13 +268,21 @@
     half = width // 2
     split_target = target.reshape(seq_local, clips, width)
     pieces = []
+    me = lax.axis_index("dp")
+    by_block = jnp.transpose(split_target, (1, 0, 2))
     for part in range(2):
-        columns = lax.all_to_all(
-            split_target[:, :, part * half : (part + 1) * half], "dp", split_axis=1, concat_axis=1, tiled=True
-        )
-        columns = lax.all_gather(columns, "tensor", axis=0, tiled=True)
+        blocks = by_block[:, :, part * half : (part + 1) * half]
+        received = [lax.dynamic_index_in_dim(blocks, me, 0, keepdims=False)]
+        for shift in range(1, clips):
+            outgoing = lax.dynamic_index_in_dim(blocks, (me + shift) % clips, 0, keepdims=False)
+            received.append(
+                lax.ppermute(outgoing, "dp", [(i, (i + shift) % clips) for i in range(clips)])
+            )
+        order = (me - jnp.arange(clips)) % clips
+        columns = jnp.take(jnp.stack(received), order, axis=0)
+        columns = lax.all_gather(columns, "tensor", axis=1, tiled=True)
         terms = jnp.einsum(
-            "csi,scd->cid", attended_all, columns, preferred_element_type=jnp.float32
+            "csi,csd->cid", attended_all, columns, preferred_element_type=jnp.float32
         )
         pieces.append(jnp.sum((grad_scale * terms).astype(jnp.bfloat16).astype(jnp.float32), axis=0))
     gradient = jnp.concatenate(pieces, axis=1)

time: 410 us -> 430 us (1.049)
  blocking collectives: 106 us -> 0 us
  waiting for transfers between devices: 159 us -> 253 us
  starting transfers between devices: 23.1 us -> 47.2 us
  other arithmetic: 13.5 us -> 18.2 us
    all_to_all x3 -> x0, blocking collectives: 106 us -> none  [the longest x1 63 us: local(): lax.all_to_all(partial_value.astype(jnp.bfloat16).reshape(groups, seq_loc...]
    all_to_all x0 -> x1, waiting for transfers between devices: none -> 59.2 us  [local(): lax.all_to_all(partial_value.astype(jnp.bfloat16).reshape(groups, seq_loc...]
    all_gather x2, waiting for transfers between devices: 48.6 us -> 72.2 us  [local(): columns = lax.all_gather(columns, 'tensor', axis=1, tiled=True)]
    ppermute x0 -> x14, starting transfers between devices: none -> 19 us  [local(): lax.ppermute(outgoing, 'dp', [(i, (i + shift) % clips) for i in range(cli...]
    ppermute x0 -> x14, waiting for transfers between devices: none -> 11 us  [local(): lax.ppermute(outgoing, 'dp', [(i, (i + shift) % clips) for i in range(cli...]
    all_to_all x0 -> x1, starting transfers between devices: none -> 5.07 us  [local(): lax.all_to_all(partial_value.astype(jnp.bfloat16).reshape(groups, seq_loc...]
  transfers between devices with their start and end apart: 10 -> 25, of which waited for: 9 -> 16; matrix products, arithmetic and copies ran while one was open for 12% -> 14% of each run, Pallas kernels for 8% -> 7%
where the time goes in v5:
time: 430 us; the launch traced here: 429 us
  waiting for transfers between devices  253 us (59%)
  starting transfers between devices  47.2 us (11%)
  matrix products  36.3 us (8%)
  Pallas kernels  31.1 us (7%)
  local copies, waits for them, and re-layouts  28.3 us (7%)
  other arithmetic  18.2 us (4%)
  between operations  15.7 us (4%)
    all_gather x2, waiting for transfers between devices, local(): columns = lax.all_gather(columns, 'tensor', axis=1, tiled=True)  72.2 us
    all_to_all x6, waiting for transfers between devices, local(): lax.all_to_all(source[0], 'tensor', split_axis=1, concat_axis=0, tiled=True)  60.2 us
    all_to_all x1, waiting for transfers between devices, local(): lax.all_to_all(partial_value.astype(jnp.bfloat16).reshape(groups, seq_loc...  59.2 us
    all_gather x1, waiting for transfers between devices, local(): pieces = lax.all_gather(stacked, 'dp', axis=2, tiled=True)  49.4 us
    pallas_call x2, Pallas kernels, head_call(): pl.pallas_call(kernel, grid=(heads,), in_specs=in_specs, out_specs=[head_...  31.1 us
    all_to_all x6, starting transfers between devices, local(): lax.all_to_all(source[0], 'tensor', split_axis=1, concat_axis=0, tiled=True)  22.7 us
    ppermute x14, starting transfers between devices, local(): lax.ppermute(outgoing, 'dp', [(i, (i + shift) % clips) for i in range(cli...  19 us
    all_to_all x12, local copies, waits for them, and re-layouts, local(): lax.all_to_all(source[0], 'tensor', split_axis=1, concat_axis=0, tiled=True)  16.7 us
  transfers between devices with their start and end apart: 25, of which 16 were waited for; matrix products, arithmetic and copies ran while one was open for 14% of the time, Pallas kernels for 7%

profile of v5, /device:TPU:0, one launch (start us, length us, event | category | flops | bytes accessed | tf_op | source)
XLA Modules:
  0.0 429.4 jit_solution(15803632952904451430)
XLA Ops:
  7.2 3.5 pad_maximum_fusion
  14.0 5.2 %all-to-all-start.2 = ((bf16[128,4,1024]{2,0,1:T(8,128)(2,1)}), bf16[128,4,1024]{2,0,1:T(8,128)(2,1)S(1)}, u32[]{:S(2)}, u32[]{:S(2)}) async-start(bf16[128,4,1024]{2,0,1:T(8,128)(2,1)} %copy.43), calls=%async_computation.2 | async-start | bytes 2097152 | tf_op jit(solution)/shard_map/all_to_all | solution.py:222
  21.2 11.5 %all-to-all-done.2 = bf16[128,4,1024]{2,0,1:T(8,128)(2,1)S(1)} async-done(((bf16[128,4,1024]{2,0,1:T(8,128)(2,1)}), bf16[128,4,1024]{2,0,1:T(8,128)(2,1)S(1)}, u32[]{:S(2)}, u32[]{:S(2)}) %all-to-all-start.2) | async-done | bytes 1048608 | tf_op jit(solution)/shard_map/all_to_all | solution.py:222
  32.8 3.5 all-to-all-start.3
  39.5 10.0 %all-to-all-done.3 = bf16[128,4,1024]{2,0,1:T(8,128)(2,1)S(1)} async-done(((bf16[128,4,1024]{2,0,1:T(8,128)(2,1)}), bf16[128,4,1024]{2,0,1:T(8,128)(2,1)S(1)}, u32[]{:S(2)}, u32[]{:S(2)}) %all-to-all-start.3) | async-done | bytes 1048608 | tf_op jit(solution)/shard_map/all_to_all | solution.py:222
  49.5 3.5 all-to-all-start.4
  56.2 9.9 %all-to-all-done.4 = bf16[128,4,1024]{2,0,1:T(8,128)(2,1)S(1)} async-done(((bf16[128,4,1024]{2,0,1:T(8,128)(2,1)}), bf16[128,4,1024]{2,0,1:T(8,128)(2,1)S(1)}, u32[]{:S(2)}, u32[]{:S(2)}) %all-to-all-start.4) | async-done | bytes 1048608 | tf_op jit(solution)/shard_map/all_to_all | solution.py:222
  66.2 3.5 all-to-all-start.5
  72.8 10.0 %all-to-all-done.5 = bf16[128,4,1024]{2,0,1:T(8,128)(2,1)S(1)} async-done(((bf16[128,4,1024]{2,0,1:T(8,128)(2,1)}), bf16[128,4,1024]{2,0,1:T(8,128)(2,1)S(1)}, u32[]{:S(2)}, u32[]{:S(2)}) %all-to-all-start.5) | async-done | bytes 1048608 | tf_op jit(solution)/shard_map/all_to_all | solution.py:222
  82.8 3.5 all-to-all-start
  90.4 9.2 %all-to-all-done = bf16[128,4,1024]{2,0,1:T(8,128)(2,1)S(1)} async-done(((bf16[128,4,1024]{2,0,1:T(8,128)(2,1)}), bf16[128,4,1024]{2,0,1:T(8,128)(2,1)S(1)}, u32[]{:S(2)}, u32[]{:S(2)}) %all-to-all-start) | async-done | bytes 1048608 | tf_op jit(solution)/shard_map/all_to_all | solution.py:222
  99.5 3.5 all-to-all-start.1
  106.6 9.6 %all-to-all-done.1 = bf16[128,4,1024]{2,0,1:T(8,128)(2,1)S(1)} async-done(((bf16[128,4,1024]{2,0,1:T(8,128)(2,1)}), bf16[128,4,1024]{2,0,1:T(8,128)(2,1)S(1)}, u32[]{:S(2)}, u32[]{:S(2)}) %all-to-all-start.1) | async-done | bytes 1048608 | tf_op jit(solution)/shard_map/all_to_all | solution.py:222
  117.2 15.9 %shard_map.158 = (bf16[512,1024]{1,0:T(8,128)(2,1)}, bf16[512,1024]{1,0:T(8,128)(2,1)}) custom-call(f32[2]{0:T(128)} %pad_maximum_fusion.4.scal, f32[512,128]{1,0:T(8,128)} %pad_maximum_fusion.2.cos_ref, f32[512,128]{1,0:T(8,128)} %pad_maximum_fusion.3.sin_ref, bf16[512,1024]{1,0:T(8,128)(2,1)} %bitcast.121, bf16[512,1024]{1,0:T(8,128)(2,1)} %bitcast.122, ...), custom_call_target="tpu_custom_call" | custom-call | tf_op jit(solution)/shard_map/pallas_call | solution.py:178
  134.3 15.2 %shard_map.159 = bf16[512,1024]{1,0:T(8,128)(2,1)} custom-call(f32[2]{0:T(128)} %pad_maximum_fusion.5.scal, f32[512,128]{1,0:T(8,128)} %pad_maximum_fusion.2.cos_ref, f32[512,128]{1,0:T(8,128)} %pad_maximum_fusion.3.sin_ref, bf16[2,512,1024]{2,1,0:T(8,128)(2,1)} %bitcast.110, bf16[2,512,1024]{2,1,0:T(8,128)(2,1)} %bitcast.112, ...), custom_call_target="tpu_custom_call" | custom-call | tf_op jit(solution)/shard_map/pallas_call | solution.py:178
  149.6 49.4 %all-gather.6.cloned.1.call-done = bf16[2,1024,5120]{2,1,0:T(8,128)(2,1)} async-done(((bf16[2,1024,640]{2,1,0:T(8,128)(2,1)}), bf16[2,1024,5120]{2,1,0:T(8,128)(2,1)}) %all-gather.6.cloned.1.call-update) | async-done | bytes 20971536 | tf_op jit(solution)/shard_map/all_gather | solution.py:250
  199.0 8.6 %fusion = f32[512,5120]{1,0:T(8,128)S(1)} fusion(bf16[512,1024]{1,0:T(8,128)(2,1)} %shard_map.159, bf16[2,1024,5120]{2,1,0:T(8,128)(2,1)} %all-gather.6.cloned.1.call-done), kind=kOutput, calls=%fused_computation.3 | convolution fusion | flops 5368709120 | bytes 22020096 | tf_op jit(solution)/shard_map/dot_general | solution.py:251
  207.5 12.1 %add_convert_fusion = bf16[512,5120]{1,0:T(8,128)(2,1)} fusion(f32[512,5120]{1,0:T(8,128)S(1)} %fusion, bf16[512,1024]{1,0:T(8,128)(2,1)S(1)} %copy-done.11, bf16[2,1024,5120]{2,1,0:T(8,128)(2,1)} %all-gather.6.cloned.1.call-done), kind=kOutput, calls=%fused_computation.11 | convolution fusion | flops 5373952000 | bytes 27262976 | tf_op jit(solution)/shard_map/dot_general | solution.py:251
  219.6 5.1 %all-to-all-start.6 = ((bf16[4,128,5120]{2,1,0:T(8,128)(2,1)}), bf16[4,128,5120]{2,1,0:T(8,128)(2,1)}, u32[]{:S(2)}, u32[]{:S(2)}) async-start(bf16[4,128,5120]{2,1,0:T(8,128)(2,1)} %bitcast.116), calls=%async_computation.6 | async-start | bytes 10485760 | tf_op jit(solution)/shard_map/all_to_all | solution.py:255
  224.9 59.2 %all-to-all-done.6 = bf16[4,128,5120]{2,1,0:T(8,128)(2,1)} async-done(((bf16[4,128,5120]{2,1,0:T(8,128)(2,1)}), bf16[4,128,5120]{2,1,0:T(8,128)(2,1)}, u32[]{:S(2)}, u32[]{:S(2)}) %all-to-all-start.6) | async-done | bytes 5242912 | tf_op jit(solution)/shard_map/all_to_all | solution.py:255
  284.1 3.7 convert_reduce_fusion.2
  287.8 2.1 copy.47
  289.9 3.6 convert_multiply_fusion
  293.5 3.4 copy.48
  300.6 2.7 collective-permute-start.10
  307.4 5.3 %collective-permute-done.9 = bf16[128,320]{0,1:T(8,128)(2,1)S(1)} collective-permute-done((bf16[128,320]{0,1:T(8,128)(2,1)S(1)}, bf16[128,320]{0,1:T(8,128)(2,1)S(1)}, u32[]{:S(2)}, u32[]{:S(2)}) %collective-permute-start.9) | collective-permute-done | bytes 81952 | tf_op jit(solution)/shard_map/ppermute | solution.py:279
  316.1 3.2 collective-permute-start.3
  320.8 5.1 %collective-permute-start.5 = (bf16[128,320]{0,1:T(8,128)(2,1)S(1)}, bf16[128,320]{0,1:T(8,128)(2,1)S(1)}, u32[]{:S(2)}, u32[]{:S(2)}) collective-permute-start(bf16[128,320]{0,1:T(8,128)(2,1)S(1)} %get-tuple-element.16), channel_id=1, source_target_pairs={{0,24},{4,28},{8,0},{12,4},{16,8},{20,12},{24,16},{28,20},{1,25},{... | collective-permute-start | bytes 245768 | tf_op jit(solution)/shard_map/ppermute | solution.py:279
  332.7 39.3 %all-gather.8.cloned.1.call-done = bf16[8,512,320]{1,2,0:T(8,128)(2,1)} async-done(((bf16[8,128,320]{1,2,0:T(8,128)(2,1)}), bf16[8,512,320]{1,2,0:T(8,128)(2,1)}) %all-gather.8.cloned.1.call-update) | async-done | bytes 2621456 | tf_op jit(solution)/shard_map/all_gather | solution.py:283
  372.0 8.3 %convert_reduce_fusion.1 = f32[1024,320]{0,1:T(8,128)} fusion(bf16[8,512,320]{1,2,0:T(8,128)(2,1)} %all-gather.8.cloned.1.call-done, bf16[8,512,1024]{2,1,0:T(8,128)(2,1)} %bitcast.128), kind=kOutput, calls=%fused_computation.8 | convolution fusion | flops 2694512640 | bytes 12320768 | tf_op jit(solution)/shard_map/csi,csd->cid/dot_general | solution.py:284
  380.3 32.9 %all-gather.10.cloned.1.call-done = bf16[8,512,320]{1,2,0:T(8,128)(2,1)} async-done(((bf16[8,128,320]{1,2,0:T(8,128)(2,1)}), bf16[8,512,320]{1,2,0:T(8,128)(2,1)}) %all-gather.10.cloned.1.call-update) | async-done | bytes 2621456 | tf_op jit(solution)/shard_map/all_gather | solution.py:283
  413.2 7.3 %convert_reduce_fusion = f32[1024,320]{0,1:T(8,128)S(1)} fusion(bf16[8,512,320]{1,2,0:T(8,128)(2,1)} %all-gather.10.cloned.1.call-done, bf16[8,512,1024]{2,1,0:T(8,128)(2,1)} %bitcast.129), kind=kOutput, calls=%fused_computation.6 | convolution fusion | flops 2694512640 | bytes 12320768 | tf_op jit(solution)/shard_map/csi,csd->cid/dot_general | solution.py:284
  (103 shorter events, 44.9 us)
Async XLA Ops:
  7.2 191.8 %all-gather.6.cloned.1.call-start = ((), (), s32[]{:S(2)}) async-start(), calls=%async_computation.7 | async-start | bytes 23592960 | tf_op jit(solution)/shard_map/all_gather | solution.py:250
  11.9 7.2 %copy-start.9 = (bf16[1,128,4096]{2,1,0:T(8,128)(2,1)S(1)}, bf16[1,128,4096]{2,1,0:T(8,128)(2,1)}, u32[]{:S(2)}) copy-start(bf16[1,128,4096]{2,1,0:T(8,128)(2,1)} %param.27) | copy-start | bytes 3145732
  14.0 18.8 %all-to-all-start.2 = ((bf16[128,4,1024]{2,0,1:T(8,128)(2,1)}), bf16[128,4,1024]{2,0,1:T(8,128)(2,1)S(1)}, u32[]{:S(2)}, u32[]{:S(2)}) async-start(bf16[128,4,1024]{2,0,1:T(8,128)(2,1)} %copy.43), calls=%async_computation.2 | async-start | bytes 2097152 | tf_op jit(solution)/shard_map/all_to_all | solution.py:222
  32.8 16.7 %all-to-all-start.3 = ((bf16[128,4,1024]{2,0,1:T(8,128)(2,1)}), bf16[128,4,1024]{2,0,1:T(8,128)(2,1)S(1)}, u32[]{:S(2)}, u32[]{:S(2)}) async-start(bf16[128,4,1024]{2,0,1:T(8,128)(2,1)} %copy.44), calls=%async_computation.3 | async-start | bytes 2097152 | tf_op jit(solution)/shard_map/all_to_all | solution.py:222
  49.5 6.7 %copy-start.2 = (bf16[128,4,1024]{2,0,1:T(8,128)(2,1)}, bf16[128,4,1024]{2,0,1:T(8,128)(2,1)S(1)}, u32[]{:S(2)}) copy-start(bf16[128,4,1024]{2,0,1:T(8,128)(2,1)S(1)} %all-to-all-done.3) | copy-start | bytes 3145732
  49.5 16.7 %all-to-all-start.4 = ((bf16[128,4,1024]{2,0,1:T(8,128)(2,1)}), bf16[128,4,1024]{2,0,1:T(8,128)(2,1)S(1)}, u32[]{:S(2)}, u32[]{:S(2)}) async-start(bf16[128,4,1024]{2,0,1:T(8,128)(2,1)} %copy.45), calls=%async_computation.4 | async-start | bytes 2097152 | tf_op jit(solution)/shard_map/all_to_all | solution.py:222
  66.2 16.7 %all-to-all-start.5 = ((bf16[128,4,1024]{2,0,1:T(8,128)(2,1)}), bf16[128,4,1024]{2,0,1:T(8,128)(2,1)S(1)}, u32[]{:S(2)}, u32[]{:S(2)}) async-start(bf16[128,4,1024]{2,0,1:T(8,128)(2,1)} %copy.46), calls=%async_computation.5 | async-start | bytes 2097152 | tf_op jit(solution)/shard_map/all_to_all | solution.py:222
  82.8 7.5 %copy-start.4 = (bf16[128,4,1024]{2,0,1:T(8,128)(2,1)}, bf16[128,4,1024]{2,0,1:T(8,128)(2,1)S(1)}, u32[]{:S(2)}) copy-start(bf16[128,4,1024]{2,0,1:T(8,128)(2,1)S(1)} %all-to-all-done.5) | copy-start | bytes 3145732
  82.8 16.7 %all-to-all-start = ((bf16[128,4,1024]{2,0,1:T(8,128)(2,1)}), bf16[128,4,1024]{2,0,1:T(8,128)(2,1)S(1)}, u32[]{:S(2)}, u32[]{:S(2)}) async-start(bf16[128,4,1024]{2,0,1:T(8,128)(2,1)} %copy.41), calls=%async_computation | async-start | bytes 2097152 | tf_op jit(solution)/shard_map/all_to_all | solution.py:222
  89.0 14.8 %copy-start.10 = (s32[1,3,512]{2,0,1:T(1,128)S(1)}, s32[1,3,512]{2,0,1:T(1,128)}, u32[]{:S(2)}) copy-start(s32[1,3,512]{2,0,1:T(1,128)} %param.19) | copy-start | bytes 18436
  99.5 16.7 %copy-start.5 = (bf16[128,4,1024]{2,0,1:T(8,128)(2,1)}, bf16[128,4,1024]{2,0,1:T(8,128)(2,1)S(1)}, u32[]{:S(2)}) copy-start(bf16[128,4,1024]{2,0,1:T(8,128)(2,1)S(1)} %all-to-all-done) | copy-start | bytes 3145732
  99.5 16.7 %all-to-all-start.1 = ((bf16[128,4,1024]{2,0,1:T(8,128)(2,1)}), bf16[128,4,1024]{2,0,1:T(8,128)(2,1)S(1)}, u32[]{:S(2)}, u32[]{:S(2)}) async-start(bf16[128,4,1024]{2,0,1:T(8,128)(2,1)} %copy.42), calls=%async_computation.1 | async-start | bytes 2097152 | tf_op jit(solution)/shard_map/all_to_all | solution.py:222
  103.0 229.6 %all-gather.12.cloned.1.call-start = ((), (), s32[]{:S(2)}) async-start(), calls=%async_computation.10 | async-start | bytes 9437184 | tf_op jit(solution)/shard_map/all_gather | solution.py:266
  149.6 58.0 %copy-start.11 = (bf16[512,1024]{1,0:T(8,128)(2,1)S(1)}, bf16[512,1024]{1,0:T(8,128)(2,1)}, u32[]{:S(2)}) copy-start(bf16[512,1024]{1,0:T(8,128)(2,1)} %get-tuple-element.5) | copy-start | bytes 3145732
  219.6 64.5 %all-to-all-start.6 = ((bf16[4,128,5120]{2,1,0:T(8,128)(2,1)}), bf16[4,128,5120]{2,1,0:T(8,128)(2,1)}, u32[]{:S(2)}, u32[]{:S(2)}) async-start(bf16[4,128,5120]{2,1,0:T(8,128)(2,1)} %bitcast.116), calls=%async_computation.6 | async-start | bytes 10485760 | tf_op jit(solution)/shard_map/all_to_all | solution.py:255
  224.7 147.3 %all-gather.8.cloned.1.call-start = ((), (), s32[]{:S(2)}) async-start(), calls=%async_computation.8 | async-start | bytes 3276800 | tf_op jit(solution)/shard_map/all_gather | solution.py:283
  299.1 6.1 %collective-permute-start.7 = (bf16[128,320]{0,1:T(8,128)(2,1)S(1)}, bf16[128,320]{0,1:T(8,128)(2,1)S(1)}, u32[]{:S(2)}, u32[]{:S(2)}) collective-permute-start(bf16[128,320]{0,1:T(8,128)(2,1)S(1)} %get-tuple-element.29), channel_id=1, source_target_pairs={{0,4},{4,8},{8,12},{12,16},{16,20},{20,24},{24,28},{28,0},{1,5},{5... | collective-permute-start | bytes 245768 | tf_op jit(solution)/shard_map/ppermute | solution.py:279
  299.1 7.2 %collective-permute-start.8 = (bf16[128,320]{0,1:T(8,128)(2,1)S(1)}, bf16[128,320]{0,1:T(8,128)(2,1)S(1)}, u32[]{:S(2)}, u32[]{:S(2)}) collective-permute-start(bf16[128,320]{0,1:T(8,128)(2,1)S(1)} %get-tuple-element.28), channel_id=1, source_target_pairs={{0,8},{4,12},{8,16},{12,20},{16,24},{20,28},{24,0},{28,4},{1,9},{5... | collective-permute-start | bytes 245768 | tf_op jit(solution)/shard_map/ppermute | solution.py:279
  299.2 13.5 %collective-permute-start.9 = (bf16[128,320]{0,1:T(8,128)(2,1)S(1)}, bf16[128,320]{0,1:T(8,128)(2,1)S(1)}, u32[]{:S(2)}, u32[]{:S(2)}) collective-permute-start(bf16[128,320]{0,1:T(8,128)(2,1)S(1)} %get-tuple-element.27), channel_id=1, source_target_pairs={{0,12},{4,16},{8,20},{12,24},{16,28},{20,0},{24,4},{28,8},{1,13},{... | collective-permute-start | bytes 245768 | tf_op jit(solution)/shard_map/ppermute | solution.py:279
  300.6 12.3 %collective-permute-start.10 = (bf16[128,320]{0,1:T(8,128)(2,1)S(1)}, bf16[128,320]{0,1:T(8,128)(2,1)S(1)}, u32[]{:S(2)}, u32[]{:S(2)}) collective-permute-start(bf16[128,320]{0,1:T(8,128)(2,1)S(1)} %get-tuple-element.26), channel_id=1, source_target_pairs={{0,16},{4,20},{8,24},{12,28},{16,0},{20,4},{24,8},{28,12},{1,17},{... | collective-permute-start | bytes 245768 | tf_op jit(solution)/shard_map/ppermute | solution.py:279
  303.3 11.5 %collective-permute-start.11 = (bf16[128,320]{0,1:T(8,128)(2,1)S(1)}, bf16[128,320]{0,1:T(8,128)(2,1)S(1)}, u32[]{:S(2)}, u32[]{:S(2)}) collective-permute-start(bf16[128,320]{0,1:T(8,128)(2,1)S(1)} %get-tuple-element.25), channel_id=1, source_target_pairs={{0,20},{4,24},{8,28},{12,0},{16,4},{20,8},{24,12},{28,16},{1,21},{... | collective-permute-start | bytes 245768 | tf_op jit(solution)/shard_map/ppermute | solution.py:279
  305.2 10.9 %collective-permute-start.12 = (bf16[128,320]{0,1:T(8,128)(2,1)S(1)}, bf16[128,320]{0,1:T(8,128)(2,1)S(1)}, u32[]{:S(2)}, u32[]{:S(2)}) collective-permute-start(bf16[128,320]{0,1:T(8,128)(2,1)S(1)} %get-tuple-element.24), channel_id=1, source_target_pairs={{0,24},{4,28},{8,0},{12,4},{16,8},{20,12},{24,16},{28,20},{1,25},{... | collective-permute-start | bytes 245768 | tf_op jit(solution)/shard_map/ppermute | solution.py:279
  306.3 13.0 %collective-permute-start.13 = (bf16[128,320]{0,1:T(8,128)(2,1)S(1)}, bf16[128,320]{0,1:T(8,128)(2,1)S(1)}, u32[]{:S(2)}, u32[]{:S(2)}) collective-permute-start(bf16[128,320]{0,1:T(8,128)(2,1)S(1)} %get-tuple-element.23), channel_id=1, source_target_pairs={{0,28},{4,0},{8,4},{12,8},{16,12},{20,16},{24,20},{28,24},{1,29},{... | collective-permute-start | bytes 245768 | tf_op jit(solution)/shard_map/ppermute | solution.py:279
  312.7 8.1 %collective-permute-start = (bf16[128,320]{0,1:T(8,128)(2,1)S(1)}, bf16[128,320]{0,1:T(8,128)(2,1)S(1)}, u32[]{:S(2)}, u32[]{:S(2)}) collective-permute-start(bf16[128,320]{0,1:T(8,128)(2,1)S(1)} %get-tuple-element.21), channel_id=1, source_target_pairs={{0,4},{4,8},{8,12},{12,16},{16,20},{20,24},{24,28},{28,0},{1,5},{5... | collective-permute-start | bytes 245768 | tf_op jit(solution)/shard_map/ppermute | solution.py:279
  312.9 13.0 %collective-permute-start.1 = (bf16[128,320]{0,1:T(8,128)(2,1)S(1)}, bf16[128,320]{0,1:T(8,128)(2,1)S(1)}, u32[]{:S(2)}, u32[]{:S(2)}) collective-permute-start(bf16[128,320]{0,1:T(8,128)(2,1)S(1)} %get-tuple-element.20), channel_id=1, source_target_pairs={{0,8},{4,12},{8,16},{12,20},{16,24},{20,28},{24,0},{28,4},{1,9},{5... | collective-permute-start | bytes 245768 | tf_op jit(solution)/shard_map/ppermute | solution.py:279
  314.8 11.2 %collective-permute-start.2 = (bf16[128,320]{0,1:T(8,128)(2,1)S(1)}, bf16[128,320]{0,1:T(8,128)(2,1)S(1)}, u32[]{:S(2)}, u32[]{:S(2)}) collective-permute-start(bf16[128,320]{0,1:T(8,128)(2,1)S(1)} %get-tuple-element.19), channel_id=1, source_target_pairs={{0,12},{4,16},{8,20},{12,24},{16,28},{20,0},{24,4},{28,8},{1,13},{... | collective-permute-start | bytes 245768 | tf_op jit(solution)/shard_map/ppermute | solution.py:279
  316.1 9.9 %collective-permute-start.3 = (bf16[128,320]{0,1:T(8,128)(2,1)S(1)}, bf16[128,320]{0,1:T(8,128)(2,1)S(1)}, u32[]{:S(2)}, u32[]{:S(2)}) collective-permute-start(bf16[128,320]{0,1:T(8,128)(2,1)S(1)} %get-tuple-element.18), channel_id=1, source_target_pairs={{0,16},{4,20},{8,24},{12,28},{16,0},{20,4},{24,8},{28,12},{1,17},{... | collective-permute-start | bytes 245768 | tf_op jit(solution)/shard_map/ppermute | solution.py:279
  319.3 8.3 %collective-permute-start.4 = (bf16[128,320]{0,1:T(8,128)(2,1)S(1)}, bf16[128,320]{0,1:T(8,128)(2,1)S(1)}, u32[]{:S(2)}, u32[]{:S(2)}) collective-permute-start(bf16[128,320]{0,1:T(8,128)(2,1)S(1)} %get-tuple-element.17), channel_id=1, source_target_pairs={{0,20},{4,24},{8,28},{12,0},{16,4},{20,8},{24,12},{28,16},{1,21},{... | collective-permute-start | bytes 245768 | tf_op jit(solution)/shard_map/ppermute | solution.py:279
  320.8 8.6 %collective-permute-start.5 = (bf16[128,320]{0,1:T(8,128)(2,1)S(1)}, bf16[128,320]{0,1:T(8,128)(2,1)S(1)}, u32[]{:S(2)}, u32[]{:S(2)}) collective-permute-start(bf16[128,320]{0,1:T(8,128)(2,1)S(1)} %get-tuple-element.16), channel_id=1, source_target_pairs={{0,24},{4,28},{8,0},{12,4},{16,8},{20,12},{24,16},{28,20},{1,25},{... | collective-permute-start | bytes 245768 | tf_op jit(solution)/shard_map/ppermute | solution.py:279
  325.9 4.2 collective-permute-start.6
  332.1 81.1 %all-gather.10.cloned.1.call-start = ((), (), s32[]{:S(2)}) async-start(), calls=%async_computation.9 | async-start | bytes 3276800 | tf_op jit(solution)/shard_map/all_gather | solution.py:283
  413.2 7.3 %copy-start.7 = (f32[1024,320]{0,1:T(8,128)S(1)}, f32[1024,320]{0,1:T(8,128)}, u32[]{:S(2)}) copy-start(f32[1024,320]{0,1:T(8,128)} %convert_reduce_fusion.1) | copy-start | bytes 3932164
  (5 other events, 18.9 us)
Sparse Core Ops, SparseCore 0:
  10.8 188.0 all-gather.5
  200.6 80.2 all-gather.11
  332.2 39.7 all-gather.7
  373.7 39.4 all-gather.9

commit v6 on v3

--- a/solution.py
+++ b/solution.py
@@ -247,37 +247,42 @@
         [jax.ShapeDtypeStruct((seq_whole, cols), jnp.bfloat16)] * 2,
     )
     stacked = jnp.stack([student_out, teacher_out])
-    pieces = lax.all_gather(stacked, "dp", axis=2, tiled=True)
-    partial_value = jnp.dot(student_term, pieces[0], preferred_element_type=jnp.float32) + jnp.dot(
-        teacher_term, pieces[1], preferred_element_type=jnp.float32
-    )
+    clips = lax.axis_size("dp")
+    width = student_out.shape[1]
+    half = width // 2
+    pieces = lax.all_gather(stacked, "dp", axis=2, tiled=False)
     latent_weight = cos_time * sin_time
-    pieces_in = lax.all_to_all(
-        partial_value.astype(jnp.bfloat16).reshape(groups, seq_local, -1),
-        "tensor",
-        split_axis=0,
-        concat_axis=0,
-        tiled=True,
-    )
-    velocity = jnp.sum(pieces_in.astype(jnp.float32), axis=0)
-    target = (velocity - latent_weight * latent[0].astype(jnp.float32)).astype(jnp.bfloat16)
-    clips = lax.axis_size("dp")
-    width = target.shape[1] // clips
     attended_all = lax.all_gather(attended, "dp", axis=0, tiled=False)
     grad_scale = -2.0 / math.sqrt(clips * seq_whole)
-    half = width // 2
-    split_target = target.reshape(seq_local, clips, width)
-    pieces = []
+    latent_blocks = latent[0].reshape(seq_local, clips, width)
+    targets = []
+    grads = []
     for part in range(2):
-        columns = lax.all_to_all(
-            split_target[:, :, part * half : (part + 1) * half], "dp", split_axis=1, concat_axis=1, tiled=True
-        )
+        chosen = slice(part * half, (part + 1) * half)
+        weights = pieces[:, :, :, chosen].reshape(2, pieces.shape[1], clips * half)
+        partial_value = jnp.dot(student_term, weights[0], preferred_element_type=jnp.float32) + jnp.dot(
+            teacher_term, weights[1], preferred_element_type=jnp.float32
+        )
+        pieces_in = lax.all_to_all(
+            partial_value.astype(jnp.bfloat16).reshape(groups, seq_local, clips, half),
+            "tensor",
+            split_axis=0,
+            concat_axis=0,
+            tiled=True,
+        )
+        velocity = jnp.sum(pieces_in.astype(jnp.float32), axis=0)
+        target_part = (
+            velocity - latent_weight * latent_blocks[:, :, chosen].astype(jnp.float32)
+        ).astype(jnp.bfloat16)
+        targets.append(target_part)
+        columns = lax.all_to_all(target_part, "dp", split_axis=1, concat_axis=1, tiled=True)
         columns = lax.all_gather(columns, "tensor", axis=0, tiled=True)
         terms = jnp.einsum(
             "csi,scd->cid", attended_all, columns, preferred_element_type=jnp.float32
         )
-        pieces.append(jnp.sum((grad_scale * terms).astype(jnp.bfloat16).astype(jnp.float32), axis=0))
-    gradient = jnp.concatenate(pieces, axis=1)
+        grads.append(jnp.sum((grad_scale * terms).astype(jnp.bfloat16).astype(jnp.float32), axis=0))
+    target = jnp.concatenate(targets, axis=2).reshape(seq_local, clips * width)
+    gradient = jnp.concatenate(grads, axis=1)
     return (target[None], gradient)
 
 

time: 410 us -> 443 us (1.080)
  blocking collectives: 106 us -> 42.5 us
  local copies, waits for them, and re-layouts: 26.8 us -> 80.6 us
  waiting for transfers between devices: 159 us -> 196 us
  starting transfers between devices: 23.1 us -> 31.6 us
    all_to_all x3 -> x2, blocking collectives: 106 us -> 42.5 us  [local(): lax.all_to_all(target_part, 'dp', split_axis=1, concat_axis=1, tiled=True)]
    all_to_all x0 -> x2, waiting for transfers between devices: none -> 38.3 us  [local(): lax.all_to_all(partial_value.astype(jnp.bfloat16).reshape(groups, seq_loc...]
    all_gather x0 -> x1, local copies, waits for them, and re-layouts: none -> 26.9 us  [local(): pieces = lax.all_gather(stacked, 'dp', axis=2, tiled=False)]
    reshape x0 -> x4, local copies, waits for them, and re-layouts: none -> 15.9 us  [local(): partial_value.astype(jnp.bfloat16).reshape(groups, seq_local, clips, half)]
    slice x1, local copies, waits for them, and re-layouts: 0.09 us -> 11.5 us  [local(): weights[1]]
    all_to_all x0 -> x2, starting transfers between devices: none -> 8.55 us  [local(): lax.all_to_all(partial_value.astype(jnp.bfloat16).reshape(groups, seq_loc...]
    unnamed x25 -> x39, local copies, waits for them, and re-layouts: 4.36 us -> 9.48 us
    dot_general x2 -> x4, matrix products: 19.2 us -> 16.5 us  [the longest x2 8.47 us: local(): jnp.dot(teacher_term, weights[1], preferred_element_type=jnp.float32)]
  transfers between devices with their start and end apart: 10 -> 12, of which waited for: 9 -> 11; matrix products, arithmetic and copies ran while one was open for 12% -> 22% of each run, Pallas kernels for 8% -> 7%
where the time goes in v6:
time: 443 us; the launch traced here: 441 us
  waiting for transfers between devices  196 us (44%)
  local copies, waits for them, and re-layouts  80.6 us (18%)
  blocking collectives  42.5 us (10%)
  matrix products  32.1 us (7%)
  starting transfers between devices  31.6 us (7%)
  Pallas kernels  31.1 us (7%)
  between operations  15.5 us (3%)
  other arithmetic  11.1 us (3%)
    all_to_all x6, waiting for transfers between devices, local(): lax.all_to_all(source[0], 'tensor', split_axis=1, concat_axis=0, tiled=True)  60.8 us
    all_gather x1, waiting for transfers between devices, local(): pieces = lax.all_gather(stacked, 'dp', axis=2, tiled=False)  49.4 us
    all_gather x2, waiting for transfers between devices, local(): columns = lax.all_gather(columns, 'tensor', axis=0, tiled=True)  47.6 us
    all_to_all x2, blocking collectives, local(): lax.all_to_all(target_part, 'dp', split_axis=1, concat_axis=1, tiled=True)  42.5 us
    all_to_all x2, waiting for transfers between devices, local(): lax.all_to_all(partial_value.astype(jnp.bfloat16).reshape(groups, seq_loc...  38.3 us
    pallas_call x2, Pallas kernels, head_call(): pl.pallas_call(kernel, grid=(heads,), in_specs=in_specs, out_specs=[head_...  31.1 us
    all_gather x1, local copies, waits for them, and re-layouts, local(): pieces = lax.all_gather(stacked, 'dp', axis=2, tiled=False)  26.9 us
    all_to_all x6, starting transfers between devices, local(): lax.all_to_all(source[0], 'tensor', split_axis=1, concat_axis=0, tiled=True)  22.7 us
  transfers between devices with their start and end apart: 12, of which 11 were waited for; matrix products, arithmetic and copies ran while one was open for 22% of the time, Pallas kernels for 7%

profile of v6, /device:TPU:0, one launch (start us, length us, event | category | flops | bytes accessed | tf_op | source)
XLA Modules:
  0.0 440.9 jit_solution(5705060395048597409)
XLA Ops:
  14.0 5.2 %all-to-all-start.2 = ((bf16[128,4,1024]{2,0,1:T(8,128)(2,1)}), bf16[128,4,1024]{2,0,1:T(8,128)(2,1)S(1)}, u32[]{:S(2)}, u32[]{:S(2)}) async-start(bf16[128,4,1024]{2,0,1:T(8,128)(2,1)} %copy.53), calls=%async_computation.2 | async-start | bytes 2097152 | tf_op jit(solution)/shard_map/all_to_all | solution.py:222
  21.2 11.5 %all-to-all-done.2 = bf16[128,4,1024]{2,0,1:T(8,128)(2,1)S(1)} async-done(((bf16[128,4,1024]{2,0,1:T(8,128)(2,1)}), bf16[128,4,1024]{2,0,1:T(8,128)(2,1)S(1)}, u32[]{:S(2)}, u32[]{:S(2)}) %all-to-all-start.2) | async-done | bytes 1048608 | tf_op jit(solution)/shard_map/all_to_all | solution.py:222
  32.8 3.5 all-to-all-start.3
  39.5 10.0 %all-to-all-done.3 = bf16[128,4,1024]{2,0,1:T(8,128)(2,1)S(1)} async-done(((bf16[128,4,1024]{2,0,1:T(8,128)(2,1)}), bf16[128,4,1024]{2,0,1:T(8,128)(2,1)S(1)}, u32[]{:S(2)}, u32[]{:S(2)}) %all-to-all-start.3) | async-done | bytes 1048608 | tf_op jit(solution)/shard_map/all_to_all | solution.py:222
  49.5 3.5 all-to-all-start.4
  56.3 9.9 %all-to-all-done.4 = bf16[128,4,1024]{2,0,1:T(8,128)(2,1)S(1)} async-done(((bf16[128,4,1024]{2,0,1:T(8,128)(2,1)}), bf16[128,4,1024]{2,0,1:T(8,128)(2,1)S(1)}, u32[]{:S(2)}, u32[]{:S(2)}) %all-to-all-start.4) | async-done | bytes 1048608 | tf_op jit(solution)/shard_map/all_to_all | solution.py:222
  66.2 3.5 all-to-all-start.5
  72.8 10.0 %all-to-all-done.5 = bf16[128,4,1024]{2,0,1:T(8,128)(2,1)S(1)} async-done(((bf16[128,4,1024]{2,0,1:T(8,128)(2,1)}), bf16[128,4,1024]{2,0,1:T(8,128)(2,1)S(1)}, u32[]{:S(2)}, u32[]{:S(2)}) %all-to-all-start.5) | async-done | bytes 1048608 | tf_op jit(solution)/shard_map/all_to_all | solution.py:222
  82.8 3.5 all-to-all-start
  90.4 9.1 %all-to-all-done = bf16[128,4,1024]{2,0,1:T(8,128)(2,1)S(1)} async-done(((bf16[128,4,1024]{2,0,1:T(8,128)(2,1)}), bf16[128,4,1024]{2,0,1:T(8,128)(2,1)S(1)}, u32[]{:S(2)}, u32[]{:S(2)}) %all-to-all-start) | async-done | bytes 1048608 | tf_op jit(solution)/shard_map/all_to_all | solution.py:222
  99.5 3.5 all-to-all-start.1
  105.9 10.3 %all-to-all-done.1 = bf16[128,4,1024]{2,0,1:T(8,128)(2,1)S(1)} async-done(((bf16[128,4,1024]{2,0,1:T(8,128)(2,1)}), bf16[128,4,1024]{2,0,1:T(8,128)(2,1)S(1)}, u32[]{:S(2)}, u32[]{:S(2)}) %all-to-all-start.1) | async-done | bytes 1048608 | tf_op jit(solution)/shard_map/all_to_all | solution.py:222
  117.2 15.9 %shard_map.158 = (bf16[512,1024]{1,0:T(8,128)(2,1)}, bf16[512,1024]{1,0:T(8,128)(2,1)}) custom-call(f32[2]{0:T(128)} %pad_maximum_fusion.5.scal, f32[512,128]{1,0:T(8,128)} %get-tuple-element.26.cos_ref, f32[512,128]{1,0:T(8,128)} %get-tuple-element.27.sin_ref, bf16[512,1024]{1,0:T(8,128)(2,1)} %bitcast.67, bf16[512,1024]{1,0:T(8,128)(2,1)} %bitcast.68, ...), custom_call_target="tpu_custom_call" | custom-call | tf_op jit(solution)/shard_map/pallas_call | solution.py:178
  134.3 15.2 %shard_map.159 = bf16[512,1024]{1,0:T(8,128)(2,1)} custom-call(f32[2]{0:T(128)} %pad_maximum_fusion.6.scal, f32[512,128]{1,0:T(8,128)} %get-tuple-element.26.cos_ref, f32[512,128]{1,0:T(8,128)} %get-tuple-element.27.sin_ref, bf16[2,512,1024]{2,1,0:T(8,128)(2,1)} %bitcast.49, bf16[2,512,1024]{2,1,0:T(8,128)(2,1)} %bitcast.51, bf16[2,512,1024]{2,1,0:T(8,128)(2,1)} %bitcast.53, ...), custom_call_target="tpu_custom_call" | custom-call | tf_op jit(solution)/shard_map/pallas_call | solution.py:178
  149.6 49.4 %all-gather.11.cloned.1.call-done = bf16[2,1024,5120]{2,1,0:T(8,128)(2,1)} async-done(((bf16[2,1024,640]{2,1,0:T(8,128)(2,1)}), bf16[2,1024,5120]{2,1,0:T(8,128)(2,1)}) %all-gather.11.cloned.1.call-update) | async-done | bytes 20971536 | tf_op jit(solution)/shard_map/all_gather | solution.py:253
  199.0 26.9 %copy.57 = bf16[2,1024,5120]{1,2,0:T(8,128)(2,1)} copy(bf16[2,1024,5120]{2,1,0:T(8,128)(2,1)} %all-gather.11.cloned.1.call-done) | data formatting | bytes 41943040 | tf_op jit(solution)/shard_map/all_gather | solution.py:253
  225.9 11.5 %fusion.8 = (bf16[1,1024,8,320]{1,3,2,0:T(8,128)(2,1)}, bf16[1,1024,8,320]{1,3,2,0:T(8,128)(2,1)S(1)}, bf16[1,1024,8,320]{1,3,2,0:T(8,128)(2,1)S(1)}, bf16[1,1024,8,320]{1,3,2,0:T(8,128)(2,1)}) fusion(bf16[2,1024,8,640]{1,3,2,0:T(8,128)(2,1)} %bitcast.48), kind=kLoop, calls=%fused_computation.37 | loop fusion | bytes 41943040 | tf_op jit(solution)/shard_map/slice | solution.py:264
  240.3 4.2 add_convert_fusion
  244.5 4.8 %reshape.136 = bf16[4,128,8,320]{3,2,1,0:T(8,128)(2,1)S(1)} reshape(bf16[512,2560]{1,0:T(8,128)(2,1)} %add_convert_fusion) | data formatting | bytes 5242880 | tf_op jit(solution)/shard_map/reshape | solution.py:267
  252.5 4.9 %all-to-all-start.7 = ((bf16[4,128,8,320]{1,3,2,0:T(8,128)(2,1)}), bf16[4,128,8,320]{1,3,2,0:T(8,128)(2,1)}, u32[]{:S(2)}, u32[]{:S(2)}) async-start(bf16[4,128,8,320]{1,3,2,0:T(8,128)(2,1)} %copy.62), calls=%async_computation.7 | async-start | bytes 5242880 | tf_op jit(solution)/shard_map/all_to_all | solution.py:266
  257.4 5.1 %fusion.9 = f32[512,2560]{1,0:T(8,128)S(1)} fusion(bf16[512,1024]{1,0:T(8,128)(2,1)S(1)} %copy-done.15, bf16[1024,2560]{0,1:T(8,128)(2,1)} %bitcast.58), kind=kOutput, calls=%fused_computation.38 | convolution fusion | flops 2684354560 | bytes 11534336 | tf_op jit(solution)/shard_map/dot_general | solution.py:263
  262.6 4.2 add_convert_fusion.1
  266.8 4.8 %reshape.135 = bf16[4,128,8,320]{3,2,1,0:T(8,128)(2,1)S(1)} reshape(bf16[512,2560]{1,0:T(8,128)(2,1)} %add_convert_fusion.1) | data formatting | bytes 5242880 | tf_op jit(solution)/shard_map/reshape | solution.py:267
  274.7 13.7 %all-to-all-done.7 = bf16[4,128,8,320]{1,3,2,0:T(8,128)(2,1)} async-done(((bf16[4,128,8,320]{1,3,2,0:T(8,128)(2,1)}), bf16[4,128,8,320]{1,3,2,0:T(8,128)(2,1)}, u32[]{:S(2)}, u32[]{:S(2)}) %all-to-all-start.7) | async-done | bytes 2621472 | tf_op jit(solution)/shard_map/all_to_all | solution.py:266
  288.4 3.7 all-to-all-start.6
  298.0 24.6 %all-to-all-done.6 = bf16[4,128,8,320]{1,3,2,0:T(8,128)(2,1)S(1)} async-done(((bf16[4,128,8,320]{1,3,2,0:T(8,128)(2,1)}), bf16[4,128,8,320]{1,3,2,0:T(8,128)(2,1)S(1)}, u32[]{:S(2)}, u32[]{:S(2)}) %all-to-all-start.6) | async-done | bytes 2621472 | tf_op jit(solution)/shard_map/all_to_all | solution.py:266
  324.6 21.3 %all_to_all.134 = bf16[128,8,320]{0,2,1:T(8,128)(2,1)} all-to-all(bf16[128,8,320]{0,2,1:T(8,128)(2,1)S(1)} %get-tuple-element.18), channel_id=1, replica_groups=mesh['dp'=8,'tensor'=4] {'dp'}, dimensions={1} | all-to-all | bytes 1310720 | tf_op jit(solution)/shard_map/all_to_all | solution.py:278
  345.9 21.3 %all_to_all.135 = bf16[128,8,320]{0,2,1:T(8,128)(2,1)} all-to-all(bf16[128,8,320]{0,2,1:T(8,128)(2,1)S(1)} %get-tuple-element.19), channel_id=1, replica_groups=mesh['dp'=8,'tensor'=4] {'dp'}, dimensions={1} | all-to-all | bytes 1310720 | tf_op jit(solution)/shard_map/all_to_all | solution.py:278
  368.8 14.7 %all-gather.7.cloned.1.call-done = bf16[512,8,320]{0,2,1:T(8,128)(2,1)} async-done(((bf16[128,8,320]{0,2,1:T(8,128)(2,1)}), bf16[512,8,320]{0,2,1:T(8,128)(2,1)}) %all-gather.7.cloned.1.call-update) | async-done | bytes 2621456 | tf_op jit(solution)/shard_map/all_gather | solution.py:279
  383.5 8.3 %convert_reduce_fusion.1 = f32[1024,320]{0,1:T(8,128)} fusion(bf16[512,8,320]{0,2,1:T(8,128)(2,1)} %all-gather.7.cloned.1.call-done, bf16[8,512,1024]{2,1,0:T(8,128)(2,1)} %bitcast.74), kind=kOutput, calls=%fused_computation.2 | convolution fusion | flops 2694512640 | bytes 12320768 | tf_op jit(solution)/shard_map/csi,scd->cid/dot_general | solution.py:280
  391.8 32.9 %all-gather.9.cloned.1.call-done = bf16[512,8,320]{0,2,1:T(8,128)(2,1)} async-done(((bf16[128,8,320]{0,2,1:T(8,128)(2,1)}), bf16[512,8,320]{0,2,1:T(8,128)(2,1)}) %all-gather.9.cloned.1.call-update) | async-done | bytes 2621456 | tf_op jit(solution)/shard_map/all_gather | solution.py:279
  424.7 7.3 %convert_reduce_fusion = f32[1024,320]{0,1:T(8,128)S(1)} fusion(bf16[512,8,320]{0,2,1:T(8,128)(2,1)} %all-gather.9.cloned.1.call-done, bf16[8,512,1024]{2,1,0:T(8,128)(2,1)} %bitcast.75), kind=kOutput, calls=%fused_computation | convolution fusion | flops 2694512640 | bytes 12320768 | tf_op jit(solution)/shard_map/csi,scd->cid/dot_general | solution.py:280
  (78 shorter events, 47.0 us)
Async XLA Ops:
  7.2 191.8 %all-gather.11.cloned.1.call-start = ((), (), s32[]{:S(2)}) async-start(), calls=%async_computation.12 | async-start | bytes 23592960 | tf_op jit(solution)/shard_map/all_gather | solution.py:253
  10.7 1.2 copy-start.9
  11.9 7.2 %copy-start.10 = (bf16[1,128,4096]{2,1,0:T(8,128)(2,1)S(1)}, bf16[1,128,4096]{2,1,0:T(8,128)(2,1)}, u32[]{:S(2)}) copy-start(bf16[1,128,4096]{2,1,0:T(8,128)(2,1)} %param.25) | copy-start | bytes 3145732
  14.0 18.8 %all-to-all-start.2 = ((bf16[128,4,1024]{2,0,1:T(8,128)(2,1)}), bf16[128,4,1024]{2,0,1:T(8,128)(2,1)S(1)}, u32[]{:S(2)}, u32[]{:S(2)}) async-start(bf16[128,4,1024]{2,0,1:T(8,128)(2,1)} %copy.53), calls=%async_computation.2 | async-start | bytes 2097152 | tf_op jit(solution)/shard_map/all_to_all | solution.py:222
  32.8 6.7 %copy-start.2 = (bf16[128,4,1024]{2,0,1:T(8,128)(2,1)}, bf16[128,4,1024]{2,0,1:T(8,128)(2,1)S(1)}, u32[]{:S(2)}) copy-start(bf16[128,4,1024]{2,0,1:T(8,128)(2,1)S(1)} %all-to-all-done.2) | copy-start | bytes 3145732
  32.8 16.7 %all-to-all-start.3 = ((bf16[128,4,1024]{2,0,1:T(8,128)(2,1)}), bf16[128,4,1024]{2,0,1:T(8,128)(2,1)S(1)}, u32[]{:S(2)}, u32[]{:S(2)}) async-start(bf16[128,4,1024]{2,0,1:T(8,128)(2,1)} %copy.54), calls=%async_computation.3 | async-start | bytes 2097152 | tf_op jit(solution)/shard_map/all_to_all | solution.py:222
  49.5 6.8 %copy-start.3 = (bf16[128,4,1024]{2,0,1:T(8,128)(2,1)}, bf16[128,4,1024]{2,0,1:T(8,128)(2,1)S(1)}, u32[]{:S(2)}) copy-start(bf16[128,4,1024]{2,0,1:T(8,128)(2,1)S(1)} %all-to-all-done.3) | copy-start | bytes 3145732
  49.5 16.7 %all-to-all-start.4 = ((bf16[128,4,1024]{2,0,1:T(8,128)(2,1)}), bf16[128,4,1024]{2,0,1:T(8,128)(2,1)S(1)}, u32[]{:S(2)}, u32[]{:S(2)}) async-start(bf16[128,4,1024]{2,0,1:T(8,128)(2,1)} %copy.55), calls=%async_computation.4 | async-start | bytes 2097152 | tf_op jit(solution)/shard_map/all_to_all | solution.py:222
  66.2 6.7 %copy-start.4 = (bf16[128,4,1024]{2,0,1:T(8,128)(2,1)}, bf16[128,4,1024]{2,0,1:T(8,128)(2,1)S(1)}, u32[]{:S(2)}) copy-start(bf16[128,4,1024]{2,0,1:T(8,128)(2,1)S(1)} %all-to-all-done.4) | copy-start | bytes 3145732
  66.2 16.7 %all-to-all-start.5 = ((bf16[128,4,1024]{2,0,1:T(8,128)(2,1)}), bf16[128,4,1024]{2,0,1:T(8,128)(2,1)S(1)}, u32[]{:S(2)}, u32[]{:S(2)}) async-start(bf16[128,4,1024]{2,0,1:T(8,128)(2,1)} %copy.56), calls=%async_computation.5 | async-start | bytes 2097152 | tf_op jit(solution)/shard_map/all_to_all | solution.py:222
  82.8 7.5 %copy-start.5 = (bf16[128,4,1024]{2,0,1:T(8,128)(2,1)}, bf16[128,4,1024]{2,0,1:T(8,128)(2,1)S(1)}, u32[]{:S(2)}) copy-start(bf16[128,4,1024]{2,0,1:T(8,128)(2,1)S(1)} %all-to-all-done.5) | copy-start | bytes 3145732
  82.8 16.7 %all-to-all-start = ((bf16[128,4,1024]{2,0,1:T(8,128)(2,1)}), bf16[128,4,1024]{2,0,1:T(8,128)(2,1)S(1)}, u32[]{:S(2)}, u32[]{:S(2)}) async-start(bf16[128,4,1024]{2,0,1:T(8,128)(2,1)} %copy.51), calls=%async_computation | async-start | bytes 2097152 | tf_op jit(solution)/shard_map/all_to_all | solution.py:222
  89.0 14.8 %copy-start.13 = (s32[1,3,512]{2,0,1:T(1,128)S(1)}, s32[1,3,512]{2,0,1:T(1,128)}, u32[]{:S(2)}) copy-start(s32[1,3,512]{2,0,1:T(1,128)} %param.17) | copy-start | bytes 18436
  99.5 16.7 %copy-start.6 = (bf16[128,4,1024]{2,0,1:T(8,128)(2,1)}, bf16[128,4,1024]{2,0,1:T(8,128)(2,1)S(1)}, u32[]{:S(2)}) copy-start(bf16[128,4,1024]{2,0,1:T(8,128)(2,1)S(1)} %all-to-all-done) | copy-start | bytes 3145732
  99.5 16.7 %all-to-all-start.1 = ((bf16[128,4,1024]{2,0,1:T(8,128)(2,1)}), bf16[128,4,1024]{2,0,1:T(8,128)(2,1)S(1)}, u32[]{:S(2)}, u32[]{:S(2)}) async-start(bf16[128,4,1024]{2,0,1:T(8,128)(2,1)} %copy.52), calls=%async_computation.1 | async-start | bytes 2097152 | tf_op jit(solution)/shard_map/all_to_all | solution.py:222
  103.0 265.7 %all-gather.13.cloned.1.call-start = ((), (), s32[]{:S(2)}) async-start(), calls=%async_computation.13 | async-start | bytes 9437184 | tf_op jit(solution)/shard_map/all_gather | solution.py:255
  116.2 1.0 copy-start.7
  225.9 11.5 %copy-start.14 = (bf16[512,1024]{1,0:T(8,128)(2,1)S(1)}, bf16[512,1024]{1,0:T(8,128)(2,1)}, u32[]{:S(2)}) copy-start(bf16[512,1024]{1,0:T(8,128)(2,1)} %get-tuple-element.4) | copy-start | bytes 3145732
  237.4 2.9 copy-start.11
  252.5 4.9 %copy-start.15 = (bf16[512,1024]{1,0:T(8,128)(2,1)S(1)}, bf16[512,1024]{1,0:T(8,128)(2,1)}, u32[]{:S(2)}) copy-start(bf16[512,1024]{1,0:T(8,128)(2,1)} %get-tuple-element.4) | copy-start | bytes 3145732
  252.5 10.0 %slice-start = ((s8[5242880]{0:T(1024)(128)(4,1)}), s8[1048576]{0:T(1024)(128)(4,1)S(1)}, s32[]{:S(2)}) async-start(s8[5242880]{0:T(1024)(128)(4,1)} %bitcast.55), calls=%async_computation.14 | async-start | bytes 2097152
  252.5 36.0 %all-to-all-start.7 = ((bf16[4,128,8,320]{1,3,2,0:T(8,128)(2,1)}), bf16[4,128,8,320]{1,3,2,0:T(8,128)(2,1)}, u32[]{:S(2)}, u32[]{:S(2)}) async-start(bf16[4,128,8,320]{1,3,2,0:T(8,128)(2,1)} %copy.62), calls=%async_computation.7 | async-start | bytes 5242880 | tf_op jit(solution)/shard_map/all_to_all | solution.py:266
  257.4 5.1 %slice-start.1 = ((s8[5242880]{0:T(1024)(128)(4,1)}), s8[4194304]{0:T(1024)(128)(4,1)S(1)}, s32[]{:S(2)}) async-start(s8[5242880]{0:T(1024)(128)(4,1)} %bitcast.55), calls=%async_computation.15 | async-start | bytes 8388608
  257.4 5.1 %copy-start.12 = (bf16[512,1024]{1,0:T(8,128)(2,1)S(1)}, bf16[512,1024]{1,0:T(8,128)(2,1)}, u32[]{:S(2)}) copy-start(bf16[512,1024]{1,0:T(8,128)(2,1)} %shard_map.159) | copy-start | bytes 3145732
  288.4 34.1 %all-to-all-start.6 = ((bf16[4,128,8,320]{1,3,2,0:T(8,128)(2,1)}), bf16[4,128,8,320]{1,3,2,0:T(8,128)(2,1)S(1)}, u32[]{:S(2)}, u32[]{:S(2)}) async-start(bf16[4,128,8,320]{1,3,2,0:T(8,128)(2,1)} %copy.59), calls=%async_computation.6 | async-start | bytes 5242880 | tf_op jit(solution)/shard_map/all_to_all | solution.py:266
  292.1 91.4 %all-gather.7.cloned.1.call-start = ((), (), s32[]{:S(2)}) async-start(), calls=%async_computation.10 | async-start | bytes 3276800 | tf_op jit(solution)/shard_map/all_gather | solution.py:279
  322.5 1.3 copy-start
  322.5 1.7 copy-start.1
  345.9 78.8 %all-gather.9.cloned.1.call-start = ((), (), s32[]{:S(2)}) async-start(), calls=%async_computation.11 | async-start | bytes 3276800 | tf_op jit(solution)/shard_map/all_gather | solution.py:279
  424.7 7.3 %copy-start.8 = (f32[1024,320]{0,1:T(8,128)S(1)}, f32[1024,320]{0,1:T(8,128)}, u32[]{:S(2)}) copy-start(f32[1024,320]{0,1:T(8,128)} %convert_reduce_fusion.1) | copy-start | bytes 3932164
Sparse Core Ops, SparseCore 0:
  10.8 188.0 all-gather.10
  200.6 80.2 all-gather.12
  346.0 37.4 all-gather.6
  385.2 39.4 all-gather.8

commit v7 on v3

--- a/solution.py
+++ b/solution.py
@@ -248,19 +248,26 @@
     )
     stacked = jnp.stack([student_out, teacher_out])
     pieces = lax.all_gather(stacked, "dp", axis=2, tiled=True)
-    partial_value = jnp.dot(student_term, pieces[0], preferred_element_type=jnp.float32) + jnp.dot(
-        teacher_term, pieces[1], preferred_element_type=jnp.float32
-    )
     latent_weight = cos_time * sin_time
-    pieces_in = lax.all_to_all(
-        partial_value.astype(jnp.bfloat16).reshape(groups, seq_local, -1),
-        "tensor",
-        split_axis=0,
-        concat_axis=0,
-        tiled=True,
-    )
-    velocity = jnp.sum(pieces_in.astype(jnp.float32), axis=0)
-    target = (velocity - latent_weight * latent[0].astype(jnp.float32)).astype(jnp.bfloat16)
+    span = pieces.shape[2] // 2
+    target_parts = []
+    for part in range(2):
+        chosen = slice(part * span, (part + 1) * span)
+        partial_value = jnp.dot(
+            student_term, pieces[0, :, chosen], preferred_element_type=jnp.float32
+        ) + jnp.dot(teacher_term, pieces[1, :, chosen], preferred_element_type=jnp.float32)
+        pieces_in = lax.all_to_all(
+            partial_value.astype(jnp.bfloat16).reshape(groups, seq_local, -1),
+            "tensor",
+            split_axis=0,
+            concat_axis=0,
+            tiled=True,
+        )
+        velocity = jnp.sum(pieces_in.astype(jnp.float32), axis=0)
+        target_parts.append(
+            (velocity - latent_weight * latent[0, :, chosen].astype(jnp.float32)).astype(jnp.bfloat16)
+        )
+    target = jnp.concatenate(target_parts, axis=1)
     clips = lax.axis_size("dp")
     width = target.shape[1] // clips
     attended_all = lax.all_gather(attended, "dp", axis=0, tiled=False)

time: 410 us -> 407 us (level)
  blocking collectives: 106 us -> 42.7 us
  waiting for transfers between devices: 159 us -> 198 us
  starting transfers between devices: 23.1 us -> 31.3 us
  matrix products: 34.8 us -> 39.7 us
  other arithmetic: 13.5 us -> 18.3 us
    all_to_all x1 -> x0, blocking collectives: 63 us -> none  [local(): lax.all_to_all(partial_value.astype(jnp.bfloat16).reshape(groups, seq_loc...]
    all_to_all x0 -> x2, waiting for transfers between devices: none -> 41.4 us  [local(): lax.all_to_all(partial_value.astype(jnp.bfloat16).reshape(groups, seq_loc...]
    all_to_all x0 -> x2, starting transfers between devices: none -> 8.22 us  [local(): lax.all_to_all(partial_value.astype(jnp.bfloat16).reshape(groups, seq_loc...]
    dot_general x2 -> x4, matrix products: 19.2 us -> 24.1 us  [the longest x2 13.8 us: local(): jnp.dot(student_term, pieces[0, :, chosen], preferred_element_type=jnp.fl...]
  transfers between devices with their start and end apart: 10 -> 12, of which waited for: 9 -> 11; matrix products, arithmetic and copies ran while one was open for 12% -> 15% of each run, Pallas kernels for 8% -> 8%
where the time goes in v7:
time: 407 us; the launch traced here: 406 us
  waiting for transfers between devices  198 us (49%)
  blocking collectives  42.7 us (10%)
  matrix products  39.7 us (10%)
  starting transfers between devices  31.3 us (8%)
  Pallas kernels  31.1 us (8%)
  local copies, waits for them, and re-layouts  29.1 us (7%)
  other arithmetic  18.3 us (4%)
  between operations  15.5 us (4%)
    all_to_all x6, waiting for transfers between devices, local(): lax.all_to_all(source[0], 'tensor', split_axis=1, concat_axis=0, tiled=True)  60.8 us
    all_gather x1, waiting for transfers between devices, local(): pieces = lax.all_gather(stacked, 'dp', axis=2, tiled=True)  49.3 us
    all_gather x2, waiting for transfers between devices, local(): columns = lax.all_gather(columns, 'tensor', axis=0, tiled=True)  46.3 us
    all_to_all x2, blocking collectives, local(): lax.all_to_all(split_target[:, :, part * half:(part + 1) * half], 'dp', s...  42.7 us
    all_to_all x2, waiting for transfers between devices, local(): lax.all_to_all(partial_value.astype(jnp.bfloat16).reshape(groups, seq_loc...  41.4 us
    pallas_call x2, Pallas kernels, head_call(): pl.pallas_call(kernel, grid=(heads,), in_specs=in_specs, out_specs=[head_...  31.1 us
    all_to_all x6, starting transfers between devices, local(): lax.all_to_all(source[0], 'tensor', split_axis=1, concat_axis=0, tiled=True)  22.7 us
    all_to_all x12, local copies, waits for them, and re-layouts, local(): lax.all_to_all(source[0], 'tensor', split_axis=1, concat_axis=0, tiled=True)  16.8 us
  transfers between devices with their start and end apart: 12, of which 11 were waited for; matrix products, arithmetic and copies ran while one was open for 15% of the time, Pallas kernels for 8%

profile of v7, /device:TPU:0, one launch (start us, length us, event | category | flops | bytes accessed | tf_op | source)
XLA Modules:
  0.0 405.6 jit_solution(17670569224482415788)
XLA Ops:
  7.2 3.5 pad_maximum_fusion
  14.0 5.2 %all-to-all-start.2 = ((bf16[128,4,1024]{2,0,1:T(8,128)(2,1)}), bf16[128,4,1024]{2,0,1:T(8,128)(2,1)S(1)}, u32[]{:S(2)}, u32[]{:S(2)}) async-start(bf16[128,4,1024]{2,0,1:T(8,128)(2,1)} %copy.41), calls=%async_computation.2 | async-start | bytes 2097152 | tf_op jit(solution)/shard_map/all_to_all | solution.py:222
  21.2 11.5 %all-to-all-done.2 = bf16[128,4,1024]{2,0,1:T(8,128)(2,1)S(1)} async-done(((bf16[128,4,1024]{2,0,1:T(8,128)(2,1)}), bf16[128,4,1024]{2,0,1:T(8,128)(2,1)S(1)}, u32[]{:S(2)}, u32[]{:S(2)}) %all-to-all-start.2) | async-done | bytes 1048608 | tf_op jit(solution)/shard_map/all_to_all | solution.py:222
  32.8 3.5 all-to-all-start.3
  39.5 10.0 %all-to-all-done.3 = bf16[128,4,1024]{2,0,1:T(8,128)(2,1)S(1)} async-done(((bf16[128,4,1024]{2,0,1:T(8,128)(2,1)}), bf16[128,4,1024]{2,0,1:T(8,128)(2,1)S(1)}, u32[]{:S(2)}, u32[]{:S(2)}) %all-to-all-start.3) | async-done | bytes 1048608 | tf_op jit(solution)/shard_map/all_to_all | solution.py:222
  49.5 3.5 all-to-all-start.4
  56.3 9.9 %all-to-all-done.4 = bf16[128,4,1024]{2,0,1:T(8,128)(2,1)S(1)} async-done(((bf16[128,4,1024]{2,0,1:T(8,128)(2,1)}), bf16[128,4,1024]{2,0,1:T(8,128)(2,1)S(1)}, u32[]{:S(2)}, u32[]{:S(2)}) %all-to-all-start.4) | async-done | bytes 1048608 | tf_op jit(solution)/shard_map/all_to_all | solution.py:222
  66.2 3.5 all-to-all-start.5
  72.8 10.0 %all-to-all-done.5 = bf16[128,4,1024]{2,0,1:T(8,128)(2,1)S(1)} async-done(((bf16[128,4,1024]{2,0,1:T(8,128)(2,1)}), bf16[128,4,1024]{2,0,1:T(8,128)(2,1)S(1)}, u32[]{:S(2)}, u32[]{:S(2)}) %all-to-all-start.5) | async-done | bytes 1048608 | tf_op jit(solution)/shard_map/all_to_all | solution.py:222
  82.8 3.5 all-to-all-start
  90.4 9.1 %all-to-all-done = bf16[128,4,1024]{2,0,1:T(8,128)(2,1)S(1)} async-done(((bf16[128,4,1024]{2,0,1:T(8,128)(2,1)}), bf16[128,4,1024]{2,0,1:T(8,128)(2,1)S(1)}, u32[]{:S(2)}, u32[]{:S(2)}) %all-to-all-start) | async-done | bytes 1048608 | tf_op jit(solution)/shard_map/all_to_all | solution.py:222
  99.5 3.5 all-to-all-start.1
  106.0 10.2 %all-to-all-done.1 = bf16[128,4,1024]{2,0,1:T(8,128)(2,1)S(1)} async-done(((bf16[128,4,1024]{2,0,1:T(8,128)(2,1)}), bf16[128,4,1024]{2,0,1:T(8,128)(2,1)S(1)}, u32[]{:S(2)}, u32[]{:S(2)}) %all-to-all-start.1) | async-done | bytes 1048608 | tf_op jit(solution)/shard_map/all_to_all | solution.py:222
  117.2 15.9 %shard_map.158 = (bf16[512,1024]{1,0:T(8,128)(2,1)}, bf16[512,1024]{1,0:T(8,128)(2,1)}) custom-call(f32[2]{0:T(128)} %pad_maximum_fusion.5.scal, f32[512,128]{1,0:T(8,128)} %get-tuple-element.22.cos_ref, f32[512,128]{1,0:T(8,128)} %get-tuple-element.23.sin_ref, bf16[512,1024]{1,0:T(8,128)(2,1)} %bitcast.83, bf16[512,1024]{1,0:T(8,128)(2,1)} %bitcast.84, ...), custom_call_target="tpu_custom_call" | custom-call | tf_op jit(solution)/shard_map/pallas_call | solution.py:178
  134.4 15.2 %shard_map.159 = bf16[512,1024]{1,0:T(8,128)(2,1)} custom-call(f32[2]{0:T(128)} %pad_maximum_fusion.6.scal, f32[512,128]{1,0:T(8,128)} %get-tuple-element.22.cos_ref, f32[512,128]{1,0:T(8,128)} %get-tuple-element.23.sin_ref, bf16[2,512,1024]{2,1,0:T(8,128)(2,1)} %bitcast.69, bf16[2,512,1024]{2,1,0:T(8,128)(2,1)} %bitcast.71, bf16[2,512,1024]{2,1,0:T(8,128)(2,1)} %bitcast.73, ...), custom_call_target="tpu_custom_call" | custom-call | tf_op jit(solution)/shard_map/pallas_call | solution.py:178
  149.6 49.3 %all-gather.6.cloned.1.call-done = bf16[2,1024,5120]{2,1,0:T(8,128)(2,1)} async-done(((bf16[2,1024,640]{2,1,0:T(8,128)(2,1)}), bf16[2,1024,5120]{2,1,0:T(8,128)(2,1)}) %all-gather.6.cloned.1.call-update) | async-done | bytes 20971536 | tf_op jit(solution)/shard_map/all_gather | solution.py:250
  199.0 5.1 %fusion = f32[512,2560]{1,0:T(8,128)S(1)} fusion(bf16[512,1024]{1,0:T(8,128)(2,1)} %shard_map.159, bf16[2,1024,5120]{2,1,0:T(8,128)(2,1)} %all-gather.6.cloned.1.call-done), kind=kOutput, calls=%fused_computation.5 | convolution fusion | flops 2684354560 | bytes 11534336 | tf_op jit(solution)/shard_map/dot_general | solution.py:258
  204.1 7.1 %add_convert_fusion = bf16[512,2560]{1,0:T(8,128)(2,1)} fusion(f32[512,2560]{1,0:T(8,128)S(1)} %fusion, bf16[512,1024]{1,0:T(8,128)(2,1)S(1)} %copy-done.13, bf16[2,1024,5120]{2,1,0:T(8,128)(2,1)} %all-gather.6.cloned.1.call-done), kind=kOutput, calls=%fused_computation.13 | convolution fusion | flops 2686976000 | bytes 14155776 | tf_op jit(solution)/shard_map/dot_general | solution.py:256
  211.2 3.7 all-to-all-start.7
  214.9 5.2 %fusion.2 = f32[512,2560]{1,0:T(8,128)S(1)} fusion(bf16[512,1024]{1,0:T(8,128)(2,1)} %shard_map.159, bf16[2,1024,5120]{2,1,0:T(8,128)(2,1)} %all-gather.6.cloned.1.call-done), kind=kOutput, calls=%fused_computation.9 | convolution fusion | flops 2684354560 | bytes 11534336 | tf_op jit(solution)/shard_map/dot_general | solution.py:258
  220.1 6.7 %add_convert_fusion.1 = bf16[512,2560]{1,0:T(8,128)(2,1)} fusion(f32[512,2560]{1,0:T(8,128)S(1)} %fusion.2, bf16[512,1024]{1,0:T(8,128)(2,1)S(1)} %copy-done.14, bf16[2,1024,5120]{2,1,0:T(8,128)(2,1)} %all-gather.6.cloned.1.call-done), kind=kOutput, calls=%fused_computation.15 | convolution fusion | flops 2686976000 | bytes 14155776 | tf_op jit(solution)/shard_map/dot_general | solution.py:256
  226.8 19.3 %all-to-all-done.7 = bf16[4,128,2560]{2,1,0:T(8,128)(2,1)S(1)} async-done(((bf16[4,128,2560]{2,1,0:T(8,128)(2,1)}), bf16[4,128,2560]{2,1,0:T(8,128)(2,1)S(1)}, u32[]{:S(2)}, u32[]{:S(2)}) %all-to-all-start.7) | async-done | bytes 2621472 | tf_op jit(solution)/shard_map/all_to_all | solution.py:259
  247.6 4.6 %all-to-all-start.6 = ((bf16[4,128,2560]{2,1,0:T(8,128)(2,1)}), bf16[4,128,2560]{2,1,0:T(8,128)(2,1)}, u32[]{:S(2)}, u32[]{:S(2)}) async-start(bf16[4,128,2560]{2,1,0:T(8,128)(2,1)} %bitcast.85), calls=%async_computation.6 | async-start | bytes 5242880 | tf_op jit(solution)/shard_map/all_to_all | solution.py:259
  256.8 2.3 convert_reduce_fusion.2
  260.6 22.1 %all-to-all-done.6 = bf16[4,128,2560]{2,1,0:T(8,128)(2,1)} async-done(((bf16[4,128,2560]{2,1,0:T(8,128)(2,1)}), bf16[4,128,2560]{2,1,0:T(8,128)(2,1)}, u32[]{:S(2)}, u32[]{:S(2)}) %all-to-all-start.6) | async-done | bytes 2621472 | tf_op jit(solution)/shard_map/all_to_all | solution.py:259
  282.7 2.2 convert_reduce_fusion.3
  289.1 21.5 %all_to_all.134 = bf16[128,8,320]{0,2,1:T(8,128)(2,1)} all-to-all(bf16[128,8,320]{0,2,1:T(8,128)(2,1)S(1)} %get-tuple-element.10), channel_id=1, replica_groups=mesh['dp'=8,'tensor'=4] {'dp'}, dimensions={1} | all-to-all | bytes 1310720 | tf_op jit(solution)/shard_map/all_to_all | solution.py:279
  310.6 21.3 %all_to_all.135 = bf16[128,8,320]{0,2,1:T(8,128)(2,1)} all-to-all(bf16[128,8,320]{0,2,1:T(8,128)(2,1)S(1)} %get-tuple-element.11), channel_id=1, replica_groups=mesh['dp'=8,'tensor'=4] {'dp'}, dimensions={1} | all-to-all | bytes 1310720 | tf_op jit(solution)/shard_map/all_to_all | solution.py:279
  334.8 13.4 %all-gather.8.cloned.1.call-done = bf16[512,8,320]{0,2,1:T(8,128)(2,1)} async-done(((bf16[128,8,320]{0,2,1:T(8,128)(2,1)}), bf16[512,8,320]{0,2,1:T(8,128)(2,1)}) %all-gather.8.cloned.1.call-update) | async-done | bytes 2621456 | tf_op jit(solution)/shard_map/all_gather | solution.py:282
  348.2 8.3 %convert_reduce_fusion.1 = f32[1024,320]{0,1:T(8,128)} fusion(bf16[512,8,320]{0,2,1:T(8,128)(2,1)} %all-gather.8.cloned.1.call-done, bf16[8,512,1024]{2,1,0:T(8,128)(2,1)} %bitcast.92), kind=kOutput, calls=%fused_computation.2 | convolution fusion | flops 2694512640 | bytes 12320768 | tf_op jit(solution)/shard_map/csi,scd->cid/dot_general | solution.py:283
  356.5 32.9 %all-gather.10.cloned.1.call-done = bf16[512,8,320]{0,2,1:T(8,128)(2,1)} async-done(((bf16[128,8,320]{0,2,1:T(8,128)(2,1)}), bf16[512,8,320]{0,2,1:T(8,128)(2,1)}) %all-gather.10.cloned.1.call-update) | async-done | bytes 2621456 | tf_op jit(solution)/shard_map/all_gather | solution.py:282
  389.4 7.3 %convert_reduce_fusion = f32[1024,320]{0,1:T(8,128)S(1)} fusion(bf16[512,8,320]{0,2,1:T(8,128)(2,1)} %all-gather.10.cloned.1.call-done, bf16[8,512,1024]{2,1,0:T(8,128)(2,1)} %bitcast.93), kind=kOutput, calls=%fused_computation | convolution fusion | flops 2694512640 | bytes 12320768 | tf_op jit(solution)/shard_map/csi,scd->cid/dot_general | solution.py:283
  (71 shorter events, 39.8 us)
Async XLA Ops:
  7.2 191.8 %all-gather.6.cloned.1.call-start = ((), (), s32[]{:S(2)}) async-start(), calls=%async_computation.10 | async-start | bytes 23592960 | tf_op jit(solution)/shard_map/all_gather | solution.py:250
  10.7 1.2 copy-start.10
  11.9 7.2 %copy-start.11 = (bf16[1,128,4096]{2,1,0:T(8,128)(2,1)S(1)}, bf16[1,128,4096]{2,1,0:T(8,128)(2,1)}, u32[]{:S(2)}) copy-start(bf16[1,128,4096]{2,1,0:T(8,128)(2,1)} %param.25) | copy-start | bytes 3145732
  14.0 18.8 %all-to-all-start.2 = ((bf16[128,4,1024]{2,0,1:T(8,128)(2,1)}), bf16[128,4,1024]{2,0,1:T(8,128)(2,1)S(1)}, u32[]{:S(2)}, u32[]{:S(2)}) async-start(bf16[128,4,1024]{2,0,1:T(8,128)(2,1)} %copy.41), calls=%async_computation.2 | async-start | bytes 2097152 | tf_op jit(solution)/shard_map/all_to_all | solution.py:222
  32.8 6.7 %copy-start.3 = (bf16[128,4,1024]{2,0,1:T(8,128)(2,1)}, bf16[128,4,1024]{2,0,1:T(8,128)(2,1)S(1)}, u32[]{:S(2)}) copy-start(bf16[128,4,1024]{2,0,1:T(8,128)(2,1)S(1)} %all-to-all-done.2) | copy-start | bytes 3145732
  32.8 16.7 %all-to-all-start.3 = ((bf16[128,4,1024]{2,0,1:T(8,128)(2,1)}), bf16[128,4,1024]{2,0,1:T(8,128)(2,1)S(1)}, u32[]{:S(2)}, u32[]{:S(2)}) async-start(bf16[128,4,1024]{2,0,1:T(8,128)(2,1)} %copy.42), calls=%async_computation.3 | async-start | bytes 2097152 | tf_op jit(solution)/shard_map/all_to_all | solution.py:222
  49.5 6.8 %copy-start.4 = (bf16[128,4,1024]{2,0,1:T(8,128)(2,1)}, bf16[128,4,1024]{2,0,1:T(8,128)(2,1)S(1)}, u32[]{:S(2)}) copy-start(bf16[128,4,1024]{2,0,1:T(8,128)(2,1)S(1)} %all-to-all-done.3) | copy-start | bytes 3145732
  49.5 16.7 %all-to-all-start.4 = ((bf16[128,4,1024]{2,0,1:T(8,128)(2,1)}), bf16[128,4,1024]{2,0,1:T(8,128)(2,1)S(1)}, u32[]{:S(2)}, u32[]{:S(2)}) async-start(bf16[128,4,1024]{2,0,1:T(8,128)(2,1)} %copy.43), calls=%async_computation.4 | async-start | bytes 2097152 | tf_op jit(solution)/shard_map/all_to_all | solution.py:222
  66.2 6.7 %copy-start.5 = (bf16[128,4,1024]{2,0,1:T(8,128)(2,1)}, bf16[128,4,1024]{2,0,1:T(8,128)(2,1)S(1)}, u32[]{:S(2)}) copy-start(bf16[128,4,1024]{2,0,1:T(8,128)(2,1)S(1)} %all-to-all-done.4) | copy-start | bytes 3145732
  66.2 16.7 %all-to-all-start.5 = ((bf16[128,4,1024]{2,0,1:T(8,128)(2,1)}), bf16[128,4,1024]{2,0,1:T(8,128)(2,1)S(1)}, u32[]{:S(2)}, u32[]{:S(2)}) async-start(bf16[128,4,1024]{2,0,1:T(8,128)(2,1)} %copy.44), calls=%async_computation.5 | async-start | bytes 2097152 | tf_op jit(solution)/shard_map/all_to_all | solution.py:222
  82.8 7.5 %copy-start.6 = (bf16[128,4,1024]{2,0,1:T(8,128)(2,1)}, bf16[128,4,1024]{2,0,1:T(8,128)(2,1)S(1)}, u32[]{:S(2)}) copy-start(bf16[128,4,1024]{2,0,1:T(8,128)(2,1)S(1)} %all-to-all-done.5) | copy-start | bytes 3145732
  82.8 16.7 %all-to-all-start = ((bf16[128,4,1024]{2,0,1:T(8,128)(2,1)}), bf16[128,4,1024]{2,0,1:T(8,128)(2,1)S(1)}, u32[]{:S(2)}, u32[]{:S(2)}) async-start(bf16[128,4,1024]{2,0,1:T(8,128)(2,1)} %copy.39), calls=%async_computation | async-start | bytes 2097152 | tf_op jit(solution)/shard_map/all_to_all | solution.py:222
  89.0 14.9 %copy-start.12 = (s32[1,3,512]{2,0,1:T(1,128)S(1)}, s32[1,3,512]{2,0,1:T(1,128)}, u32[]{:S(2)}) copy-start(s32[1,3,512]{2,0,1:T(1,128)} %param.17) | copy-start | bytes 18436
  99.5 16.7 %copy-start.7 = (bf16[128,4,1024]{2,0,1:T(8,128)(2,1)}, bf16[128,4,1024]{2,0,1:T(8,128)(2,1)S(1)}, u32[]{:S(2)}) copy-start(bf16[128,4,1024]{2,0,1:T(8,128)(2,1)S(1)} %all-to-all-done) | copy-start | bytes 3145732
  99.5 16.7 %all-to-all-start.1 = ((bf16[128,4,1024]{2,0,1:T(8,128)(2,1)}), bf16[128,4,1024]{2,0,1:T(8,128)(2,1)S(1)}, u32[]{:S(2)}, u32[]{:S(2)}) async-start(bf16[128,4,1024]{2,0,1:T(8,128)(2,1)} %copy.40), calls=%async_computation.1 | async-start | bytes 2097152 | tf_op jit(solution)/shard_map/all_to_all | solution.py:222
  103.0 231.8 %all-gather.12.cloned.1.call-start = ((), (), s32[]{:S(2)}) async-start(), calls=%async_computation.13 | async-start | bytes 9437184 | tf_op jit(solution)/shard_map/all_gather | solution.py:273
  116.2 1.0 copy-start.8
  149.6 54.4 %copy-start.13 = (bf16[512,1024]{1,0:T(8,128)(2,1)S(1)}, bf16[512,1024]{1,0:T(8,128)(2,1)}, u32[]{:S(2)}) copy-start(bf16[512,1024]{1,0:T(8,128)(2,1)} %get-tuple-element.4) | copy-start | bytes 3145732
  211.2 34.8 %all-to-all-start.7 = ((bf16[4,128,2560]{2,1,0:T(8,128)(2,1)}), bf16[4,128,2560]{2,1,0:T(8,128)(2,1)S(1)}, u32[]{:S(2)}, u32[]{:S(2)}) async-start(bf16[4,128,2560]{2,1,0:T(8,128)(2,1)} %bitcast.86), calls=%async_computation.7 | async-start | bytes 5242880 | tf_op jit(solution)/shard_map/all_to_all | solution.py:259
  214.9 5.2 %copy-start.14 = (bf16[512,1024]{1,0:T(8,128)(2,1)S(1)}, bf16[512,1024]{1,0:T(8,128)(2,1)}, u32[]{:S(2)}) copy-start(bf16[512,1024]{1,0:T(8,128)(2,1)} %get-tuple-element.4) | copy-start | bytes 3145732
  246.0 1.5 copy-start
  247.6 35.1 %all-to-all-start.6 = ((bf16[4,128,2560]{2,1,0:T(8,128)(2,1)}), bf16[4,128,2560]{2,1,0:T(8,128)(2,1)}, u32[]{:S(2)}, u32[]{:S(2)}) async-start(bf16[4,128,2560]{2,1,0:T(8,128)(2,1)} %bitcast.85), calls=%async_computation.6 | async-start | bytes 5242880 | tf_op jit(solution)/shard_map/all_to_all | solution.py:259
  252.1 96.0 %all-gather.8.cloned.1.call-start = ((), (), s32[]{:S(2)}) async-start(), calls=%async_computation.11 | async-start | bytes 3276800 | tf_op jit(solution)/shard_map/all_gather | solution.py:282
  286.4 2.1 copy-start.1
  286.4 2.5 copy-start.2
  310.6 78.8 %all-gather.10.cloned.1.call-start = ((), (), s32[]{:S(2)}) async-start(), calls=%async_computation.12 | async-start | bytes 3276800 | tf_op jit(solution)/shard_map/all_gather | solution.py:282
  389.4 7.3 %copy-start.9 = (f32[1024,320]{0,1:T(8,128)S(1)}, f32[1024,320]{0,1:T(8,128)}, u32[]{:S(2)}) copy-start(f32[1024,320]{0,1:T(8,128)} %convert_reduce_fusion.1) | copy-start | bytes 3932164
Sparse Core Ops, SparseCore 0:
  10.8 188.0 all-gather.5
  200.6 80.2 all-gather.11
  310.7 37.4 all-gather.7
  349.9 39.4 all-gather.9

commit v8 on v7

--- a/solution.py
+++ b/solution.py
@@ -279,7 +279,12 @@
         columns = lax.all_to_all(
             split_target[:, :, part * half : (part + 1) * half], "dp", split_axis=1, concat_axis=1, tiled=True
         )
-        columns = lax.all_gather(columns, "tensor", axis=0, tiled=True)
+        if part == 0:
+            columns = lax.all_gather(columns, "tensor", axis=0, tiled=True)
+        else:
+            copies = jnp.broadcast_to(columns[None], (groups,) + columns.shape)
+            columns = lax.all_to_all(copies, "tensor", split_axis=0, concat_axis=0, tiled=True)
+            columns = columns.reshape((groups * seq_local,) + columns.shape[2:])
         terms = jnp.einsum(
             "csi,scd->cid", attended_all, columns, preferred_element_type=jnp.float32
         )

time: 407 us -> 410 us (level)
  blocking collectives: 42.7 us -> 21.5 us
  waiting for transfers between devices: 198 us -> 212 us
  starting transfers between devices: 31.3 us -> 39.4 us
    all_to_all x0 -> x2, waiting for transfers between devices: none -> 59.2 us  [the longest x1 41.8 us: local(): lax.all_to_all(copies, 'tensor', split_axis=0, concat_axis=0, tiled=True)]
    all_gather x2 -> x1, waiting for transfers between devices: 46.3 us -> 0.01 us  [local(): columns = lax.all_gather(columns, 'tensor', axis=0, tiled=True)]
    all_to_all x2 -> x1, blocking collectives: 42.7 us -> 21.5 us  [local(): lax.all_to_all(split_target[:, :, part * half:(part + 1) * half], 'dp', s...]
    all_to_all x0 -> x2, starting transfers between devices: none -> 8.09 us  [the longest x1 4.55 us: local(): lax.all_to_all(copies, 'tensor', split_axis=0, concat_axis=0, tiled=True)]
  transfers between devices with their start and end apart: 12 -> 13, of which waited for: 11 -> 11; matrix products, arithmetic and copies ran while one was open for 15% -> 16% of each run, Pallas kernels for 8% -> 8%
where the time goes in v8:
time: 410 us; the launch traced here: 409 us
  waiting for transfers between devices  212 us (52%)
  matrix products  39.7 us (10%)
  starting transfers between devices  39.4 us (10%)
  local copies, waits for them, and re-layouts  31.3 us (8%)
  Pallas kernels  31.1 us (8%)
  blocking collectives  21.5 us (5%)
  other arithmetic  19 us (5%)
  between operations  15.5 us (4%)
    all_to_all x6, waiting for transfers between devices, local(): lax.all_to_all(source[0], 'tensor', split_axis=1, concat_axis=0, tiled=True)  60.8 us
    all_gather x1, waiting for transfers between devices, local(): pieces = lax.all_gather(stacked, 'dp', axis=2, tiled=True)  49.4 us
    all_to_all x1, waiting for transfers between devices, local(): lax.all_to_all(copies, 'tensor', split_axis=0, concat_axis=0, tiled=True)  41.8 us
    all_to_all x2, waiting for transfers between devices, local(): lax.all_to_all(partial_value.astype(jnp.bfloat16).reshape(groups, seq_loc...  41.4 us
    pallas_call x2, Pallas kernels, head_call(): pl.pallas_call(kernel, grid=(heads,), in_specs=in_specs, out_specs=[head_...  31.1 us
    all_to_all x6, starting transfers between devices, local(): lax.all_to_all(source[0], 'tensor', split_axis=1, concat_axis=0, tiled=True)  22.7 us
    all_to_all x1, blocking collectives, local(): lax.all_to_all(split_target[:, :, part * half:(part + 1) * half], 'dp', s...  21.5 us
    all_to_all x1, waiting for transfers between devices, local(): lax.all_to_all(split_target[:, :, part * half:(part + 1) * half], 'dp', s...  17.4 us
  transfers between devices with their start and end apart: 13, of which 11 were waited for; matrix products, arithmetic and copies ran while one was open for 16% of the time, Pallas kernels for 8%

profile of v8, /device:TPU:0, one launch (start us, length us, event | category | flops | bytes accessed | tf_op | source)
XLA Modules:
  0.0 408.9 jit_solution(109533244159685304)
XLA Ops:
  7.2 3.5 pad_maximum_fusion
  14.0 5.2 %all-to-all-start.2 = ((bf16[128,4,1024]{2,0,1:T(8,128)(2,1)}), bf16[128,4,1024]{2,0,1:T(8,128)(2,1)S(1)}, u32[]{:S(2)}, u32[]{:S(2)}) async-start(bf16[128,4,1024]{2,0,1:T(8,128)(2,1)} %copy.42), calls=%async_computation.2 | async-start | bytes 2097152 | tf_op jit(solution)/shard_map/all_to_all | solution.py:222
  21.3 11.5 %all-to-all-done.2 = bf16[128,4,1024]{2,0,1:T(8,128)(2,1)S(1)} async-done(((bf16[128,4,1024]{2,0,1:T(8,128)(2,1)}), bf16[128,4,1024]{2,0,1:T(8,128)(2,1)S(1)}, u32[]{:S(2)}, u32[]{:S(2)}) %all-to-all-start.2) | async-done | bytes 1048608 | tf_op jit(solution)/shard_map/all_to_all | solution.py:222
  32.8 3.5 all-to-all-start.3
  39.5 10.0 %all-to-all-done.3 = bf16[128,4,1024]{2,0,1:T(8,128)(2,1)S(1)} async-done(((bf16[128,4,1024]{2,0,1:T(8,128)(2,1)}), bf16[128,4,1024]{2,0,1:T(8,128)(2,1)S(1)}, u32[]{:S(2)}, u32[]{:S(2)}) %all-to-all-start.3) | async-done | bytes 1048608 | tf_op jit(solution)/shard_map/all_to_all | solution.py:222
  49.5 3.5 all-to-all-start.4
  56.3 9.9 %all-to-all-done.4 = bf16[128,4,1024]{2,0,1:T(8,128)(2,1)S(1)} async-done(((bf16[128,4,1024]{2,0,1:T(8,128)(2,1)}), bf16[128,4,1024]{2,0,1:T(8,128)(2,1)S(1)}, u32[]{:S(2)}, u32[]{:S(2)}) %all-to-all-start.4) | async-done | bytes 1048608 | tf_op jit(solution)/shard_map/all_to_all | solution.py:222
  66.2 3.5 all-to-all-start.5
  72.8 10.0 %all-to-all-done.5 = bf16[128,4,1024]{2,0,1:T(8,128)(2,1)S(1)} async-done(((bf16[128,4,1024]{2,0,1:T(8,128)(2,1)}), bf16[128,4,1024]{2,0,1:T(8,128)(2,1)S(1)}, u32[]{:S(2)}, u32[]{:S(2)}) %all-to-all-start.5) | async-done | bytes 1048608 | tf_op jit(solution)/shard_map/all_to_all | solution.py:222
  82.8 3.5 all-to-all-start
  90.4 9.1 %all-to-all-done = bf16[128,4,1024]{2,0,1:T(8,128)(2,1)S(1)} async-done(((bf16[128,4,1024]{2,0,1:T(8,128)(2,1)}), bf16[128,4,1024]{2,0,1:T(8,128)(2,1)S(1)}, u32[]{:S(2)}, u32[]{:S(2)}) %all-to-all-start) | async-done | bytes 1048608 | tf_op jit(solution)/shard_map/all_to_all | solution.py:222
  99.5 3.5 all-to-all-start.1
  106.0 10.2 %all-to-all-done.1 = bf16[128,4,1024]{2,0,1:T(8,128)(2,1)S(1)} async-done(((bf16[128,4,1024]{2,0,1:T(8,128)(2,1)}), bf16[128,4,1024]{2,0,1:T(8,128)(2,1)S(1)}, u32[]{:S(2)}, u32[]{:S(2)}) %all-to-all-start.1) | async-done | bytes 1048608 | tf_op jit(solution)/shard_map/all_to_all | solution.py:222
  117.2 15.9 %shard_map.158 = (bf16[512,1024]{1,0:T(8,128)(2,1)}, bf16[512,1024]{1,0:T(8,128)(2,1)}) custom-call(f32[2]{0:T(128)} %pad_maximum_fusion.5.scal, f32[512,128]{1,0:T(8,128)} %get-tuple-element.22.cos_ref, f32[512,128]{1,0:T(8,128)} %get-tuple-element.23.sin_ref, bf16[512,1024]{1,0:T(8,128)(2,1)} %bitcast.89, bf16[512,1024]{1,0:T(8,128)(2,1)} %bitcast.90, ...), custom_call_target="tpu_custom_call" | custom-call | tf_op jit(solution)/shard_map/pallas_call | solution.py:178
  134.3 15.2 %shard_map.159 = bf16[512,1024]{1,0:T(8,128)(2,1)} custom-call(f32[2]{0:T(128)} %pad_maximum_fusion.6.scal, f32[512,128]{1,0:T(8,128)} %get-tuple-element.22.cos_ref, f32[512,128]{1,0:T(8,128)} %get-tuple-element.23.sin_ref, bf16[2,512,1024]{2,1,0:T(8,128)(2,1)} %bitcast.75, bf16[2,512,1024]{2,1,0:T(8,128)(2,1)} %bitcast.77, bf16[2,512,1024]{2,1,0:T(8,128)(2,1)} %bitcast.79, ...), custom_call_target="tpu_custom_call" | custom-call | tf_op jit(solution)/shard_map/pallas_call | solution.py:178
  149.6 49.4 %all-gather.5.cloned.1.call-done = bf16[2,1024,5120]{2,1,0:T(8,128)(2,1)} async-done(((bf16[2,1024,640]{2,1,0:T(8,128)(2,1)}), bf16[2,1024,5120]{2,1,0:T(8,128)(2,1)}) %all-gather.5.cloned.1.call-update) | async-done | bytes 20971536 | tf_op jit(solution)/shard_map/all_gather | solution.py:250
  199.0 5.1 %fusion = f32[512,2560]{1,0:T(8,128)S(1)} fusion(bf16[512,1024]{1,0:T(8,128)(2,1)} %shard_map.159, bf16[2,1024,5120]{2,1,0:T(8,128)(2,1)} %all-gather.5.cloned.1.call-done), kind=kOutput, calls=%fused_computation.5 | convolution fusion | flops 2684354560 | bytes 11534336 | tf_op jit(solution)/shard_map/dot_general | solution.py:258
  204.1 7.1 %add_convert_fusion = bf16[512,2560]{1,0:T(8,128)(2,1)} fusion(f32[512,2560]{1,0:T(8,128)S(1)} %fusion, bf16[512,1024]{1,0:T(8,128)(2,1)S(1)} %copy-done.13, bf16[2,1024,5120]{2,1,0:T(8,128)(2,1)} %all-gather.5.cloned.1.call-done), kind=kOutput, calls=%fused_computation.13 | convolution fusion | flops 2686976000 | bytes 14155776 | tf_op jit(solution)/shard_map/dot_general | solution.py:256
  211.2 3.7 all-to-all-start.7
  214.9 5.2 %fusion.2 = f32[512,2560]{1,0:T(8,128)S(1)} fusion(bf16[512,1024]{1,0:T(8,128)(2,1)} %shard_map.159, bf16[2,1024,5120]{2,1,0:T(8,128)(2,1)} %all-gather.5.cloned.1.call-done), kind=kOutput, calls=%fused_computation.9 | convolution fusion | flops 2684354560 | bytes 11534336 | tf_op jit(solution)/shard_map/dot_general | solution.py:258
  220.1 6.7 %add_convert_fusion.1 = bf16[512,2560]{1,0:T(8,128)(2,1)} fusion(f32[512,2560]{1,0:T(8,128)S(1)} %fusion.2, bf16[512,1024]{1,0:T(8,128)(2,1)S(1)} %copy-done.14, bf16[2,1024,5120]{2,1,0:T(8,128)(2,1)} %all-gather.5.cloned.1.call-done), kind=kOutput, calls=%fused_computation.15 | convolution fusion | flops 2686976000 | bytes 14155776 | tf_op jit(solution)/shard_map/dot_general | solution.py:256
  226.8 19.3 %all-to-all-done.7 = bf16[4,128,2560]{2,1,0:T(8,128)(2,1)S(1)} async-done(((bf16[4,128,2560]{2,1,0:T(8,128)(2,1)}), bf16[4,128,2560]{2,1,0:T(8,128)(2,1)S(1)}, u32[]{:S(2)}, u32[]{:S(2)}) %all-to-all-start.7) | async-done | bytes 2621472 | tf_op jit(solution)/shard_map/all_to_all | solution.py:259
  247.6 4.6 %all-to-all-start.6 = ((bf16[4,128,2560]{2,1,0:T(8,128)(2,1)}), bf16[4,128,2560]{2,1,0:T(8,128)(2,1)}, u32[]{:S(2)}, u32[]{:S(2)}) async-start(bf16[4,128,2560]{2,1,0:T(8,128)(2,1)} %bitcast.91), calls=%async_computation.6 | async-start | bytes 5242880 | tf_op jit(solution)/shard_map/all_to_all | solution.py:259
  256.7 2.3 convert_reduce_fusion.2
  260.5 22.2 %all-to-all-done.6 = bf16[4,128,2560]{2,1,0:T(8,128)(2,1)} async-done(((bf16[4,128,2560]{2,1,0:T(8,128)(2,1)}), bf16[4,128,2560]{2,1,0:T(8,128)(2,1)}, u32[]{:S(2)}, u32[]{:S(2)}) %all-to-all-start.6) | async-done | bytes 2621472 | tf_op jit(solution)/shard_map/all_to_all | solution.py:259
  289.9 21.5 %all_to_all.139 = bf16[128,8,320]{0,2,1:T(8,128)(2,1)} all-to-all(bf16[128,8,320]{0,2,1:T(8,128)(2,1)S(1)} %get-tuple-element.10), channel_id=1, replica_groups=mesh['dp'=8,'tensor'=4] {'dp'}, dimensions={1} | all-to-all | bytes 1310720 | tf_op jit(solution)/shard_map/all_to_all | solution.py:279
  311.4 3.5 all-to-all-start.9
  315.7 17.4 %all-to-all-done.9 = bf16[128,8,320]{0,2,1:T(8,128)(2,1)S(1)} async-done(((bf16[128,8,320]{0,2,1:T(8,128)(2,1)}), bf16[128,8,320]{0,2,1:T(8,128)(2,1)S(1)}, u32[]{:S(2)}, u32[]{:S(2)}) %all-to-all-start.9) | async-done | bytes 655392 | tf_op jit(solution)/shard_map/all_to_all | solution.py:279
  335.2 4.5 %all-to-all-start.10 = ((bf16[4,128,8,320]{1,3,2,0:T(8,128)(2,1)}), bf16[4,128,8,320]{1,3,2,0:T(8,128)(2,1)}, u32[]{:S(2)}, u32[]{:S(2)}) async-start(bf16[4,128,8,320]{1,3,2,0:T(8,128)(2,1)} %broadcast_in_dim.37), calls=%async_computation.10 | async-start | bytes 5242880 | tf_op jit(solution)/shard_map/all_to_all | solution.py:286
  342.6 41.8 %all-to-all-done.10 = bf16[4,128,8,320]{1,3,2,0:T(8,128)(2,1)} async-done(((bf16[4,128,8,320]{1,3,2,0:T(8,128)(2,1)}), bf16[4,128,8,320]{1,3,2,0:T(8,128)(2,1)}, u32[]{:S(2)}, u32[]{:S(2)}) %all-to-all-start.10) | async-done | bytes 2621472 | tf_op jit(solution)/shard_map/all_to_all | solution.py:286
  384.4 8.3 %convert_reduce_fusion = f32[1024,320]{0,1:T(8,128)} fusion(bf16[8,512,1024]{2,1,0:T(8,128)(2,1)} %bitcast.98, bf16[4,128,8,320]{1,3,2,0:T(8,128)(2,1)} %all-to-all-done.10), kind=kOutput, calls=%fused_computation | convolution fusion | flops 2694512640 | bytes 12320768 | tf_op jit(solution)/shard_map/csi,scd->cid/dot_general | solution.py:288
  392.7 7.3 %convert_reduce_fusion.1 = f32[1024,320]{0,1:T(8,128)S(1)} fusion(bf16[512,8,320]{0,2,1:T(8,128)(2,1)} %all-gather.7.cloned.1.call-done, bf16[8,512,1024]{2,1,0:T(8,128)(2,1)} %bitcast.99), kind=kOutput, calls=%fused_computation.2 | convolution fusion | flops 2694512640 | bytes 12320768 | tf_op jit(solution)/shard_map/csi,scd->cid/dot_general | solution.py:288
  (72 shorter events, 45.5 us)
Async XLA Ops:
  7.2 191.8 %all-gather.5.cloned.1.call-start = ((), (), s32[]{:S(2)}) async-start(), calls=%async_computation.11 | async-start | bytes 23592960 | tf_op jit(solution)/shard_map/all_gather | solution.py:250
  10.7 1.2 copy-start.10
  11.9 7.2 %copy-start.11 = (bf16[1,128,4096]{2,1,0:T(8,128)(2,1)S(1)}, bf16[1,128,4096]{2,1,0:T(8,128)(2,1)}, u32[]{:S(2)}) copy-start(bf16[1,128,4096]{2,1,0:T(8,128)(2,1)} %param.25) | copy-start | bytes 3145732
  14.0 18.8 %all-to-all-start.2 = ((bf16[128,4,1024]{2,0,1:T(8,128)(2,1)}), bf16[128,4,1024]{2,0,1:T(8,128)(2,1)S(1)}, u32[]{:S(2)}, u32[]{:S(2)}) async-start(bf16[128,4,1024]{2,0,1:T(8,128)(2,1)} %copy.42), calls=%async_computation.2 | async-start | bytes 2097152 | tf_op jit(solution)/shard_map/all_to_all | solution.py:222
  32.8 6.7 %copy-start.3 = (bf16[128,4,1024]{2,0,1:T(8,128)(2,1)}, bf16[128,4,1024]{2,0,1:T(8,128)(2,1)S(1)}, u32[]{:S(2)}) copy-start(bf16[128,4,1024]{2,0,1:T(8,128)(2,1)S(1)} %all-to-all-done.2) | copy-start | bytes 3145732
  32.8 16.7 %all-to-all-start.3 = ((bf16[128,4,1024]{2,0,1:T(8,128)(2,1)}), bf16[128,4,1024]{2,0,1:T(8,128)(2,1)S(1)}, u32[]{:S(2)}, u32[]{:S(2)}) async-start(bf16[128,4,1024]{2,0,1:T(8,128)(2,1)} %copy.43), calls=%async_computation.3 | async-start | bytes 2097152 | tf_op jit(solution)/shard_map/all_to_all | solution.py:222
  49.5 6.8 %copy-start.4 = (bf16[128,4,1024]{2,0,1:T(8,128)(2,1)}, bf16[128,4,1024]{2,0,1:T(8,128)(2,1)S(1)}, u32[]{:S(2)}) copy-start(bf16[128,4,1024]{2,0,1:T(8,128)(2,1)S(1)} %all-to-all-done.3) | copy-start | bytes 3145732
  49.5 16.7 %all-to-all-start.4 = ((bf16[128,4,1024]{2,0,1:T(8,128)(2,1)}), bf16[128,4,1024]{2,0,1:T(8,128)(2,1)S(1)}, u32[]{:S(2)}, u32[]{:S(2)}) async-start(bf16[128,4,1024]{2,0,1:T(8,128)(2,1)} %copy.44), calls=%async_computation.4 | async-start | bytes 2097152 | tf_op jit(solution)/shard_map/all_to_all | solution.py:222
  66.2 6.7 %copy-start.5 = (bf16[128,4,1024]{2,0,1:T(8,128)(2,1)}, bf16[128,4,1024]{2,0,1:T(8,128)(2,1)S(1)}, u32[]{:S(2)}) copy-start(bf16[128,4,1024]{2,0,1:T(8,128)(2,1)S(1)} %all-to-all-done.4) | copy-start | bytes 3145732
  66.2 16.7 %all-to-all-start.5 = ((bf16[128,4,1024]{2,0,1:T(8,128)(2,1)}), bf16[128,4,1024]{2,0,1:T(8,128)(2,1)S(1)}, u32[]{:S(2)}, u32[]{:S(2)}) async-start(bf16[128,4,1024]{2,0,1:T(8,128)(2,1)} %copy.45), calls=%async_computation.5 | async-start | bytes 2097152 | tf_op jit(solution)/shard_map/all_to_all | solution.py:222
  82.8 7.5 %copy-start.6 = (bf16[128,4,1024]{2,0,1:T(8,128)(2,1)}, bf16[128,4,1024]{2,0,1:T(8,128)(2,1)S(1)}, u32[]{:S(2)}) copy-start(bf16[128,4,1024]{2,0,1:T(8,128)(2,1)S(1)} %all-to-all-done.5) | copy-start | bytes 3145732
  82.8 16.7 %all-to-all-start = ((bf16[128,4,1024]{2,0,1:T(8,128)(2,1)}), bf16[128,4,1024]{2,0,1:T(8,128)(2,1)S(1)}, u32[]{:S(2)}, u32[]{:S(2)}) async-start(bf16[128,4,1024]{2,0,1:T(8,128)(2,1)} %copy.40), calls=%async_computation | async-start | bytes 2097152 | tf_op jit(solution)/shard_map/all_to_all | solution.py:222
  89.0 14.9 %copy-start.12 = (s32[1,3,512]{2,0,1:T(1,128)S(1)}, s32[1,3,512]{2,0,1:T(1,128)}, u32[]{:S(2)}) copy-start(s32[1,3,512]{2,0,1:T(1,128)} %param.17) | copy-start | bytes 18436
  99.5 16.7 %copy-start.7 = (bf16[128,4,1024]{2,0,1:T(8,128)(2,1)}, bf16[128,4,1024]{2,0,1:T(8,128)(2,1)S(1)}, u32[]{:S(2)}) copy-start(bf16[128,4,1024]{2,0,1:T(8,128)(2,1)S(1)} %all-to-all-done) | copy-start | bytes 3145732
  99.5 16.7 %all-to-all-start.1 = ((bf16[128,4,1024]{2,0,1:T(8,128)(2,1)}), bf16[128,4,1024]{2,0,1:T(8,128)(2,1)S(1)}, u32[]{:S(2)}, u32[]{:S(2)}) async-start(bf16[128,4,1024]{2,0,1:T(8,128)(2,1)} %copy.41), calls=%async_computation.1 | async-start | bytes 2097152 | tf_op jit(solution)/shard_map/all_to_all | solution.py:222
  103.0 239.5 %all-gather.9.cloned.1.call-start = ((), (), s32[]{:S(2)}) async-start(), calls=%async_computation.13 | async-start | bytes 9437184 | tf_op jit(solution)/shard_map/all_gather | solution.py:273
  116.2 1.0 copy-start.8
  149.6 54.5 %copy-start.13 = (bf16[512,1024]{1,0:T(8,128)(2,1)S(1)}, bf16[512,1024]{1,0:T(8,128)(2,1)}, u32[]{:S(2)}) copy-start(bf16[512,1024]{1,0:T(8,128)(2,1)} %get-tuple-element.4) | copy-start | bytes 3145732
  211.2 34.8 %all-to-all-start.7 = ((bf16[4,128,2560]{2,1,0:T(8,128)(2,1)}), bf16[4,128,2560]{2,1,0:T(8,128)(2,1)S(1)}, u32[]{:S(2)}, u32[]{:S(2)}) async-start(bf16[4,128,2560]{2,1,0:T(8,128)(2,1)} %bitcast.92), calls=%async_computation.7 | async-start | bytes 5242880 | tf_op jit(solution)/shard_map/all_to_all | solution.py:259
  214.9 5.2 %copy-start.14 = (bf16[512,1024]{1,0:T(8,128)(2,1)S(1)}, bf16[512,1024]{1,0:T(8,128)(2,1)}, u32[]{:S(2)}) copy-start(bf16[512,1024]{1,0:T(8,128)(2,1)} %get-tuple-element.4) | copy-start | bytes 3145732
  246.0 1.5 copy-start
  247.6 35.1 %all-to-all-start.6 = ((bf16[4,128,2560]{2,1,0:T(8,128)(2,1)}), bf16[4,128,2560]{2,1,0:T(8,128)(2,1)}, u32[]{:S(2)}, u32[]{:S(2)}) async-start(bf16[4,128,2560]{2,1,0:T(8,128)(2,1)} %bitcast.91), calls=%async_computation.6 | async-start | bytes 5242880 | tf_op jit(solution)/shard_map/all_to_all | solution.py:259
  286.4 2.1 copy-start.1
  286.4 2.5 copy-start.2
  311.4 21.6 %all-to-all-start.9 = ((bf16[128,8,320]{0,2,1:T(8,128)(2,1)}), bf16[128,8,320]{0,2,1:T(8,128)(2,1)S(1)}, u32[]{:S(2)}, u32[]{:S(2)}) async-start(bf16[128,8,320]{0,2,1:T(8,128)(2,1)} %get-tuple-element.11), calls=%async_computation.9 | async-start | bytes 1310720 | tf_op jit(solution)/shard_map/all_to_all | solution.py:279
  314.9 77.8 %all-gather.7.cloned.1.call-start = ((), (), s32[]{:S(2)}) async-start(), calls=%async_computation.12 | async-start | bytes 3276800 | tf_op jit(solution)/shard_map/all_gather | solution.py:283
  335.2 49.2 %all-to-all-start.10 = ((bf16[4,128,8,320]{1,3,2,0:T(8,128)(2,1)}), bf16[4,128,8,320]{1,3,2,0:T(8,128)(2,1)}, u32[]{:S(2)}, u32[]{:S(2)}) async-start(bf16[4,128,8,320]{1,3,2,0:T(8,128)(2,1)} %broadcast_in_dim.37), calls=%async_computation.10 | async-start | bytes 5242880 | tf_op jit(solution)/shard_map/all_to_all | solution.py:286
  392.7 7.3 %copy-start.9 = (f32[1024,320]{0,1:T(8,128)S(1)}, f32[1024,320]{0,1:T(8,128)}, u32[]{:S(2)}) copy-start(f32[1024,320]{0,1:T(8,128)} %convert_reduce_fusion) | copy-start | bytes 3932164
Sparse Core Ops, SparseCore 0:
  10.8 188.0 all-gather.4
  200.6 80.2 all-gather.8
  317.6 66.8 all-gather.6

commit v9 on v6

--- a/solution.py
+++ b/solution.py
@@ -246,25 +246,34 @@
         [Operand(a) for a in arrived],
         [jax.ShapeDtypeStruct((seq_whole, cols), jnp.bfloat16)] * 2,
     )
-    stacked = jnp.stack([student_out, teacher_out])
     clips = lax.axis_size("dp")
-    width = student_out.shape[1]
+    rows, width = student_out.shape
     half = width // 2
-    pieces = lax.all_gather(stacked, "dp", axis=2, tiled=False)
+    local = jnp.transpose(
+        jnp.stack([student_out, teacher_out]).reshape(2, rows, 2, half), (0, 2, 1, 3)
+    )
+    pieces = lax.all_gather(local, "dp", axis=3, tiled=False)
     latent_weight = cos_time * sin_time
     attended_all = lax.all_gather(attended, "dp", axis=0, tiled=False)
     grad_scale = -2.0 / math.sqrt(clips * seq_whole)
     latent_blocks = latent[0].reshape(seq_local, clips, width)
     targets = []
     grads = []
+    gate = None
     for part in range(2):
-        chosen = slice(part * half, (part + 1) * half)
-        weights = pieces[:, :, :, chosen].reshape(2, pieces.shape[1], clips * half)
-        partial_value = jnp.dot(student_term, weights[0], preferred_element_type=jnp.float32) + jnp.dot(
-            teacher_term, weights[1], preferred_element_type=jnp.float32
-        )
+        partial_value = (
+            jnp.einsum("si,ijd->sjd", student_term, pieces[0, part], preferred_element_type=jnp.float32)
+            + jnp.einsum("si,ijd->sjd", teacher_term, pieces[1, part], preferred_element_type=jnp.float32)
+        ).astype(jnp.bfloat16)
+        if gate is not None:
+            partial_value, columns = lax.optimization_barrier((partial_value, gate))
+            columns = lax.all_gather(columns, "tensor", axis=0, tiled=True)
+            terms = jnp.einsum(
+                "csi,scd->cid", attended_all, columns, preferred_element_type=jnp.float32
+            )
+            grads.append(jnp.sum((grad_scale * terms).astype(jnp.bfloat16).astype(jnp.float32), axis=0))
         pieces_in = lax.all_to_all(
-            partial_value.astype(jnp.bfloat16).reshape(groups, seq_local, clips, half),
+            partial_value.reshape(groups, seq_local, clips, half),
             "tensor",
             split_axis=0,
             concat_axis=0,
@@ -272,15 +281,15 @@
         )
         velocity = jnp.sum(pieces_in.astype(jnp.float32), axis=0)
         target_part = (
-            velocity - latent_weight * latent_blocks[:, :, chosen].astype(jnp.float32)
+            velocity - latent_weight * latent_blocks[:, :, part * half : (part + 1) * half].astype(jnp.float32)
         ).astype(jnp.bfloat16)
         targets.append(target_part)
-        columns = lax.all_to_all(target_part, "dp", split_axis=1, concat_axis=1, tiled=True)
-        columns = lax.all_gather(columns, "tensor", axis=0, tiled=True)
-        terms = jnp.einsum(
-            "csi,scd->cid", attended_all, columns, preferred_element_type=jnp.float32
-        )
-        grads.append(jnp.sum((grad_scale * terms).astype(jnp.bfloat16).astype(jnp.float32), axis=0))
+        gate = lax.all_to_all(target_part, "dp", split_axis=1, concat_axis=1, tiled=True)
+    columns = lax.all_gather(gate, "tensor", axis=0, tiled=True)
+    terms = jnp.einsum(
+        "csi,scd->cid", attended_all, columns, preferred_element_type=jnp.float32
+    )
+    grads.append(jnp.sum((grad_scale * terms).astype(jnp.bfloat16).astype(jnp.float32), axis=0))
     target = jnp.concatenate(targets, axis=2).reshape(seq_local, clips * width)
     gradient = jnp.concatenate(grads, axis=1)
     return (target[None], gradient)

time: 443 us -> 411 us (0.928)
  local copies, waits for them, and re-layouts: 80.6 us -> 33.9 us
  blocking collectives: 42.5 us -> 62.5 us
  waiting for transfers between devices: 196 us -> 189 us
  matrix products: 32.1 us -> 38.6 us
    all_gather x2 -> x1, waiting for transfers between devices: 47.6 us -> 0.01 us  [local(): columns = lax.all_gather(columns, 'tensor', axis=0, tiled=True)]
    all_to_all x0 -> x1, blocking collectives: none -> 41.2 us  [local(): lax.all_to_all(partial_value.reshape(groups, seq_local, clips, half), 'te...]
    all_gather x1 -> x0, local copies, waits for them, and re-layouts: 26.9 us -> none  [local(): pieces = lax.all_gather(stacked, 'dp', axis=2, tiled=False)]
    all_gather x1 -> x2, waiting for transfers between devices: 49.4 us -> 74.7 us  [the longest x1 49.4 us: local(): pieces = lax.all_gather(local, 'dp', axis=3, tiled=False)]
    all_to_all x2 -> x1, blocking collectives: 42.5 us -> 21.3 us  [local(): lax.all_to_all(target_part, 'dp', split_axis=1, concat_axis=1, tiled=True)]
    all_to_all x2, waiting for transfers between devices: 38.3 us -> 53.7 us  [the longest x1 28.7 us: local(): lax.all_to_all(partial_value.reshape(groups, seq_local, clips, half), 'te...]
    reshape x4 -> x2, local copies, waits for them, and re-layouts: 15.9 us -> 2.94 us  [local(): partial_value.reshape(groups, seq_local, clips, half)]
    slice x1 -> x0, local copies, waits for them, and re-layouts: 11.5 us -> none  [local(): weights[1]]
  transfers between devices with their start and end apart: 12 -> 12, of which waited for: 11 -> 10; matrix products, arithmetic and copies ran while one was open for 22% -> 13% of each run, Pallas kernels for 7% -> 8%
where the time goes in v9:
time: 411 us; the launch traced here: 410 us
  waiting for transfers between devices  189 us (46%)
  blocking collectives  62.5 us (15%)
  matrix products  38.6 us (9%)
  local copies, waits for them, and re-layouts  33.9 us (8%)
  Pallas kernels  31.2 us (8%)
  starting transfers between devices  30.5 us (7%)
  between operations  15.5 us (4%)
  other arithmetic  8.41 us (2%)
    all_to_all x6, waiting for transfers between devices, local(): lax.all_to_all(source[0], 'tensor', split_axis=1, concat_axis=0, tiled=True)  60.8 us
    all_gather x1, waiting for transfers between devices, local(): pieces = lax.all_gather(local, 'dp', axis=3, tiled=False)  49.4 us
    all_to_all x1, blocking collectives, local(): lax.all_to_all(partial_value.reshape(groups, seq_local, clips, half), 'te...  41.2 us
    pallas_call x2, Pallas kernels, head_call(): pl.pallas_call(kernel, grid=(heads,), in_specs=in_specs, out_specs=[head_...  31.2 us
    all_to_all x1, waiting for transfers between devices, local(): lax.all_to_all(partial_value.reshape(groups, seq_local, clips, half), 'te...  28.7 us
    all_gather x1, waiting for transfers between devices, local(): columns = lax.all_gather(gate, 'tensor', axis=0, tiled=True)  25.4 us
    all_to_all x1, waiting for transfers between devices, local(): lax.all_to_all(target_part, 'dp', split_axis=1, concat_axis=1, tiled=True)  24.9 us
    all_to_all x6, starting transfers between devices, local(): lax.all_to_all(source[0], 'tensor', split_axis=1, concat_axis=0, tiled=True)  22.8 us
  transfers between devices with their start and end apart: 12, of which 10 were waited for; matrix products, arithmetic and copies ran while one was open for 13% of the time, Pallas kernels for 8%

profile of v9, /device:TPU:0, one launch (start us, length us, event | category | flops | bytes accessed | tf_op | source)
XLA Modules:
  0.0 409.9 jit_solution(5310320574589486307)
XLA Ops:
  15.5 5.2 %all-to-all-start.2 = ((bf16[128,4,1024]{2,0,1:T(8,128)(2,1)}), bf16[128,4,1024]{2,0,1:T(8,128)(2,1)S(1)}, u32[]{:S(2)}, u32[]{:S(2)}) async-start(bf16[128,4,1024]{2,0,1:T(8,128)(2,1)} %copy.53), calls=%async_computation.2 | async-start | bytes 2097152 | tf_op jit(solution)/shard_map/all_to_all | solution.py:222
  22.7 11.5 %all-to-all-done.2 = bf16[128,4,1024]{2,0,1:T(8,128)(2,1)S(1)} async-done(((bf16[128,4,1024]{2,0,1:T(8,128)(2,1)}), bf16[128,4,1024]{2,0,1:T(8,128)(2,1)S(1)}, u32[]{:S(2)}, u32[]{:S(2)}) %all-to-all-start.2) | async-done | bytes 1048608 | tf_op jit(solution)/shard_map/all_to_all | solution.py:222
  34.3 3.5 all-to-all-start.3
  37.8 1.9 all_to_all.112
  40.9 10.0 %all-to-all-done.3 = bf16[128,4,1024]{2,0,1:T(8,128)(2,1)S(1)} async-done(((bf16[128,4,1024]{2,0,1:T(8,128)(2,1)}), bf16[128,4,1024]{2,0,1:T(8,128)(2,1)S(1)}, u32[]{:S(2)}, u32[]{:S(2)}) %all-to-all-start.3) | async-done | bytes 1048608 | tf_op jit(solution)/shard_map/all_to_all | solution.py:222
  51.0 3.5 all-to-all-start.4
  57.8 9.9 %all-to-all-done.4 = bf16[128,4,1024]{2,0,1:T(8,128)(2,1)S(1)} async-done(((bf16[128,4,1024]{2,0,1:T(8,128)(2,1)}), bf16[128,4,1024]{2,0,1:T(8,128)(2,1)S(1)}, u32[]{:S(2)}, u32[]{:S(2)}) %all-to-all-start.4) | async-done | bytes 1048608 | tf_op jit(solution)/shard_map/all_to_all | solution.py:222
  67.7 3.5 all-to-all-start.5
  74.3 10.0 %all-to-all-done.5 = bf16[128,4,1024]{2,0,1:T(8,128)(2,1)S(1)} async-done(((bf16[128,4,1024]{2,0,1:T(8,128)(2,1)}), bf16[128,4,1024]{2,0,1:T(8,128)(2,1)S(1)}, u32[]{:S(2)}, u32[]{:S(2)}) %all-to-all-start.5) | async-done | bytes 1048608 | tf_op jit(solution)/shard_map/all_to_all | solution.py:222
  84.4 3.5 all-to-all-start
  91.9 9.1 %all-to-all-done = bf16[128,4,1024]{2,0,1:T(8,128)(2,1)S(1)} async-done(((bf16[128,4,1024]{2,0,1:T(8,128)(2,1)}), bf16[128,4,1024]{2,0,1:T(8,128)(2,1)S(1)}, u32[]{:S(2)}, u32[]{:S(2)}) %all-to-all-start) | async-done | bytes 1048608 | tf_op jit(solution)/shard_map/all_to_all | solution.py:222
  101.0 3.5 all-to-all-start.1
  107.5 10.2 %all-to-all-done.1 = bf16[128,4,1024]{2,0,1:T(8,128)(2,1)S(1)} async-done(((bf16[128,4,1024]{2,0,1:T(8,128)(2,1)}), bf16[128,4,1024]{2,0,1:T(8,128)(2,1)S(1)}, u32[]{:S(2)}, u32[]{:S(2)}) %all-to-all-start.1) | async-done | bytes 1048608 | tf_op jit(solution)/shard_map/all_to_all | solution.py:222
  118.7 15.9 %shard_map.158 = (bf16[512,1024]{1,0:T(8,128)(2,1)}, bf16[512,1024]{1,0:T(8,128)(2,1)}) custom-call(f32[2]{0:T(128)} %pad_maximum_fusion.4.scal, f32[512,128]{1,0:T(8,128)} %get-tuple-element.24.cos_ref, f32[512,128]{1,0:T(8,128)} %get-tuple-element.25.sin_ref, bf16[512,1024]{1,0:T(8,128)(2,1)} %bitcast.90, bf16[512,1024]{1,0:T(8,128)(2,1)} %bitcast.91, ...), custom_call_target="tpu_custom_call" | custom-call | tf_op jit(solution)/shard_map/pallas_call | solution.py:178
  135.9 15.3 %shard_map.159 = bf16[512,1024]{1,0:T(8,128)(2,1)} custom-call(f32[2]{0:T(128)} %pad_maximum_fusion.5.scal, f32[512,128]{1,0:T(8,128)} %get-tuple-element.24.cos_ref, f32[512,128]{1,0:T(8,128)} %get-tuple-element.25.sin_ref, bf16[2,512,1024]{2,1,0:T(8,128)(2,1)} %bitcast.75, bf16[2,512,1024]{2,1,0:T(8,128)(2,1)} %bitcast.77, bf16[2,512,1024]{2,1,0:T(8,128)(2,1)} %bitcast.79, ...), custom_call_target="tpu_custom_call" | custom-call | tf_op jit(solution)/shard_map/pallas_call | solution.py:178
  151.2 49.4 %all-gather.11.cloned.1.call-done = bf16[2,2,1024,2560]{2,3,1,0:T(8,128)(2,1)} async-done(((bf16[2,2,1024,320]{2,3,1,0:T(8,128)(2,1)}), bf16[2,2,1024,2560]{2,3,1,0:T(8,128)(2,1)}) %all-gather.11.cloned.1.call-update) | async-done | bytes 20971536 | tf_op jit(solution)/shard_map/all_gather | solution.py:255
  200.5 5.3 %fusion.2 = f32[512,8,320]{0,2,1:T(8,128)S(1)} fusion(bf16[2,2,1024,8,320]{2,4,3,1,0:T(8,128)(2,1)} %bitcast.95, bf16[512,1024]{1,0:T(8,128)(2,1)} %shard_map.159), kind=kOutput, calls=%fused_computation.9 | convolution fusion | flops 2684354560 | bytes 11534336 | tf_op jit(solution)/shard_map/si,ijd->sjd/dot_general | solution.py:266
  205.8 6.2 %fusion.4 = bf16[8,40,4,8,128]{4,3,2,1,0:T(8,128)(2,1)S(1)} fusion(f32[512,8,320]{0,2,1:T(8,128)S(1)} %fusion.2, bf16[2,2,1024,8,320]{2,4,3,1,0:T(8,128)(2,1)} %bitcast.96, bf16[512,1024]{1,0:T(8,128)(2,1)S(1)} %copy-done.14), kind=kOutput, calls=%fused_computation.16 | convolution fusion | flops 2686976000 | bytes 14155776 | tf_op jit(solution)/shard_map/si,ijd->sjd/dot_general | solution.py:265
  212.1 2.2 copy.68
  214.3 3.7 all-to-all-start.6
  217.9 2.4 copy.60
  220.4 28.7 %all-to-all-done.6 = bf16[4,128,8,320]{1,3,2,0:T(8,128)(2,1)S(1)} async-done(((bf16[4,128,8,320]{1,3,2,0:T(8,128)(2,1)}), bf16[4,128,8,320]{1,3,2,0:T(8,128)(2,1)S(1)}, u32[]{:S(2)}, u32[]{:S(2)}) %all-to-all-start.6) | async-done | bytes 2621472 | tf_op jit(solution)/shard_map/all_to_all | solution.py:275
  251.4 3.6 all-to-all-start.7
  255.0 5.0 %fusion = f32[512,8,320]{0,2,1:T(8,128)S(1)} fusion(bf16[2,2,1024,8,320]{2,4,3,1,0:T(8,128)(2,1)} %bitcast.97, bf16[512,1024]{1,0:T(8,128)(2,1)S(1)} %copy-done.12), kind=kOutput, calls=%fused_computation.5 | convolution fusion | flops 2684354560 | bytes 11534336 | tf_op jit(solution)/shard_map/si,ijd->sjd/dot_general | solution.py:266
  260.1 5.8 %add_convert_fusion = bf16[512,8,320]{0,2,1:T(8,128)(2,1)S(1)} fusion(f32[512,8,320]{0,2,1:T(8,128)S(1)} %fusion, bf16[2,2,1024,8,320]{2,4,3,1,0:T(8,128)(2,1)} %bitcast.98, bf16[512,1024]{1,0:T(8,128)(2,1)S(1)} %copy-done.15), kind=kOutput, calls=%fused_computation.13 | convolution fusion | flops 2686976000 | bytes 14155776 | tf_op jit(solution)/shard_map/si,ijd->sjd/dot_general | solution.py:265
  265.9 24.9 %all-to-all-done.7 = bf16[128,8,320]{0,2,1:T(8,128)(2,1)S(1)} async-done(((bf16[128,8,320]{0,2,1:T(8,128)(2,1)}), bf16[128,8,320]{0,2,1:T(8,128)(2,1)S(1)}, u32[]{:S(2)}, u32[]{:S(2)}) %all-to-all-start.7) | async-done | bytes 655392 | tf_op jit(solution)/shard_map/all_to_all | solution.py:287
  292.7 41.2 %all_to_all.134 = bf16[4,128,8,320]{1,3,2,0:T(8,128)(2,1)S(1)} all-to-all(bf16[4,128,8,320]{1,3,2,0:T(8,128)(2,1)S(1)} %copy_bitcast_fusion), channel_id=1, replica_groups=mesh['dp'=8,'tensor'=4] {'tensor'}, dimensions={0} | all-to-all | bytes 5242880 | tf_op jit(solution)/shard_map/all_to_all | solution.py:275
  335.4 21.3 %all_to_all.135 = bf16[128,8,320]{0,2,1:T(8,128)(2,1)} all-to-all(bf16[128,8,320]{0,2,1:T(8,128)(2,1)S(1)} %subtract_convert_fusion), channel_id=1, replica_groups=mesh['dp'=8,'tensor'=4] {'dp'}, dimensions={1} | all-to-all | bytes 1310720 | tf_op jit(solution)/shard_map/all_to_all | solution.py:287
  359.4 8.9 %convert_reduce_fusion.1 = f32[1024,320]{0,1:T(8,128)} fusion(bf16[512,8,320]{0,2,1:T(8,128)(2,1)} %all-gather.7.cloned.1.call-done, bf16[8,512,1024]{2,1,0:T(8,128)(2,1)} %bitcast.99), kind=kOutput, calls=%fused_computation.2 | convolution fusion | flops 2694512640 | bytes 12320768 | tf_op jit(solution)/shard_map/csi,scd->cid/dot_general | solution.py:271
  368.3 25.4 %all-gather.9.cloned.1.call-done = bf16[512,8,320]{0,2,1:T(8,128)(2,1)} async-done(((bf16[128,8,320]{0,2,1:T(8,128)(2,1)}), bf16[512,8,320]{0,2,1:T(8,128)(2,1)}) %all-gather.9.cloned.1.call-update) | async-done | bytes 2621456 | tf_op jit(solution)/shard_map/all_gather | solution.py:288
  393.7 7.3 %convert_reduce_fusion = f32[1024,320]{0,1:T(8,128)S(1)} fusion(bf16[512,8,320]{0,2,1:T(8,128)(2,1)} %all-gather.9.cloned.1.call-done, bf16[8,512,1024]{2,1,0:T(8,128)(2,1)} %bitcast.100), kind=kOutput, calls=%fused_computation | convolution fusion | flops 2694512640 | bytes 12320768 | tf_op jit(solution)/shard_map/csi,scd->cid/dot_general | solution.py:289
  401.2 2.1 copy.63
  (72 shorter events, 34.4 us)
Async XLA Ops:
  7.2 193.4 %all-gather.11.cloned.1.call-start = ((), (), s32[]{:S(2)}) async-start(), calls=%async_computation.12 | async-start | bytes 23592960 | tf_op jit(solution)/shard_map/all_gather | solution.py:255
  12.2 1.2 copy-start.10
  14.2 6.5 %copy-start.11 = (bf16[1,128,4096]{2,1,0:T(8,128)(2,1)S(1)}, bf16[1,128,4096]{2,1,0:T(8,128)(2,1)}, u32[]{:S(2)}) copy-start(bf16[1,128,4096]{2,1,0:T(8,128)(2,1)} %param.25) | copy-start | bytes 3145732
  15.5 18.8 %all-to-all-start.2 = ((bf16[128,4,1024]{2,0,1:T(8,128)(2,1)}), bf16[128,4,1024]{2,0,1:T(8,128)(2,1)S(1)}, u32[]{:S(2)}, u32[]{:S(2)}) async-start(bf16[128,4,1024]{2,0,1:T(8,128)(2,1)} %copy.53), calls=%async_computation.2 | async-start | bytes 2097152 | tf_op jit(solution)/shard_map/all_to_all | solution.py:222
  34.3 6.7 %copy-start.2 = (bf16[128,4,1024]{2,0,1:T(8,128)(2,1)}, bf16[128,4,1024]{2,0,1:T(8,128)(2,1)S(1)}, u32[]{:S(2)}) copy-start(bf16[128,4,1024]{2,0,1:T(8,128)(2,1)S(1)} %all-to-all-done.2) | copy-start | bytes 3145732
  34.3 16.7 %all-to-all-start.3 = ((bf16[128,4,1024]{2,0,1:T(8,128)(2,1)}), bf16[128,4,1024]{2,0,1:T(8,128)(2,1)S(1)}, u32[]{:S(2)}, u32[]{:S(2)}) async-start(bf16[128,4,1024]{2,0,1:T(8,128)(2,1)} %copy.54), calls=%async_computation.3 | async-start | bytes 2097152 | tf_op jit(solution)/shard_map/all_to_all | solution.py:222
  51.0 6.8 %copy-start.3 = (bf16[128,4,1024]{2,0,1:T(8,128)(2,1)}, bf16[128,4,1024]{2,0,1:T(8,128)(2,1)S(1)}, u32[]{:S(2)}) copy-start(bf16[128,4,1024]{2,0,1:T(8,128)(2,1)S(1)} %all-to-all-done.3) | copy-start | bytes 3145732
  51.0 16.7 %all-to-all-start.4 = ((bf16[128,4,1024]{2,0,1:T(8,128)(2,1)}), bf16[128,4,1024]{2,0,1:T(8,128)(2,1)S(1)}, u32[]{:S(2)}, u32[]{:S(2)}) async-start(bf16[128,4,1024]{2,0,1:T(8,128)(2,1)} %copy.55), calls=%async_computation.4 | async-start | bytes 2097152 | tf_op jit(solution)/shard_map/all_to_all | solution.py:222
  67.7 6.7 %copy-start.4 = (bf16[128,4,1024]{2,0,1:T(8,128)(2,1)}, bf16[128,4,1024]{2,0,1:T(8,128)(2,1)S(1)}, u32[]{:S(2)}) copy-start(bf16[128,4,1024]{2,0,1:T(8,128)(2,1)S(1)} %all-to-all-done.4) | copy-start | bytes 3145732
  67.7 16.7 %all-to-all-start.5 = ((bf16[128,4,1024]{2,0,1:T(8,128)(2,1)}), bf16[128,4,1024]{2,0,1:T(8,128)(2,1)S(1)}, u32[]{:S(2)}, u32[]{:S(2)}) async-start(bf16[128,4,1024]{2,0,1:T(8,128)(2,1)} %copy.56), calls=%async_computation.5 | async-start | bytes 2097152 | tf_op jit(solution)/shard_map/all_to_all | solution.py:222
  84.4 7.5 %copy-start.5 = (bf16[128,4,1024]{2,0,1:T(8,128)(2,1)}, bf16[128,4,1024]{2,0,1:T(8,128)(2,1)S(1)}, u32[]{:S(2)}) copy-start(bf16[128,4,1024]{2,0,1:T(8,128)(2,1)S(1)} %all-to-all-done.5) | copy-start | bytes 3145732
  84.4 16.7 %all-to-all-start = ((bf16[128,4,1024]{2,0,1:T(8,128)(2,1)}), bf16[128,4,1024]{2,0,1:T(8,128)(2,1)S(1)}, u32[]{:S(2)}, u32[]{:S(2)}) async-start(bf16[128,4,1024]{2,0,1:T(8,128)(2,1)} %copy.51), calls=%async_computation | async-start | bytes 2097152 | tf_op jit(solution)/shard_map/all_to_all | solution.py:222
  90.6 14.9 %copy-start.13 = (s32[1,3,512]{2,0,1:T(1,128)S(1)}, s32[1,3,512]{2,0,1:T(1,128)}, u32[]{:S(2)}) copy-start(s32[1,3,512]{2,0,1:T(1,128)} %param.17) | copy-start | bytes 18436
  101.0 16.7 %copy-start.6 = (bf16[128,4,1024]{2,0,1:T(8,128)(2,1)}, bf16[128,4,1024]{2,0,1:T(8,128)(2,1)S(1)}, u32[]{:S(2)}) copy-start(bf16[128,4,1024]{2,0,1:T(8,128)(2,1)S(1)} %all-to-all-done) | copy-start | bytes 3145732
  101.0 16.7 %all-to-all-start.1 = ((bf16[128,4,1024]{2,0,1:T(8,128)(2,1)}), bf16[128,4,1024]{2,0,1:T(8,128)(2,1)S(1)}, u32[]{:S(2)}, u32[]{:S(2)}) async-start(bf16[128,4,1024]{2,0,1:T(8,128)(2,1)} %copy.52), calls=%async_computation.1 | async-start | bytes 2097152 | tf_op jit(solution)/shard_map/all_to_all | solution.py:222
  104.6 254.8 %all-gather.13.cloned.1.call-start = ((), (), s32[]{:S(2)}) async-start(), calls=%async_computation.13 | async-start | bytes 9437184 | tf_op jit(solution)/shard_map/all_gather | solution.py:257
  117.7 1.0 copy-start.7
  200.5 5.3 %copy-start.14 = (bf16[512,1024]{1,0:T(8,128)(2,1)S(1)}, bf16[512,1024]{1,0:T(8,128)(2,1)}, u32[]{:S(2)}) copy-start(bf16[512,1024]{1,0:T(8,128)(2,1)} %get-tuple-element.6) | copy-start | bytes 3145732
  214.3 34.8 %all-to-all-start.6 = ((bf16[4,128,8,320]{1,3,2,0:T(8,128)(2,1)}), bf16[4,128,8,320]{1,3,2,0:T(8,128)(2,1)S(1)}, u32[]{:S(2)}, u32[]{:S(2)}) async-start(bf16[4,128,8,320]{1,3,2,0:T(8,128)(2,1)} %bitcast.74), calls=%async_computation.6 | async-start | bytes 5242880 | tf_op jit(solution)/shard_map/all_to_all | solution.py:275
  249.1 1.3 copy-start
  249.5 5.5 %copy-start.12 = (bf16[512,1024]{1,0:T(8,128)(2,1)S(1)}, bf16[512,1024]{1,0:T(8,128)(2,1)}, u32[]{:S(2)}) copy-start(bf16[512,1024]{1,0:T(8,128)(2,1)} %shard_map.159) | copy-start | bytes 3145732
  251.4 39.4 %all-to-all-start.7 = ((bf16[128,8,320]{0,2,1:T(8,128)(2,1)}), bf16[128,8,320]{0,2,1:T(8,128)(2,1)S(1)}, u32[]{:S(2)}, u32[]{:S(2)}) async-start(bf16[128,8,320]{0,2,1:T(8,128)(2,1)} %subtract_convert_fusion.1), calls=%async_computation.7 | async-start | bytes 1310720 | tf_op jit(solution)/shard_map/all_to_all | solution.py:287
  255.0 104.4 %all-gather.7.cloned.1.call-start = ((), (), s32[]{:S(2)}) async-start(), calls=%async_computation.10 | async-start | bytes 3276800 | tf_op jit(solution)/shard_map/all_gather | solution.py:270
  255.0 5.0 %copy-start.15 = (bf16[512,1024]{1,0:T(8,128)(2,1)S(1)}, bf16[512,1024]{1,0:T(8,128)(2,1)}, u32[]{:S(2)}) copy-start(bf16[512,1024]{1,0:T(8,128)(2,1)} %get-tuple-element.6) | copy-start | bytes 3145732
  290.8 0.8 copy-start.8
  291.7 102.0 %all-gather.9.cloned.1.call-start = ((), (), s32[]{:S(2)}) async-start(), calls=%async_computation.11 | async-start | bytes 3276800 | tf_op jit(solution)/shard_map/all_gather | solution.py:288
  333.9 1.4 copy-start.1
  393.7 7.3 %copy-start.9 = (f32[1024,320]{0,1:T(8,128)S(1)}, f32[1024,320]{0,1:T(8,128)}, u32[]{:S(2)}) copy-start(f32[1024,320]{0,1:T(8,128)} %convert_reduce_fusion.1) | copy-start | bytes 3932164
Sparse Core Ops, SparseCore 0:
  12.3 188.1 all-gather.10
  202.1 94.1 all-gather.12
  298.2 52.7 all-gather.6
  356.9 36.8 all-gather.8

commit v10 on v7

--- a/solution.py
+++ b/solution.py
@@ -249,10 +249,10 @@
     stacked = jnp.stack([student_out, teacher_out])
     pieces = lax.all_gather(stacked, "dp", axis=2, tiled=True)
     latent_weight = cos_time * sin_time
-    span = pieces.shape[2] // 2
+    bounds = (0, pieces.shape[2] // 4, pieces.shape[2])
     target_parts = []
     for part in range(2):
-        chosen = slice(part * span, (part + 1) * span)
+        chosen = slice(bounds[part], bounds[part + 1])
         partial_value = jnp.dot(
             student_term, pieces[0, :, chosen], preferred_element_type=jnp.float32
         ) + jnp.dot(teacher_term, pieces[1, :, chosen], preferred_element_type=jnp.float32)

time: 407 us -> 400 us (0.983)
  local copies, waits for them, and re-layouts: 29.1 us -> 22 us
  other arithmetic: 18.3 us -> 11.8 us
  waiting for transfers between devices: 198 us -> 204 us
  transfers between devices with their start and end apart: 12 -> 12, of which waited for: 11 -> 11; matrix products, arithmetic and copies ran while one was open for 15% -> 12% of each run, Pallas kernels for 8% -> 8%
where the time goes in v10:
time: 400 us; the launch traced here: 398 us
  waiting for transfers between devices  204 us (51%)
  blocking collectives  42.5 us (11%)
  matrix products  39.2 us (10%)
  starting transfers between devices  31.9 us (8%)
  Pallas kernels  31.2 us (8%)
  local copies, waits for them, and re-layouts  22 us (6%)
  between operations  15.5 us (4%)
  other arithmetic  11.8 us (3%)
    all_to_all x6, waiting for transfers between devices, local(): lax.all_to_all(source[0], 'tensor', split_axis=1, concat_axis=0, tiled=True)  60.7 us
    all_gather x1, waiting for transfers between devices, local(): pieces = lax.all_gather(stacked, 'dp', axis=2, tiled=True)  49.3 us
    all_gather x2, waiting for transfers between devices, local(): columns = lax.all_gather(columns, 'tensor', axis=0, tiled=True)  49.1 us
    all_to_all x2, waiting for transfers between devices, local(): lax.all_to_all(partial_value.astype(jnp.bfloat16).reshape(groups, seq_loc...  45.1 us
    all_to_all x2, blocking collectives, local(): lax.all_to_all(split_target[:, :, part * half:(part + 1) * half], 'dp', s...  42.5 us
    pallas_call x2, Pallas kernels, head_call(): pl.pallas_call(kernel, grid=(heads,), in_specs=in_specs, out_specs=[head_...  31.2 us
    all_to_all x6, starting transfers between devices, local(): lax.all_to_all(source[0], 'tensor', split_axis=1, concat_axis=0, tiled=True)  22.7 us
    all_to_all x12, local copies, waits for them, and re-layouts, local(): lax.all_to_all(source[0], 'tensor', split_axis=1, concat_axis=0, tiled=True)  16.9 us
  transfers between devices with their start and end apart: 12, of which 11 were waited for; matrix products, arithmetic and copies ran while one was open for 12% of the time, Pallas kernels for 8%

profile of v10, /device:TPU:0, one launch (start us, length us, event | category | flops | bytes accessed | tf_op | source)
XLA Modules:
  0.0 398.5 jit_solution(12624602926697827444)
XLA Ops:
  7.2 3.5 pad_maximum_fusion
  14.0 5.2 %all-to-all-start.2 = ((bf16[128,4,1024]{2,0,1:T(8,128)(2,1)}), bf16[128,4,1024]{2,0,1:T(8,128)(2,1)S(1)}, u32[]{:S(2)}, u32[]{:S(2)}) async-start(bf16[128,4,1024]{2,0,1:T(8,128)(2,1)} %copy.35), calls=%async_computation.2 | async-start | bytes 2097152 | tf_op jit(solution)/shard_map/all_to_all | solution.py:222
  21.2 11.5 %all-to-all-done.2 = bf16[128,4,1024]{2,0,1:T(8,128)(2,1)S(1)} async-done(((bf16[128,4,1024]{2,0,1:T(8,128)(2,1)}), bf16[128,4,1024]{2,0,1:T(8,128)(2,1)S(1)}, u32[]{:S(2)}, u32[]{:S(2)}) %all-to-all-start.2) | async-done | bytes 1048608 | tf_op jit(solution)/shard_map/all_to_all | solution.py:222
  32.8 3.5 all-to-all-start.3
  36.3 1.9 all_to_all.112
  39.5 10.0 %all-to-all-done.3 = bf16[128,4,1024]{2,0,1:T(8,128)(2,1)S(1)} async-done(((bf16[128,4,1024]{2,0,1:T(8,128)(2,1)}), bf16[128,4,1024]{2,0,1:T(8,128)(2,1)S(1)}, u32[]{:S(2)}, u32[]{:S(2)}) %all-to-all-start.3) | async-done | bytes 1048608 | tf_op jit(solution)/shard_map/all_to_all | solution.py:222
  49.5 3.5 all-to-all-start.4
  56.3 9.9 %all-to-all-done.4 = bf16[128,4,1024]{2,0,1:T(8,128)(2,1)S(1)} async-done(((bf16[128,4,1024]{2,0,1:T(8,128)(2,1)}), bf16[128,4,1024]{2,0,1:T(8,128)(2,1)S(1)}, u32[]{:S(2)}, u32[]{:S(2)}) %all-to-all-start.4) | async-done | bytes 1048608 | tf_op jit(solution)/shard_map/all_to_all | solution.py:222
  66.2 3.5 all-to-all-start.5
  72.8 10.0 %all-to-all-done.5 = bf16[128,4,1024]{2,0,1:T(8,128)(2,1)S(1)} async-done(((bf16[128,4,1024]{2,0,1:T(8,128)(2,1)}), bf16[128,4,1024]{2,0,1:T(8,128)(2,1)S(1)}, u32[]{:S(2)}, u32[]{:S(2)}) %all-to-all-start.5) | async-done | bytes 1048608 | tf_op jit(solution)/shard_map/all_to_all | solution.py:222
  82.8 3.5 all-to-all-start
  90.4 9.1 %all-to-all-done = bf16[128,4,1024]{2,0,1:T(8,128)(2,1)S(1)} async-done(((bf16[128,4,1024]{2,0,1:T(8,128)(2,1)}), bf16[128,4,1024]{2,0,1:T(8,128)(2,1)S(1)}, u32[]{:S(2)}, u32[]{:S(2)}) %all-to-all-start) | async-done | bytes 1048608 | tf_op jit(solution)/shard_map/all_to_all | solution.py:222
  99.5 3.5 all-to-all-start.1
  106.0 10.2 %all-to-all-done.1 = bf16[128,4,1024]{2,0,1:T(8,128)(2,1)S(1)} async-done(((bf16[128,4,1024]{2,0,1:T(8,128)(2,1)}), bf16[128,4,1024]{2,0,1:T(8,128)(2,1)S(1)}, u32[]{:S(2)}, u32[]{:S(2)}) %all-to-all-start.1) | async-done | bytes 1048608 | tf_op jit(solution)/shard_map/all_to_all | solution.py:222
  117.2 15.9 %shard_map.158 = (bf16[512,1024]{1,0:T(8,128)(2,1)}, bf16[512,1024]{1,0:T(8,128)(2,1)}) custom-call(f32[2]{0:T(128)} %pad_maximum_fusion.5.scal, f32[512,128]{1,0:T(8,128)} %get-tuple-element.20.cos_ref, f32[512,128]{1,0:T(8,128)} %get-tuple-element.21.sin_ref, bf16[512,1024]{1,0:T(8,128)(2,1)} %bitcast.75, bf16[512,1024]{1,0:T(8,128)(2,1)} %bitcast.76, ...), custom_call_target="tpu_custom_call" | custom-call | tf_op jit(solution)/shard_map/pallas_call | solution.py:178
  134.3 15.3 %shard_map.159 = bf16[512,1024]{1,0:T(8,128)(2,1)} custom-call(f32[2]{0:T(128)} %pad_maximum_fusion.6.scal, f32[512,128]{1,0:T(8,128)} %get-tuple-element.20.cos_ref, f32[512,128]{1,0:T(8,128)} %get-tuple-element.21.sin_ref, bf16[2,512,1024]{2,1,0:T(8,128)(2,1)} %bitcast.64, bf16[2,512,1024]{2,1,0:T(8,128)(2,1)} %bitcast.66, bf16[2,512,1024]{2,1,0:T(8,128)(2,1)} %bitcast.68, ...), custom_call_target="tpu_custom_call" | custom-call | tf_op jit(solution)/shard_map/pallas_call | solution.py:178
  149.6 49.3 %all-gather.6.cloned.1.call-done = bf16[2,1024,5120]{2,1,0:T(8,128)(2,1)} async-done(((bf16[2,1024,640]{2,1,0:T(8,128)(2,1)}), bf16[2,1024,5120]{2,1,0:T(8,128)(2,1)}) %all-gather.6.cloned.1.call-update) | async-done | bytes 20971536 | tf_op jit(solution)/shard_map/all_gather | solution.py:250
  199.0 3.3 fusion.3
  202.3 4.3 %fusion.2 = bf16[512,1280]{1,0:T(8,128)(2,1)} fusion(f32[512,1280]{1,0:T(8,128)S(1)} %fusion.3, bf16[512,1024]{1,0:T(8,128)(2,1)S(1)} %copy-done.10, bf16[2,1024,5120]{2,1,0:T(8,128)(2,1)} %all-gather.6.cloned.1.call-done), kind=kOutput, calls=%fused_computation.11 | convolution fusion | flops 1343488000 | bytes 7602176 | tf_op jit(solution)/shard_map/dot_general | solution.py:258
  206.7 3.7 all-to-all-start.6
  210.3 6.6 %fusion = f32[512,3840]{1,0:T(8,128)S(1)} fusion(bf16[512,1024]{1,0:T(8,128)(2,1)S(1)} %copy-done.10, bf16[2,1024,5120]{2,1,0:T(8,128)(2,1)} %all-gather.6.cloned.1.call-done), kind=kOutput, calls=%fused_computation.5 | convolution fusion | flops 4026531840 | bytes 16777216 | tf_op jit(solution)/shard_map/dot_general | solution.py:258
  216.9 9.2 %add_convert_fusion = bf16[512,3840]{1,0:T(8,128)(2,1)} fusion(f32[512,3840]{1,0:T(8,128)S(1)} %fusion, bf16[512,1024]{1,0:T(8,128)(2,1)S(1)} %copy-done.12, bf16[2,1024,5120]{2,1,0:T(8,128)(2,1)} %all-gather.6.cloned.1.call-done), kind=kOutput, calls=%fused_computation.9 | convolution fusion | flops 4030464000 | bytes 20709376 | tf_op jit(solution)/shard_map/dot_general | solution.py:256
  227.4 4.9 %all-to-all-start.7 = ((bf16[4,128,3840]{2,1,0:T(8,128)(2,1)}), bf16[4,128,3840]{2,1,0:T(8,128)(2,1)}, u32[]{:S(2)}, u32[]{:S(2)}) async-start(bf16[4,128,3840]{2,1,0:T(8,128)(2,1)} %bitcast.77), calls=%async_computation.7 | async-start | bytes 7864320 | tf_op jit(solution)/shard_map/all_to_all | solution.py:259
  232.9 43.9 %all-to-all-done.7 = bf16[4,128,3840]{2,1,0:T(8,128)(2,1)} async-done(((bf16[4,128,3840]{2,1,0:T(8,128)(2,1)}), bf16[4,128,3840]{2,1,0:T(8,128)(2,1)}, u32[]{:S(2)}, u32[]{:S(2)}) %all-to-all-start.7) | async-done | bytes 3932192 | tf_op jit(solution)/shard_map/all_to_all | solution.py:259
  276.8 2.9 convert_reduce_fusion.2
  282.2 21.3 %all_to_all.134 = bf16[128,8,320]{0,2,1:T(8,128)(2,1)} all-to-all(bf16[128,8,320]{0,2,1:T(8,128)(2,1)S(1)} %get-tuple-element.10), channel_id=1, replica_groups=mesh['dp'=8,'tensor'=4] {'dp'}, dimensions={1} | all-to-all | bytes 1310720 | tf_op jit(solution)/shard_map/all_to_all | solution.py:279
  303.5 21.3 %all_to_all.135 = bf16[128,8,320]{0,2,1:T(8,128)(2,1)} all-to-all(bf16[128,8,320]{0,2,1:T(8,128)(2,1)S(1)} %get-tuple-element.11), channel_id=1, replica_groups=mesh['dp'=8,'tensor'=4] {'dp'}, dimensions={1} | all-to-all | bytes 1310720 | tf_op jit(solution)/shard_map/all_to_all | solution.py:279
  324.9 16.2 %all-gather.8.cloned.1.call-done = bf16[512,8,320]{0,2,1:T(8,128)(2,1)} async-done(((bf16[128,8,320]{0,2,1:T(8,128)(2,1)}), bf16[512,8,320]{0,2,1:T(8,128)(2,1)}) %all-gather.8.cloned.1.call-update) | async-done | bytes 2621456 | tf_op jit(solution)/shard_map/all_gather | solution.py:282
  341.1 8.3 %convert_reduce_fusion.1 = f32[1024,320]{0,1:T(8,128)} fusion(bf16[512,8,320]{0,2,1:T(8,128)(2,1)} %all-gather.8.cloned.1.call-done, bf16[8,512,1024]{2,1,0:T(8,128)(2,1)} %bitcast.83), kind=kOutput, calls=%fused_computation.2 | convolution fusion | flops 2694512640 | bytes 12320768 | tf_op jit(solution)/shard_map/csi,scd->cid/dot_general | solution.py:283
  349.4 32.9 %all-gather.10.cloned.1.call-done = bf16[512,8,320]{0,2,1:T(8,128)(2,1)} async-done(((bf16[128,8,320]{0,2,1:T(8,128)(2,1)}), bf16[512,8,320]{0,2,1:T(8,128)(2,1)}) %all-gather.10.cloned.1.call-update) | async-done | bytes 2621456 | tf_op jit(solution)/shard_map/all_gather | solution.py:282
  382.3 7.3 %convert_reduce_fusion = f32[1024,320]{0,1:T(8,128)S(1)} fusion(bf16[512,8,320]{0,2,1:T(8,128)(2,1)} %all-gather.10.cloned.1.call-done, bf16[8,512,1024]{2,1,0:T(8,128)(2,1)} %bitcast.84), kind=kOutput, calls=%fused_computation | convolution fusion | flops 2694512640 | bytes 12320768 | tf_op jit(solution)/shard_map/csi,scd->cid/dot_general | solution.py:283
  389.8 2.1 copy.40
  (62 shorter events, 25.4 us)
Async XLA Ops:
  7.2 191.8 %all-gather.6.cloned.1.call-start = ((), (), s32[]{:S(2)}) async-start(), calls=%async_computation.10 | async-start | bytes 23592960 | tf_op jit(solution)/shard_map/all_gather | solution.py:250
  10.7 1.2 copy-start.8
  11.9 7.2 %copy-start.9 = (bf16[1,128,4096]{2,1,0:T(8,128)(2,1)S(1)}, bf16[1,128,4096]{2,1,0:T(8,128)(2,1)}, u32[]{:S(2)}) copy-start(bf16[1,128,4096]{2,1,0:T(8,128)(2,1)} %param.25) | copy-start | bytes 3145732
  14.0 18.8 %all-to-all-start.2 = ((bf16[128,4,1024]{2,0,1:T(8,128)(2,1)}), bf16[128,4,1024]{2,0,1:T(8,128)(2,1)S(1)}, u32[]{:S(2)}, u32[]{:S(2)}) async-start(bf16[128,4,1024]{2,0,1:T(8,128)(2,1)} %copy.35), calls=%async_computation.2 | async-start | bytes 2097152 | tf_op jit(solution)/shard_map/all_to_all | solution.py:222
  32.8 6.7 %copy-start = (bf16[128,4,1024]{2,0,1:T(8,128)(2,1)}, bf16[128,4,1024]{2,0,1:T(8,128)(2,1)S(1)}, u32[]{:S(2)}) copy-start(bf16[128,4,1024]{2,0,1:T(8,128)(2,1)S(1)} %all-to-all-done.2) | copy-start | bytes 3145732
  32.8 16.7 %all-to-all-start.3 = ((bf16[128,4,1024]{2,0,1:T(8,128)(2,1)}), bf16[128,4,1024]{2,0,1:T(8,128)(2,1)S(1)}, u32[]{:S(2)}, u32[]{:S(2)}) async-start(bf16[128,4,1024]{2,0,1:T(8,128)(2,1)} %copy.36), calls=%async_computation.3 | async-start | bytes 2097152 | tf_op jit(solution)/shard_map/all_to_all | solution.py:222
  49.5 6.8 %copy-start.1 = (bf16[128,4,1024]{2,0,1:T(8,128)(2,1)}, bf16[128,4,1024]{2,0,1:T(8,128)(2,1)S(1)}, u32[]{:S(2)}) copy-start(bf16[128,4,1024]{2,0,1:T(8,128)(2,1)S(1)} %all-to-all-done.3) | copy-start | bytes 3145732
  49.5 16.7 %all-to-all-start.4 = ((bf16[128,4,1024]{2,0,1:T(8,128)(2,1)}), bf16[128,4,1024]{2,0,1:T(8,128)(2,1)S(1)}, u32[]{:S(2)}, u32[]{:S(2)}) async-start(bf16[128,4,1024]{2,0,1:T(8,128)(2,1)} %copy.37), calls=%async_computation.4 | async-start | bytes 2097152 | tf_op jit(solution)/shard_map/all_to_all | solution.py:222
  66.2 6.7 %copy-start.2 = (bf16[128,4,1024]{2,0,1:T(8,128)(2,1)}, bf16[128,4,1024]{2,0,1:T(8,128)(2,1)S(1)}, u32[]{:S(2)}) copy-start(bf16[128,4,1024]{2,0,1:T(8,128)(2,1)S(1)} %all-to-all-done.4) | copy-start | bytes 3145732
  66.2 16.7 %all-to-all-start.5 = ((bf16[128,4,1024]{2,0,1:T(8,128)(2,1)}), bf16[128,4,1024]{2,0,1:T(8,128)(2,1)S(1)}, u32[]{:S(2)}, u32[]{:S(2)}) async-start(bf16[128,4,1024]{2,0,1:T(8,128)(2,1)} %copy.38), calls=%async_computation.5 | async-start | bytes 2097152 | tf_op jit(solution)/shard_map/all_to_all | solution.py:222
  82.8 7.6 %copy-start.3 = (bf16[128,4,1024]{2,0,1:T(8,128)(2,1)}, bf16[128,4,1024]{2,0,1:T(8,128)(2,1)S(1)}, u32[]{:S(2)}) copy-start(bf16[128,4,1024]{2,0,1:T(8,128)(2,1)S(1)} %all-to-all-done.5) | copy-start | bytes 3145732
  82.8 16.7 %all-to-all-start = ((bf16[128,4,1024]{2,0,1:T(8,128)(2,1)}), bf16[128,4,1024]{2,0,1:T(8,128)(2,1)S(1)}, u32[]{:S(2)}, u32[]{:S(2)}) async-start(bf16[128,4,1024]{2,0,1:T(8,128)(2,1)} %copy.33), calls=%async_computation | async-start | bytes 2097152 | tf_op jit(solution)/shard_map/all_to_all | solution.py:222
  89.0 14.9 %copy-start.11 = (s32[1,3,512]{2,0,1:T(1,128)S(1)}, s32[1,3,512]{2,0,1:T(1,128)}, u32[]{:S(2)}) copy-start(s32[1,3,512]{2,0,1:T(1,128)} %param.17) | copy-start | bytes 18436
  99.5 16.7 %copy-start.4 = (bf16[128,4,1024]{2,0,1:T(8,128)(2,1)}, bf16[128,4,1024]{2,0,1:T(8,128)(2,1)S(1)}, u32[]{:S(2)}) copy-start(bf16[128,4,1024]{2,0,1:T(8,128)(2,1)S(1)} %all-to-all-done) | copy-start | bytes 3145732
  99.5 16.7 %all-to-all-start.1 = ((bf16[128,4,1024]{2,0,1:T(8,128)(2,1)}), bf16[128,4,1024]{2,0,1:T(8,128)(2,1)S(1)}, u32[]{:S(2)}, u32[]{:S(2)}) async-start(bf16[128,4,1024]{2,0,1:T(8,128)(2,1)} %copy.34), calls=%async_computation.1 | async-start | bytes 2097152 | tf_op jit(solution)/shard_map/all_to_all | solution.py:222
  103.0 221.8 %all-gather.12.cloned.1.call-start = ((), (), s32[]{:S(2)}) async-start(), calls=%async_computation.13 | async-start | bytes 9437184 | tf_op jit(solution)/shard_map/all_gather | solution.py:273
  116.2 1.0 copy-start.5
  134.3 64.6 %copy-start.12 = (bf16[512,1024]{1,0:T(8,128)(2,1)S(1)}, bf16[512,1024]{1,0:T(8,128)(2,1)}, u32[]{:S(2)}) copy-start(bf16[512,1024]{1,0:T(8,128)(2,1)} %get-tuple-element.4) | copy-start | bytes 3145732
  199.0 3.4 copy-start.10
  206.7 20.7 %all-to-all-start.6 = ((bf16[4,128,1280]{2,1,0:T(8,128)(2,1)}), bf16[4,128,1280]{2,1,0:T(8,128)(2,1)S(1)}, u32[]{:S(2)}, u32[]{:S(2)}) async-start(bf16[4,128,1280]{2,1,0:T(8,128)(2,1)} %bitcast.24), calls=%async_computation.6 | async-start | bytes 2621440 | tf_op jit(solution)/shard_map/all_to_all | solution.py:259
  227.3 5.4 %copy-start.7 = (bf16[1,128,5120]{2,1,0:T(8,128)(2,1)S(1)}, bf16[1,128,5120]{2,1,0:T(8,128)(2,1)}, u32[]{:S(2)}) copy-start(bf16[1,128,5120]{2,1,0:T(8,128)(2,1)} %param.18) | copy-start | bytes 3932164
  227.4 49.4 %all-to-all-start.7 = ((bf16[4,128,3840]{2,1,0:T(8,128)(2,1)}), bf16[4,128,3840]{2,1,0:T(8,128)(2,1)}, u32[]{:S(2)}, u32[]{:S(2)}) async-start(bf16[4,128,3840]{2,1,0:T(8,128)(2,1)} %bitcast.77), calls=%async_computation.7 | async-start | bytes 7864320 | tf_op jit(solution)/shard_map/all_to_all | solution.py:259
  232.3 108.8 %all-gather.8.cloned.1.call-start = ((), (), s32[]{:S(2)}) async-start(), calls=%async_computation.11 | async-start | bytes 3276800 | tf_op jit(solution)/shard_map/all_gather | solution.py:282
  303.5 78.8 %all-gather.10.cloned.1.call-start = ((), (), s32[]{:S(2)}) async-start(), calls=%async_computation.12 | async-start | bytes 3276800 | tf_op jit(solution)/shard_map/all_gather | solution.py:282
  382.3 7.3 %copy-start.6 = (f32[1024,320]{0,1:T(8,128)S(1)}, f32[1024,320]{0,1:T(8,128)}, u32[]{:S(2)}) copy-start(f32[1024,320]{0,1:T(8,128)} %convert_reduce_fusion.1) | copy-start | bytes 3932164
Sparse Core Ops, SparseCore 0:
  10.8 188.0 all-gather.5
  200.6 80.2 all-gather.11
  303.6 37.4 all-gather.7
  342.8 39.4 all-gather.9

commit v11 on v10

--- a/solution.py
+++ b/solution.py
@@ -272,12 +272,12 @@
     width = target.shape[1] // clips
     attended_all = lax.all_gather(attended, "dp", axis=0, tiled=False)
     grad_scale = -2.0 / math.sqrt(clips * seq_whole)
-    half = width // 2
+    edges = (0, width * 2 // 5, width)
     split_target = target.reshape(seq_local, clips, width)
     pieces = []
     for part in range(2):
         columns = lax.all_to_all(
-            split_target[:, :, part * half : (part + 1) * half], "dp", split_axis=1, concat_axis=1, tiled=True
+            split_target[:, :, edges[part] : edges[part + 1]], "dp", split_axis=1, concat_axis=1, tiled=True
         )
         columns = lax.all_gather(columns, "tensor", axis=0, tiled=True)
         terms = jnp.einsum(

time: 400 us -> 398 us (level)
  no operation moved by 1% of the time
where the time goes in v11:
time: 398 us; the launch traced here: 397 us
  waiting for transfers between devices  203 us (51%)
  blocking collectives  42.5 us (11%)
  matrix products  39.3 us (10%)
  starting transfers between devices  31.9 us (8%)
  Pallas kernels  31.2 us (8%)
  local copies, waits for them, and re-layouts  20.5 us (5%)
  between operations  15.5 us (4%)
  other arithmetic  13.3 us (3%)
    all_to_all x6, waiting for transfers between devices, local(): lax.all_to_all(source[0], 'tensor', split_axis=1, concat_axis=0, tiled=True)  60.8 us
    all_gather x1, waiting for transfers between devices, local(): pieces = lax.all_gather(stacked, 'dp', axis=2, tiled=True)  49.3 us
    all_gather x2, waiting for transfers between devices, local(): columns = lax.all_gather(columns, 'tensor', axis=0, tiled=True)  47.6 us
    all_to_all x2, waiting for transfers between devices, local(): lax.all_to_all(partial_value.astype(jnp.bfloat16).reshape(groups, seq_loc...  45.1 us
    all_to_all x2, blocking collectives, local(): lax.all_to_all(split_target[:, :, edges[part]:edges[part + 1]], 'dp', spl...  42.5 us
    pallas_call x2, Pallas kernels, head_call(): pl.pallas_call(kernel, grid=(heads,), in_specs=in_specs, out_specs=[head_...  31.2 us
    all_to_all x6, starting transfers between devices, local(): lax.all_to_all(source[0], 'tensor', split_axis=1, concat_axis=0, tiled=True)  22.7 us
    all_to_all x12, local copies, waits for them, and re-layouts, local(): lax.all_to_all(source[0], 'tensor', split_axis=1, concat_axis=0, tiled=True)  16.9 us
  transfers between devices with their start and end apart: 12, of which 11 were waited for; matrix products, arithmetic and copies ran while one was open for 12% of the time, Pallas kernels for 8%

profile of v11, /device:TPU:0, one launch (start us, length us, event | category | flops | bytes accessed | tf_op | source)
XLA Modules:
  0.0 397.1 jit_solution(4793724174043922151)
XLA Ops:
  7.2 3.5 pad_maximum_fusion
  14.0 5.2 %all-to-all-start.2 = ((bf16[128,4,1024]{2,0,1:T(8,128)(2,1)}), bf16[128,4,1024]{2,0,1:T(8,128)(2,1)S(1)}, u32[]{:S(2)}, u32[]{:S(2)}) async-start(bf16[128,4,1024]{2,0,1:T(8,128)(2,1)} %copy.52), calls=%async_computation.2 | async-start | bytes 2097152 | tf_op jit(solution)/shard_map/all_to_all | solution.py:222
  21.3 11.5 %all-to-all-done.2 = bf16[128,4,1024]{2,0,1:T(8,128)(2,1)S(1)} async-done(((bf16[128,4,1024]{2,0,1:T(8,128)(2,1)}), bf16[128,4,1024]{2,0,1:T(8,128)(2,1)S(1)}, u32[]{:S(2)}, u32[]{:S(2)}) %all-to-all-start.2) | async-done | bytes 1048608 | tf_op jit(solution)/shard_map/all_to_all | solution.py:222
  32.8 3.5 all-to-all-start.3
  36.3 1.9 all_to_all.112
  39.5 10.0 %all-to-all-done.3 = bf16[128,4,1024]{2,0,1:T(8,128)(2,1)S(1)} async-done(((bf16[128,4,1024]{2,0,1:T(8,128)(2,1)}), bf16[128,4,1024]{2,0,1:T(8,128)(2,1)S(1)}, u32[]{:S(2)}, u32[]{:S(2)}) %all-to-all-start.3) | async-done | bytes 1048608 | tf_op jit(solution)/shard_map/all_to_all | solution.py:222
  49.5 3.5 all-to-all-start.4
  53.0 1.9 all_to_all.116
  56.3 9.9 %all-to-all-done.4 = bf16[128,4,1024]{2,0,1:T(8,128)(2,1)S(1)} async-done(((bf16[128,4,1024]{2,0,1:T(8,128)(2,1)}), bf16[128,4,1024]{2,0,1:T(8,128)(2,1)S(1)}, u32[]{:S(2)}, u32[]{:S(2)}) %all-to-all-start.4) | async-done | bytes 1048608 | tf_op jit(solution)/shard_map/all_to_all | solution.py:222
  66.2 3.5 all-to-all-start.5
  72.8 10.0 %all-to-all-done.5 = bf16[128,4,1024]{2,0,1:T(8,128)(2,1)S(1)} async-done(((bf16[128,4,1024]{2,0,1:T(8,128)(2,1)}), bf16[128,4,1024]{2,0,1:T(8,128)(2,1)S(1)}, u32[]{:S(2)}, u32[]{:S(2)}) %all-to-all-start.5) | async-done | bytes 1048608 | tf_op jit(solution)/shard_map/all_to_all | solution.py:222
  82.8 3.5 all-to-all-start
  90.4 9.1 %all-to-all-done = bf16[128,4,1024]{2,0,1:T(8,128)(2,1)S(1)} async-done(((bf16[128,4,1024]{2,0,1:T(8,128)(2,1)}), bf16[128,4,1024]{2,0,1:T(8,128)(2,1)S(1)}, u32[]{:S(2)}, u32[]{:S(2)}) %all-to-all-start) | async-done | bytes 1048608 | tf_op jit(solution)/shard_map/all_to_all | solution.py:222
  99.5 3.5 all-to-all-start.1
  106.0 10.2 %all-to-all-done.1 = bf16[128,4,1024]{2,0,1:T(8,128)(2,1)S(1)} async-done(((bf16[128,4,1024]{2,0,1:T(8,128)(2,1)}), bf16[128,4,1024]{2,0,1:T(8,128)(2,1)S(1)}, u32[]{:S(2)}, u32[]{:S(2)}) %all-to-all-start.1) | async-done | bytes 1048608 | tf_op jit(solution)/shard_map/all_to_all | solution.py:222
  117.2 15.9 %shard_map.158 = (bf16[512,1024]{1,0:T(8,128)(2,1)}, bf16[512,1024]{1,0:T(8,128)(2,1)}) custom-call(f32[2]{0:T(128)} %pad_maximum_fusion.5.scal, f32[512,128]{1,0:T(8,128)} %get-tuple-element.16.cos_ref, f32[512,128]{1,0:T(8,128)} %get-tuple-element.17.sin_ref, bf16[512,1024]{1,0:T(8,128)(2,1)} %bitcast.76, bf16[512,1024]{1,0:T(8,128)(2,1)} %bitcast.77, ...), custom_call_target="tpu_custom_call" | custom-call | tf_op jit(solution)/shard_map/pallas_call | solution.py:178
  134.4 15.3 %shard_map.159 = bf16[512,1024]{1,0:T(8,128)(2,1)} custom-call(f32[2]{0:T(128)} %pad_maximum_fusion.6.scal, f32[512,128]{1,0:T(8,128)} %get-tuple-element.16.cos_ref, f32[512,128]{1,0:T(8,128)} %get-tuple-element.17.sin_ref, bf16[2,512,1024]{2,1,0:T(8,128)(2,1)} %bitcast.64, bf16[2,512,1024]{2,1,0:T(8,128)(2,1)} %bitcast.66, bf16[2,512,1024]{2,1,0:T(8,128)(2,1)} %bitcast.68, ...), custom_call_target="tpu_custom_call" | custom-call | tf_op jit(solution)/shard_map/pallas_call | solution.py:178
  149.7 49.3 %all-gather.6.cloned.1.call-done = bf16[2,1024,5120]{2,1,0:T(8,128)(2,1)} async-done(((bf16[2,1024,640]{2,1,0:T(8,128)(2,1)}), bf16[2,1024,5120]{2,1,0:T(8,128)(2,1)}) %all-gather.6.cloned.1.call-update) | async-done | bytes 20971536 | tf_op jit(solution)/shard_map/all_gather | solution.py:250
  199.0 3.3 fusion.3
  202.3 4.3 %fusion.2 = bf16[512,1280]{1,0:T(8,128)(2,1)} fusion(f32[512,1280]{1,0:T(8,128)S(1)} %fusion.3, bf16[512,1024]{1,0:T(8,128)(2,1)S(1)} %copy-done.9, bf16[2,1024,5120]{2,1,0:T(8,128)(2,1)} %all-gather.6.cloned.1.call-done), kind=kOutput, calls=%fused_computation.11 | convolution fusion | flops 1343488000 | bytes 7602176 | tf_op jit(solution)/shard_map/dot_general | solution.py:258
  206.7 3.7 all-to-all-start.6
  210.3 6.6 %fusion = f32[512,3840]{1,0:T(8,128)S(1)} fusion(bf16[512,1024]{1,0:T(8,128)(2,1)S(1)} %copy-done.9, bf16[2,1024,5120]{2,1,0:T(8,128)(2,1)} %all-gather.6.cloned.1.call-done), kind=kOutput, calls=%fused_computation.5 | convolution fusion | flops 4026531840 | bytes 16777216 | tf_op jit(solution)/shard_map/dot_general | solution.py:258
  216.9 9.2 %add_convert_fusion = bf16[512,3840]{1,0:T(8,128)(2,1)} fusion(f32[512,3840]{1,0:T(8,128)S(1)} %fusion, bf16[512,1024]{1,0:T(8,128)(2,1)S(1)} %copy-done.11, bf16[2,1024,5120]{2,1,0:T(8,128)(2,1)} %all-gather.6.cloned.1.call-done), kind=kOutput, calls=%fused_computation.9 | convolution fusion | flops 4030464000 | bytes 20709376 | tf_op jit(solution)/shard_map/dot_general | solution.py:256
  227.4 4.9 %all-to-all-start.7 = ((bf16[4,128,3840]{2,1,0:T(8,128)(2,1)}), bf16[4,128,3840]{2,1,0:T(8,128)(2,1)}, u32[]{:S(2)}, u32[]{:S(2)}) async-start(bf16[4,128,3840]{2,1,0:T(8,128)(2,1)} %bitcast.78), calls=%async_computation.7 | async-start | bytes 7864320 | tf_op jit(solution)/shard_map/all_to_all | solution.py:259
  232.9 43.9 %all-to-all-done.7 = bf16[4,128,3840]{2,1,0:T(8,128)(2,1)} async-done(((bf16[4,128,3840]{2,1,0:T(8,128)(2,1)}), bf16[4,128,3840]{2,1,0:T(8,128)(2,1)}, u32[]{:S(2)}, u32[]{:S(2)}) %all-to-all-start.7) | async-done | bytes 3932192 | tf_op jit(solution)/shard_map/all_to_all | solution.py:259
  276.7 2.9 convert_reduce_fusion.2
  282.4 18.4 %all_to_all.134 = bf16[128,8,256]{2,0,1:T(8,128)(2,1)} all-to-all(bf16[128,8,256]{2,0,1:T(8,128)(2,1)S(1)} %copy.63), channel_id=1, replica_groups=mesh['dp'=8,'tensor'=4] {'dp'}, dimensions={1} | all-to-all | bytes 1048576 | tf_op jit(solution)/shard_map/all_to_all | solution.py:279
  301.3 24.1 %all_to_all.135 = bf16[128,8,384]{2,0,1:T(8,128)(2,1)} all-to-all(bf16[128,8,384]{2,0,1:T(8,128)(2,1)S(1)} %copy.64), channel_id=1, replica_groups=mesh['dp'=8,'tensor'=4] {'dp'}, dimensions={1} | all-to-all | bytes 1572864 | tf_op jit(solution)/shard_map/all_to_all | solution.py:279
  325.4 8.8 %all-gather.8.cloned.1.call-done = bf16[512,8,256]{2,0,1:T(8,128)(2,1)} async-done(((bf16[128,8,256]{2,0,1:T(8,128)(2,1)}), bf16[512,8,256]{2,0,1:T(8,128)(2,1)}) %all-gather.8.cloned.1.call-update) | async-done | bytes 2097168 | tf_op jit(solution)/shard_map/all_gather | solution.py:282
  334.2 6.9 %convert_reduce_fusion.1 = f32[1024,256]{1,0:T(8,128)S(1)} fusion(bf16[8,512,1024]{2,1,0:T(8,128)(2,1)} %bitcast.84, bf16[512,8,256]{2,0,1:T(8,128)(2,1)} %all-gather.8.cloned.1.call-done), kind=kOutput, calls=%fused_computation.2 | convolution fusion | flops 2155610112 | bytes 11534336 | tf_op jit(solution)/shard_map/csi,scd->cid/dot_general | solution.py:283
  341.1 38.8 %all-gather.10.cloned.1.call-done = bf16[512,8,384]{2,0,1:T(8,128)(2,1)} async-done(((bf16[128,8,384]{2,0,1:T(8,128)(2,1)}), bf16[512,8,384]{2,0,1:T(8,128)(2,1)}) %all-gather.10.cloned.1.call-update) | async-done | bytes 3145744 | tf_op jit(solution)/shard_map/all_gather | solution.py:282
  379.9 8.9 %convert_reduce_fusion = f32[1024,384]{1,0:T(8,128)S(1)} fusion(bf16[8,512,1024]{2,1,0:T(8,128)(2,1)} %bitcast.85, bf16[512,8,384]{2,0,1:T(8,128)(2,1)} %all-gather.10.cloned.1.call-done), kind=kOutput, calls=%fused_computation | convolution fusion | flops 3233415168 | bytes 13107200 | tf_op jit(solution)/shard_map/csi,scd->cid/dot_general | solution.py:283
  (62 shorter events, 25.6 us)
Async XLA Ops:
  7.2 191.8 %all-gather.6.cloned.1.call-start = ((), (), s32[]{:S(2)}) async-start(), calls=%async_computation.10 | async-start | bytes 23592960 | tf_op jit(solution)/shard_map/all_gather | solution.py:250
  10.7 1.2 copy-start.7
  11.9 7.2 %copy-start.8 = (bf16[1,128,4096]{2,1,0:T(8,128)(2,1)S(1)}, bf16[1,128,4096]{2,1,0:T(8,128)(2,1)}, u32[]{:S(2)}) copy-start(bf16[1,128,4096]{2,1,0:T(8,128)(2,1)} %param.25) | copy-start | bytes 3145732
  14.0 18.8 %all-to-all-start.2 = ((bf16[128,4,1024]{2,0,1:T(8,128)(2,1)}), bf16[128,4,1024]{2,0,1:T(8,128)(2,1)S(1)}, u32[]{:S(2)}, u32[]{:S(2)}) async-start(bf16[128,4,1024]{2,0,1:T(8,128)(2,1)} %copy.52), calls=%async_computation.2 | async-start | bytes 2097152 | tf_op jit(solution)/shard_map/all_to_all | solution.py:222
  32.8 6.7 %copy-start = (bf16[128,4,1024]{2,0,1:T(8,128)(2,1)}, bf16[128,4,1024]{2,0,1:T(8,128)(2,1)S(1)}, u32[]{:S(2)}) copy-start(bf16[128,4,1024]{2,0,1:T(8,128)(2,1)S(1)} %all-to-all-done.2) | copy-start | bytes 3145732
  32.8 16.7 %all-to-all-start.3 = ((bf16[128,4,1024]{2,0,1:T(8,128)(2,1)}), bf16[128,4,1024]{2,0,1:T(8,128)(2,1)S(1)}, u32[]{:S(2)}, u32[]{:S(2)}) async-start(bf16[128,4,1024]{2,0,1:T(8,128)(2,1)} %copy.53), calls=%async_computation.3 | async-start | bytes 2097152 | tf_op jit(solution)/shard_map/all_to_all | solution.py:222
  49.5 6.8 %copy-start.1 = (bf16[128,4,1024]{2,0,1:T(8,128)(2,1)}, bf16[128,4,1024]{2,0,1:T(8,128)(2,1)S(1)}, u32[]{:S(2)}) copy-start(bf16[128,4,1024]{2,0,1:T(8,128)(2,1)S(1)} %all-to-all-done.3) | copy-start | bytes 3145732
  49.5 16.7 %all-to-all-start.4 = ((bf16[128,4,1024]{2,0,1:T(8,128)(2,1)}), bf16[128,4,1024]{2,0,1:T(8,128)(2,1)S(1)}, u32[]{:S(2)}, u32[]{:S(2)}) async-start(bf16[128,4,1024]{2,0,1:T(8,128)(2,1)} %copy.54), calls=%async_computation.4 | async-start | bytes 2097152 | tf_op jit(solution)/shard_map/all_to_all | solution.py:222
  66.2 6.7 %copy-start.2 = (bf16[128,4,1024]{2,0,1:T(8,128)(2,1)}, bf16[128,4,1024]{2,0,1:T(8,128)(2,1)S(1)}, u32[]{:S(2)}) copy-start(bf16[128,4,1024]{2,0,1:T(8,128)(2,1)S(1)} %all-to-all-done.4) | copy-start | bytes 3145732
  66.2 16.7 %all-to-all-start.5 = ((bf16[128,4,1024]{2,0,1:T(8,128)(2,1)}), bf16[128,4,1024]{2,0,1:T(8,128)(2,1)S(1)}, u32[]{:S(2)}, u32[]{:S(2)}) async-start(bf16[128,4,1024]{2,0,1:T(8,128)(2,1)} %copy.55), calls=%async_computation.5 | async-start | bytes 2097152 | tf_op jit(solution)/shard_map/all_to_all | solution.py:222
  82.8 7.6 %copy-start.3 = (bf16[128,4,1024]{2,0,1:T(8,128)(2,1)}, bf16[128,4,1024]{2,0,1:T(8,128)(2,1)S(1)}, u32[]{:S(2)}) copy-start(bf16[128,4,1024]{2,0,1:T(8,128)(2,1)S(1)} %all-to-all-done.5) | copy-start | bytes 3145732
  82.8 16.7 %all-to-all-start = ((bf16[128,4,1024]{2,0,1:T(8,128)(2,1)}), bf16[128,4,1024]{2,0,1:T(8,128)(2,1)S(1)}, u32[]{:S(2)}, u32[]{:S(2)}) async-start(bf16[128,4,1024]{2,0,1:T(8,128)(2,1)} %copy.50), calls=%async_computation | async-start | bytes 2097152 | tf_op jit(solution)/shard_map/all_to_all | solution.py:222
  89.0 14.9 %copy-start.10 = (s32[1,3,512]{2,0,1:T(1,128)S(1)}, s32[1,3,512]{2,0,1:T(1,128)}, u32[]{:S(2)}) copy-start(s32[1,3,512]{2,0,1:T(1,128)} %param.17) | copy-start | bytes 18436
  99.5 16.7 %copy-start.4 = (bf16[128,4,1024]{2,0,1:T(8,128)(2,1)}, bf16[128,4,1024]{2,0,1:T(8,128)(2,1)S(1)}, u32[]{:S(2)}) copy-start(bf16[128,4,1024]{2,0,1:T(8,128)(2,1)S(1)} %all-to-all-done) | copy-start | bytes 3145732
  99.5 16.7 %all-to-all-start.1 = ((bf16[128,4,1024]{2,0,1:T(8,128)(2,1)}), bf16[128,4,1024]{2,0,1:T(8,128)(2,1)S(1)}, u32[]{:S(2)}, u32[]{:S(2)}) async-start(bf16[128,4,1024]{2,0,1:T(8,128)(2,1)} %copy.51), calls=%async_computation.1 | async-start | bytes 2097152 | tf_op jit(solution)/shard_map/all_to_all | solution.py:222
  103.0 222.4 %all-gather.12.cloned.1.call-start = ((), (), s32[]{:S(2)}) async-start(), calls=%async_computation.13 | async-start | bytes 9437184 | tf_op jit(solution)/shard_map/all_gather | solution.py:273
  116.2 1.0 copy-start.5
  134.4 64.6 %copy-start.11 = (bf16[512,1024]{1,0:T(8,128)(2,1)S(1)}, bf16[512,1024]{1,0:T(8,128)(2,1)}, u32[]{:S(2)}) copy-start(bf16[512,1024]{1,0:T(8,128)(2,1)} %get-tuple-element.4) | copy-start | bytes 3145732
  199.0 3.4 copy-start.9
  206.7 20.7 %all-to-all-start.6 = ((bf16[4,128,1280]{2,1,0:T(8,128)(2,1)}), bf16[4,128,1280]{2,1,0:T(8,128)(2,1)S(1)}, u32[]{:S(2)}, u32[]{:S(2)}) async-start(bf16[4,128,1280]{2,1,0:T(8,128)(2,1)} %bitcast.24), calls=%async_computation.6 | async-start | bytes 2621440 | tf_op jit(solution)/shard_map/all_to_all | solution.py:259
  227.3 5.4 %copy-start.6 = (bf16[1,128,5120]{2,1,0:T(8,128)(2,1)S(1)}, bf16[1,128,5120]{2,1,0:T(8,128)(2,1)}, u32[]{:S(2)}) copy-start(bf16[1,128,5120]{2,1,0:T(8,128)(2,1)} %param.18) | copy-start | bytes 3932164
  227.4 49.4 %all-to-all-start.7 = ((bf16[4,128,3840]{2,1,0:T(8,128)(2,1)}), bf16[4,128,3840]{2,1,0:T(8,128)(2,1)}, u32[]{:S(2)}, u32[]{:S(2)}) async-start(bf16[4,128,3840]{2,1,0:T(8,128)(2,1)} %bitcast.78), calls=%async_computation.7 | async-start | bytes 7864320 | tf_op jit(solution)/shard_map/all_to_all | solution.py:259
  232.3 101.9 %all-gather.8.cloned.1.call-start = ((), (), s32[]{:S(2)}) async-start(), calls=%async_computation.11 | async-start | bytes 2621440 | tf_op jit(solution)/shard_map/all_gather | solution.py:282
  300.8 79.1 %all-gather.10.cloned.1.call-start = ((), (), s32[]{:S(2)}) async-start(), calls=%async_computation.12 | async-start | bytes 3932160 | tf_op jit(solution)/shard_map/all_gather | solution.py:282
Sparse Core Ops, SparseCore 0:
  10.8 188.0 all-gather.5
  200.6 80.2 all-gather.11
  301.0 33.2 all-gather.7
  335.9 43.9 all-gather.9

commit v12 on v11

--- a/solution.py
+++ b/solution.py
@@ -263,6 +263,8 @@
             concat_axis=0,
             tiled=True,
         )
+        if target_parts:
+            target_parts[0], pieces_in = lax.optimization_barrier((target_parts[0], pieces_in))
         velocity = jnp.sum(pieces_in.astype(jnp.float32), axis=0)
         target_parts.append(
             (velocity - latent_weight * latent[0, :, chosen].astype(jnp.float32)).astype(jnp.bfloat16)

time: 398 us -> 398 us (level)
  no operation moved by 1% of the time
where the time goes in v12:
time: 398 us; the launch traced here: 397 us
  waiting for transfers between devices  203 us (51%)
  blocking collectives  42.5 us (11%)
  matrix products  39.3 us (10%)
  starting transfers between devices  31.9 us (8%)
  Pallas kernels  31.2 us (8%)
  local copies, waits for them, and re-layouts  20.5 us (5%)
  between operations  15.5 us (4%)
  other arithmetic  13.3 us (3%)
    all_to_all x6, waiting for transfers between devices, local(): lax.all_to_all(source[0], 'tensor', split_axis=1, concat_axis=0, tiled=True)  60.8 us
    all_gather x1, waiting for transfers between devices, local(): pieces = lax.all_gather(stacked, 'dp', axis=2, tiled=True)  49.3 us
    all_gather x2, waiting for transfers between devices, local(): columns = lax.all_gather(columns, 'tensor', axis=0, tiled=True)  47.6 us
    all_to_all x2, waiting for transfers between devices, local(): lax.all_to_all(partial_value.astype(jnp.bfloat16).reshape(groups, seq_loc...  45.1 us
    all_to_all x2, blocking collectives, local(): lax.all_to_all(split_target[:, :, edges[part]:edges[part + 1]], 'dp', spl...  42.5 us
    pallas_call x2, Pallas kernels, head_call(): pl.pallas_call(kernel, grid=(heads,), in_specs=in_specs, out_specs=[head_...  31.2 us
    all_to_all x6, starting transfers between devices, local(): lax.all_to_all(source[0], 'tensor', split_axis=1, concat_axis=0, tiled=True)  22.7 us
    all_to_all x12, local copies, waits for them, and re-layouts, local(): lax.all_to_all(source[0], 'tensor', split_axis=1, concat_axis=0, tiled=True)  16.9 us
  transfers between devices with their start and end apart: 12, of which 11 were waited for; matrix products, arithmetic and copies ran while one was open for 12% of the time, Pallas kernels for 8%

profile of v12, /device:TPU:0, one launch (start us, length us, event | category | flops | bytes accessed | tf_op | source)
XLA Modules:
  0.0 397.1 jit_solution(4793724174043922151)
XLA Ops:
  7.2 3.5 pad_maximum_fusion
  14.0 5.2 %all-to-all-start.2 = ((bf16[128,4,1024]{2,0,1:T(8,128)(2,1)}), bf16[128,4,1024]{2,0,1:T(8,128)(2,1)S(1)}, u32[]{:S(2)}, u32[]{:S(2)}) async-start(bf16[128,4,1024]{2,0,1:T(8,128)(2,1)} %copy.52), calls=%async_computation.2 | async-start | bytes 2097152 | tf_op jit(solution)/shard_map/all_to_all | solution.py:222
  21.3 11.5 %all-to-all-done.2 = bf16[128,4,1024]{2,0,1:T(8,128)(2,1)S(1)} async-done(((bf16[128,4,1024]{2,0,1:T(8,128)(2,1)}), bf16[128,4,1024]{2,0,1:T(8,128)(2,1)S(1)}, u32[]{:S(2)}, u32[]{:S(2)}) %all-to-all-start.2) | async-done | bytes 1048608 | tf_op jit(solution)/shard_map/all_to_all | solution.py:222
  32.8 3.5 all-to-all-start.3
  36.3 1.9 all_to_all.112
  39.5 10.0 %all-to-all-done.3 = bf16[128,4,1024]{2,0,1:T(8,128)(2,1)S(1)} async-done(((bf16[128,4,1024]{2,0,1:T(8,128)(2,1)}), bf16[128,4,1024]{2,0,1:T(8,128)(2,1)S(1)}, u32[]{:S(2)}, u32[]{:S(2)}) %all-to-all-start.3) | async-done | bytes 1048608 | tf_op jit(solution)/shard_map/all_to_all | solution.py:222
  49.5 3.5 all-to-all-start.4
  53.0 1.9 all_to_all.116
  56.3 9.9 %all-to-all-done.4 = bf16[128,4,1024]{2,0,1:T(8,128)(2,1)S(1)} async-done(((bf16[128,4,1024]{2,0,1:T(8,128)(2,1)}), bf16[128,4,1024]{2,0,1:T(8,128)(2,1)S(1)}, u32[]{:S(2)}, u32[]{:S(2)}) %all-to-all-start.4) | async-done | bytes 1048608 | tf_op jit(solution)/shard_map/all_to_all | solution.py:222
  66.2 3.5 all-to-all-start.5
  72.8 10.0 %all-to-all-done.5 = bf16[128,4,1024]{2,0,1:T(8,128)(2,1)S(1)} async-done(((bf16[128,4,1024]{2,0,1:T(8,128)(2,1)}), bf16[128,4,1024]{2,0,1:T(8,128)(2,1)S(1)}, u32[]{:S(2)}, u32[]{:S(2)}) %all-to-all-start.5) | async-done | bytes 1048608 | tf_op jit(solution)/shard_map/all_to_all | solution.py:222
  82.8 3.5 all-to-all-start
  90.4 9.1 %all-to-all-done = bf16[128,4,1024]{2,0,1:T(8,128)(2,1)S(1)} async-done(((bf16[128,4,1024]{2,0,1:T(8,128)(2,1)}), bf16[128,4,1024]{2,0,1:T(8,128)(2,1)S(1)}, u32[]{:S(2)}, u32[]{:S(2)}) %all-to-all-start) | async-done | bytes 1048608 | tf_op jit(solution)/shard_map/all_to_all | solution.py:222
  99.5 3.5 all-to-all-start.1
  106.0 10.2 %all-to-all-done.1 = bf16[128,4,1024]{2,0,1:T(8,128)(2,1)S(1)} async-done(((bf16[128,4,1024]{2,0,1:T(8,128)(2,1)}), bf16[128,4,1024]{2,0,1:T(8,128)(2,1)S(1)}, u32[]{:S(2)}, u32[]{:S(2)}) %all-to-all-start.1) | async-done | bytes 1048608 | tf_op jit(solution)/shard_map/all_to_all | solution.py:222
  117.2 15.9 %shard_map.158 = (bf16[512,1024]{1,0:T(8,128)(2,1)}, bf16[512,1024]{1,0:T(8,128)(2,1)}) custom-call(f32[2]{0:T(128)} %pad_maximum_fusion.5.scal, f32[512,128]{1,0:T(8,128)} %get-tuple-element.20.cos_ref, f32[512,128]{1,0:T(8,128)} %get-tuple-element.21.sin_ref, bf16[512,1024]{1,0:T(8,128)(2,1)} %bitcast.76, bf16[512,1024]{1,0:T(8,128)(2,1)} %bitcast.77, ...), custom_call_target="tpu_custom_call" | custom-call | tf_op jit(solution)/shard_map/pallas_call | solution.py:178
  134.4 15.3 %shard_map.159 = bf16[512,1024]{1,0:T(8,128)(2,1)} custom-call(f32[2]{0:T(128)} %pad_maximum_fusion.6.scal, f32[512,128]{1,0:T(8,128)} %get-tuple-element.20.cos_ref, f32[512,128]{1,0:T(8,128)} %get-tuple-element.21.sin_ref, bf16[2,512,1024]{2,1,0:T(8,128)(2,1)} %bitcast.64, bf16[2,512,1024]{2,1,0:T(8,128)(2,1)} %bitcast.66, bf16[2,512,1024]{2,1,0:T(8,128)(2,1)} %bitcast.68, ...), custom_call_target="tpu_custom_call" | custom-call | tf_op jit(solution)/shard_map/pallas_call | solution.py:178
  149.7 49.3 %all-gather.6.cloned.1.call-done = bf16[2,1024,5120]{2,1,0:T(8,128)(2,1)} async-done(((bf16[2,1024,640]{2,1,0:T(8,128)(2,1)}), bf16[2,1024,5120]{2,1,0:T(8,128)(2,1)}) %all-gather.6.cloned.1.call-update) | async-done | bytes 20971536 | tf_op jit(solution)/shard_map/all_gather | solution.py:250
  199.0 3.3 fusion.3
  202.3 4.3 %fusion.2 = bf16[512,1280]{1,0:T(8,128)(2,1)} fusion(f32[512,1280]{1,0:T(8,128)S(1)} %fusion.3, bf16[512,1024]{1,0:T(8,128)(2,1)S(1)} %copy-done.9, bf16[2,1024,5120]{2,1,0:T(8,128)(2,1)} %all-gather.6.cloned.1.call-done), kind=kOutput, calls=%fused_computation.11 | convolution fusion | flops 1343488000 | bytes 7602176 | tf_op jit(solution)/shard_map/dot_general | solution.py:258
  206.7 3.7 all-to-all-start.6
  210.3 6.6 %fusion = f32[512,3840]{1,0:T(8,128)S(1)} fusion(bf16[512,1024]{1,0:T(8,128)(2,1)S(1)} %copy-done.9, bf16[2,1024,5120]{2,1,0:T(8,128)(2,1)} %all-gather.6.cloned.1.call-done), kind=kOutput, calls=%fused_computation.5 | convolution fusion | flops 4026531840 | bytes 16777216 | tf_op jit(solution)/shard_map/dot_general | solution.py:258
  216.9 9.2 %add_convert_fusion = bf16[512,3840]{1,0:T(8,128)(2,1)} fusion(f32[512,3840]{1,0:T(8,128)S(1)} %fusion, bf16[512,1024]{1,0:T(8,128)(2,1)S(1)} %copy-done.11, bf16[2,1024,5120]{2,1,0:T(8,128)(2,1)} %all-gather.6.cloned.1.call-done), kind=kOutput, calls=%fused_computation.9 | convolution fusion | flops 4030464000 | bytes 20709376 | tf_op jit(solution)/shard_map/dot_general | solution.py:256
  227.4 4.9 %all-to-all-start.7 = ((bf16[4,128,3840]{2,1,0:T(8,128)(2,1)}), bf16[4,128,3840]{2,1,0:T(8,128)(2,1)}, u32[]{:S(2)}, u32[]{:S(2)}) async-start(bf16[4,128,3840]{2,1,0:T(8,128)(2,1)} %bitcast.78), calls=%async_computation.7 | async-start | bytes 7864320 | tf_op jit(solution)/shard_map/all_to_all | solution.py:259
  232.9 43.9 %all-to-all-done.7 = bf16[4,128,3840]{2,1,0:T(8,128)(2,1)} async-done(((bf16[4,128,3840]{2,1,0:T(8,128)(2,1)}), bf16[4,128,3840]{2,1,0:T(8,128)(2,1)}, u32[]{:S(2)}, u32[]{:S(2)}) %all-to-all-start.7) | async-done | bytes 3932192 | tf_op jit(solution)/shard_map/all_to_all | solution.py:259
  276.7 2.9 convert_reduce_fusion.2
  282.4 18.4 %all_to_all.134 = bf16[128,8,256]{2,0,1:T(8,128)(2,1)} all-to-all(bf16[128,8,256]{2,0,1:T(8,128)(2,1)S(1)} %copy.63), channel_id=1, replica_groups=mesh['dp'=8,'tensor'=4] {'dp'}, dimensions={1} | all-to-all | bytes 1048576 | tf_op jit(solution)/shard_map/all_to_all | solution.py:281
  301.3 24.1 %all_to_all.135 = bf16[128,8,384]{2,0,1:T(8,128)(2,1)} all-to-all(bf16[128,8,384]{2,0,1:T(8,128)(2,1)S(1)} %copy.64), channel_id=1, replica_groups=mesh['dp'=8,'tensor'=4] {'dp'}, dimensions={1} | all-to-all | bytes 1572864 | tf_op jit(solution)/shard_map/all_to_all | solution.py:281
  325.4 8.8 %all-gather.8.cloned.1.call-done = bf16[512,8,256]{2,0,1:T(8,128)(2,1)} async-done(((bf16[128,8,256]{2,0,1:T(8,128)(2,1)}), bf16[512,8,256]{2,0,1:T(8,128)(2,1)}) %all-gather.8.cloned.1.call-update) | async-done | bytes 2097168 | tf_op jit(solution)/shard_map/all_gather | solution.py:284
  334.2 6.9 %convert_reduce_fusion.1 = f32[1024,256]{1,0:T(8,128)S(1)} fusion(bf16[8,512,1024]{2,1,0:T(8,128)(2,1)} %bitcast.84, bf16[512,8,256]{2,0,1:T(8,128)(2,1)} %all-gather.8.cloned.1.call-done), kind=kOutput, calls=%fused_computation.2 | convolution fusion | flops 2155610112 | bytes 11534336 | tf_op jit(solution)/shard_map/csi,scd->cid/dot_general | solution.py:285
  341.1 38.8 %all-gather.10.cloned.1.call-done = bf16[512,8,384]{2,0,1:T(8,128)(2,1)} async-done(((bf16[128,8,384]{2,0,1:T(8,128)(2,1)}), bf16[512,8,384]{2,0,1:T(8,128)(2,1)}) %all-gather.10.cloned.1.call-update) | async-done | bytes 3145744 | tf_op jit(solution)/shard_map/all_gather | solution.py:284
  379.9 8.9 %convert_reduce_fusion = f32[1024,384]{1,0:T(8,128)S(1)} fusion(bf16[8,512,1024]{2,1,0:T(8,128)(2,1)} %bitcast.85, bf16[512,8,384]{2,0,1:T(8,128)(2,1)} %all-gather.10.cloned.1.call-done), kind=kOutput, calls=%fused_computation | convolution fusion | flops 3233415168 | bytes 13107200 | tf_op jit(solution)/shard_map/csi,scd->cid/dot_general | solution.py:285
  (62 shorter events, 25.6 us)
Async XLA Ops:
  7.2 191.8 %all-gather.6.cloned.1.call-start = ((), (), s32[]{:S(2)}) async-start(), calls=%async_computation.10 | async-start | bytes 23592960 | tf_op jit(solution)/shard_map/all_gather | solution.py:250
  10.7 1.2 copy-start.7
  11.9 7.2 %copy-start.8 = (bf16[1,128,4096]{2,1,0:T(8,128)(2,1)S(1)}, bf16[1,128,4096]{2,1,0:T(8,128)(2,1)}, u32[]{:S(2)}) copy-start(bf16[1,128,4096]{2,1,0:T(8,128)(2,1)} %param.25) | copy-start | bytes 3145732
  14.0 18.8 %all-to-all-start.2 = ((bf16[128,4,1024]{2,0,1:T(8,128)(2,1)}), bf16[128,4,1024]{2,0,1:T(8,128)(2,1)S(1)}, u32[]{:S(2)}, u32[]{:S(2)}) async-start(bf16[128,4,1024]{2,0,1:T(8,128)(2,1)} %copy.52), calls=%async_computation.2 | async-start | bytes 2097152 | tf_op jit(solution)/shard_map/all_to_all | solution.py:222
  32.8 6.7 %copy-start = (bf16[128,4,1024]{2,0,1:T(8,128)(2,1)}, bf16[128,4,1024]{2,0,1:T(8,128)(2,1)S(1)}, u32[]{:S(2)}) copy-start(bf16[128,4,1024]{2,0,1:T(8,128)(2,1)S(1)} %all-to-all-done.2) | copy-start | bytes 3145732
  32.8 16.7 %all-to-all-start.3 = ((bf16[128,4,1024]{2,0,1:T(8,128)(2,1)}), bf16[128,4,1024]{2,0,1:T(8,128)(2,1)S(1)}, u32[]{:S(2)}, u32[]{:S(2)}) async-start(bf16[128,4,1024]{2,0,1:T(8,128)(2,1)} %copy.53), calls=%async_computation.3 | async-start | bytes 2097152 | tf_op jit(solution)/shard_map/all_to_all | solution.py:222
  49.5 6.8 %copy-start.1 = (bf16[128,4,1024]{2,0,1:T(8,128)(2,1)}, bf16[128,4,1024]{2,0,1:T(8,128)(2,1)S(1)}, u32[]{:S(2)}) copy-start(bf16[128,4,1024]{2,0,1:T(8,128)(2,1)S(1)} %all-to-all-done.3) | copy-start | bytes 3145732
  49.5 16.7 %all-to-all-start.4 = ((bf16[128,4,1024]{2,0,1:T(8,128)(2,1)}), bf16[128,4,1024]{2,0,1:T(8,128)(2,1)S(1)}, u32[]{:S(2)}, u32[]{:S(2)}) async-start(bf16[128,4,1024]{2,0,1:T(8,128)(2,1)} %copy.54), calls=%async_computation.4 | async-start | bytes 2097152 | tf_op jit(solution)/shard_map/all_to_all | solution.py:222
  66.2 6.7 %copy-start.2 = (bf16[128,4,1024]{2,0,1:T(8,128)(2,1)}, bf16[128,4,1024]{2,0,1:T(8,128)(2,1)S(1)}, u32[]{:S(2)}) copy-start(bf16[128,4,1024]{2,0,1:T(8,128)(2,1)S(1)} %all-to-all-done.4) | copy-start | bytes 3145732
  66.2 16.7 %all-to-all-start.5 = ((bf16[128,4,1024]{2,0,1:T(8,128)(2,1)}), bf16[128,4,1024]{2,0,1:T(8,128)(2,1)S(1)}, u32[]{:S(2)}, u32[]{:S(2)}) async-start(bf16[128,4,1024]{2,0,1:T(8,128)(2,1)} %copy.55), calls=%async_computation.5 | async-start | bytes 2097152 | tf_op jit(solution)/shard_map/all_to_all | solution.py:222
  82.8 7.6 %copy-start.3 = (bf16[128,4,1024]{2,0,1:T(8,128)(2,1)}, bf16[128,4,1024]{2,0,1:T(8,128)(2,1)S(1)}, u32[]{:S(2)}) copy-start(bf16[128,4,1024]{2,0,1:T(8,128)(2,1)S(1)} %all-to-all-done.5) | copy-start | bytes 3145732
  82.8 16.7 %all-to-all-start = ((bf16[128,4,1024]{2,0,1:T(8,128)(2,1)}), bf16[128,4,1024]{2,0,1:T(8,128)(2,1)S(1)}, u32[]{:S(2)}, u32[]{:S(2)}) async-start(bf16[128,4,1024]{2,0,1:T(8,128)(2,1)} %copy.50), calls=%async_computation | async-start | bytes 2097152 | tf_op jit(solution)/shard_map/all_to_all | solution.py:222
  89.0 14.9 %copy-start.10 = (s32[1,3,512]{2,0,1:T(1,128)S(1)}, s32[1,3,512]{2,0,1:T(1,128)}, u32[]{:S(2)}) copy-start(s32[1,3,512]{2,0,1:T(1,128)} %param.17) | copy-start | bytes 18436
  99.5 16.7 %copy-start.4 = (bf16[128,4,1024]{2,0,1:T(8,128)(2,1)}, bf16[128,4,1024]{2,0,1:T(8,128)(2,1)S(1)}, u32[]{:S(2)}) copy-start(bf16[128,4,1024]{2,0,1:T(8,128)(2,1)S(1)} %all-to-all-done) | copy-start | bytes 3145732
  99.5 16.7 %all-to-all-start.1 = ((bf16[128,4,1024]{2,0,1:T(8,128)(2,1)}), bf16[128,4,1024]{2,0,1:T(8,128)(2,1)S(1)}, u32[]{:S(2)}, u32[]{:S(2)}) async-start(bf16[128,4,1024]{2,0,1:T(8,128)(2,1)} %copy.51), calls=%async_computation.1 | async-start | bytes 2097152 | tf_op jit(solution)/shard_map/all_to_all | solution.py:222
  103.0 222.4 %all-gather.12.cloned.1.call-start = ((), (), s32[]{:S(2)}) async-start(), calls=%async_computation.13 | async-start | bytes 9437184 | tf_op jit(solution)/shard_map/all_gather | solution.py:275
  116.2 1.0 copy-start.5
  134.4 64.6 %copy-start.11 = (bf16[512,1024]{1,0:T(8,128)(2,1)S(1)}, bf16[512,1024]{1,0:T(8,128)(2,1)}, u32[]{:S(2)}) copy-start(bf16[512,1024]{1,0:T(8,128)(2,1)} %get-tuple-element.6) | copy-start | bytes 3145732
  199.0 3.4 copy-start.9
  206.7 20.7 %all-to-all-start.6 = ((bf16[4,128,1280]{2,1,0:T(8,128)(2,1)}), bf16[4,128,1280]{2,1,0:T(8,128)(2,1)S(1)}, u32[]{:S(2)}, u32[]{:S(2)}) async-start(bf16[4,128,1280]{2,1,0:T(8,128)(2,1)} %bitcast.24), calls=%async_computation.6 | async-start | bytes 2621440 | tf_op jit(solution)/shard_map/all_to_all | solution.py:259
  227.3 5.4 %copy-start.6 = (bf16[1,128,5120]{2,1,0:T(8,128)(2,1)S(1)}, bf16[1,128,5120]{2,1,0:T(8,128)(2,1)}, u32[]{:S(2)}) copy-start(bf16[1,128,5120]{2,1,0:T(8,128)(2,1)} %param.18) | copy-start | bytes 3932164
  227.4 49.4 %all-to-all-start.7 = ((bf16[4,128,3840]{2,1,0:T(8,128)(2,1)}), bf16[4,128,3840]{2,1,0:T(8,128)(2,1)}, u32[]{:S(2)}, u32[]{:S(2)}) async-start(bf16[4,128,3840]{2,1,0:T(8,128)(2,1)} %bitcast.78), calls=%async_computation.7 | async-start | bytes 7864320 | tf_op jit(solution)/shard_map/all_to_all | solution.py:259
  232.3 101.9 %all-gather.8.cloned.1.call-start = ((), (), s32[]{:S(2)}) async-start(), calls=%async_computation.11 | async-start | bytes 2621440 | tf_op jit(solution)/shard_map/all_gather | solution.py:284
  300.8 79.1 %all-gather.10.cloned.1.call-start = ((), (), s32[]{:S(2)}) async-start(), calls=%async_computation.12 | async-start | bytes 3932160 | tf_op jit(solution)/shard_map/all_gather | solution.py:284
Sparse Core Ops, SparseCore 0:
  10.8 188.0 all-gather.5
  200.6 80.2 all-gather.11
  301.0 33.2 all-gather.7
  335.9 43.9 all-gather.9

commit v13 on v11

--- a/solution.py
+++ b/solution.py
@@ -274,6 +274,7 @@
     grad_scale = -2.0 / math.sqrt(clips * seq_whole)
     edges = (0, width * 2 // 5, width)
     split_target = target.reshape(seq_local, clips, width)
+    attended_rows = jnp.swapaxes(attended_all, 1, 2)
     pieces = []
     for part in range(2):
         columns = lax.all_to_all(
@@ -281,7 +282,7 @@
         )
         columns = lax.all_gather(columns, "tensor", axis=0, tiled=True)
         terms = jnp.einsum(
-            "csi,scd->cid", attended_all, columns, preferred_element_type=jnp.float32
+            "cis,scd->cid", attended_rows, columns, preferred_element_type=jnp.float32
         )
         pieces.append(jnp.sum((grad_scale * terms).astype(jnp.bfloat16).astype(jnp.float32), axis=0))
     gradient = jnp.concatenate(pieces, axis=1)

time: 398 us -> 398 us (level)
  no operation moved by 1% of the time
where the time goes in v13:
time: 398 us; the launch traced here: 397 us
  waiting for transfers between devices  203 us (51%)
  blocking collectives  42.5 us (11%)
  matrix products  39.3 us (10%)
  starting transfers between devices  31.9 us (8%)
  Pallas kernels  31.2 us (8%)
  local copies, waits for them, and re-layouts  20.5 us (5%)
  between operations  15.5 us (4%)
  other arithmetic  13.3 us (3%)
    all_to_all x6, waiting for transfers between devices, local(): lax.all_to_all(source[0], 'tensor', split_axis=1, concat_axis=0, tiled=True)  60.8 us
    all_gather x1, waiting for transfers between devices, local(): pieces = lax.all_gather(stacked, 'dp', axis=2, tiled=True)  49.3 us
    all_gather x2, waiting for transfers between devices, local(): columns = lax.all_gather(columns, 'tensor', axis=0, tiled=True)  47.6 us
    all_to_all x2, waiting for transfers between devices, local(): lax.all_to_all(partial_value.astype(jnp.bfloat16).reshape(groups, seq_loc...  45.1 us
    all_to_all x2, blocking collectives, local(): lax.all_to_all(split_target[:, :, edges[part]:edges[part + 1]], 'dp', spl...  42.5 us
    pallas_call x2, Pallas kernels, head_call(): pl.pallas_call(kernel, grid=(heads,), in_specs=in_specs, out_specs=[head_...  31.2 us
    all_to_all x6, starting transfers between devices, local(): lax.all_to_all(source[0], 'tensor', split_axis=1, concat_axis=0, tiled=True)  22.7 us
    all_to_all x12, local copies, waits for them, and re-layouts, local(): lax.all_to_all(source[0], 'tensor', split_axis=1, concat_axis=0, tiled=True)  16.9 us
  transfers between devices with their start and end apart: 12, of which 11 were waited for; matrix products, arithmetic and copies ran while one was open for 12% of the time, Pallas kernels for 8%

profile of v13, /device:TPU:0, one launch (start us, length us, event | category | flops | bytes accessed | tf_op | source)
XLA Modules:
  0.0 397.1 jit_solution(4793724174043922151)
XLA Ops:
  7.2 3.5 pad_maximum_fusion
  14.0 5.2 %all-to-all-start.2 = ((bf16[128,4,1024]{2,0,1:T(8,128)(2,1)}), bf16[128,4,1024]{2,0,1:T(8,128)(2,1)S(1)}, u32[]{:S(2)}, u32[]{:S(2)}) async-start(bf16[128,4,1024]{2,0,1:T(8,128)(2,1)} %copy.52), calls=%async_computation.2 | async-start | bytes 2097152 | tf_op jit(solution)/shard_map/all_to_all | solution.py:222
  21.3 11.5 %all-to-all-done.2 = bf16[128,4,1024]{2,0,1:T(8,128)(2,1)S(1)} async-done(((bf16[128,4,1024]{2,0,1:T(8,128)(2,1)}), bf16[128,4,1024]{2,0,1:T(8,128)(2,1)S(1)}, u32[]{:S(2)}, u32[]{:S(2)}) %all-to-all-start.2) | async-done | bytes 1048608 | tf_op jit(solution)/shard_map/all_to_all | solution.py:222
  32.8 3.5 all-to-all-start.3
  36.3 1.9 all_to_all.112
  39.5 10.0 %all-to-all-done.3 = bf16[128,4,1024]{2,0,1:T(8,128)(2,1)S(1)} async-done(((bf16[128,4,1024]{2,0,1:T(8,128)(2,1)}), bf16[128,4,1024]{2,0,1:T(8,128)(2,1)S(1)}, u32[]{:S(2)}, u32[]{:S(2)}) %all-to-all-start.3) | async-done | bytes 1048608 | tf_op jit(solution)/shard_map/all_to_all | solution.py:222
  49.5 3.5 all-to-all-start.4
  53.0 1.9 all_to_all.116
  56.3 9.9 %all-to-all-done.4 = bf16[128,4,1024]{2,0,1:T(8,128)(2,1)S(1)} async-done(((bf16[128,4,1024]{2,0,1:T(8,128)(2,1)}), bf16[128,4,1024]{2,0,1:T(8,128)(2,1)S(1)}, u32[]{:S(2)}, u32[]{:S(2)}) %all-to-all-start.4) | async-done | bytes 1048608 | tf_op jit(solution)/shard_map/all_to_all | solution.py:222
  66.2 3.5 all-to-all-start.5
  72.8 10.0 %all-to-all-done.5 = bf16[128,4,1024]{2,0,1:T(8,128)(2,1)S(1)} async-done(((bf16[128,4,1024]{2,0,1:T(8,128)(2,1)}), bf16[128,4,1024]{2,0,1:T(8,128)(2,1)S(1)}, u32[]{:S(2)}, u32[]{:S(2)}) %all-to-all-start.5) | async-done | bytes 1048608 | tf_op jit(solution)/shard_map/all_to_all | solution.py:222
  82.8 3.5 all-to-all-start
  90.4 9.1 %all-to-all-done = bf16[128,4,1024]{2,0,1:T(8,128)(2,1)S(1)} async-done(((bf16[128,4,1024]{2,0,1:T(8,128)(2,1)}), bf16[128,4,1024]{2,0,1:T(8,128)(2,1)S(1)}, u32[]{:S(2)}, u32[]{:S(2)}) %all-to-all-start) | async-done | bytes 1048608 | tf_op jit(solution)/shard_map/all_to_all | solution.py:222
  99.5 3.5 all-to-all-start.1
  106.0 10.2 %all-to-all-done.1 = bf16[128,4,1024]{2,0,1:T(8,128)(2,1)S(1)} async-done(((bf16[128,4,1024]{2,0,1:T(8,128)(2,1)}), bf16[128,4,1024]{2,0,1:T(8,128)(2,1)S(1)}, u32[]{:S(2)}, u32[]{:S(2)}) %all-to-all-start.1) | async-done | bytes 1048608 | tf_op jit(solution)/shard_map/all_to_all | solution.py:222
  117.2 15.9 %shard_map.158 = (bf16[512,1024]{1,0:T(8,128)(2,1)}, bf16[512,1024]{1,0:T(8,128)(2,1)}) custom-call(f32[2]{0:T(128)} %pad_maximum_fusion.5.scal, f32[512,128]{1,0:T(8,128)} %get-tuple-element.16.cos_ref, f32[512,128]{1,0:T(8,128)} %get-tuple-element.17.sin_ref, bf16[512,1024]{1,0:T(8,128)(2,1)} %bitcast.76, bf16[512,1024]{1,0:T(8,128)(2,1)} %bitcast.77, ...), custom_call_target="tpu_custom_call" | custom-call | tf_op jit(solution)/shard_map/pallas_call | solution.py:178
  134.4 15.3 %shard_map.159 = bf16[512,1024]{1,0:T(8,128)(2,1)} custom-call(f32[2]{0:T(128)} %pad_maximum_fusion.6.scal, f32[512,128]{1,0:T(8,128)} %get-tuple-element.16.cos_ref, f32[512,128]{1,0:T(8,128)} %get-tuple-element.17.sin_ref, bf16[2,512,1024]{2,1,0:T(8,128)(2,1)} %bitcast.64, bf16[2,512,1024]{2,1,0:T(8,128)(2,1)} %bitcast.66, bf16[2,512,1024]{2,1,0:T(8,128)(2,1)} %bitcast.68, ...), custom_call_target="tpu_custom_call" | custom-call | tf_op jit(solution)/shard_map/pallas_call | solution.py:178
  149.7 49.3 %all-gather.6.cloned.1.call-done = bf16[2,1024,5120]{2,1,0:T(8,128)(2,1)} async-done(((bf16[2,1024,640]{2,1,0:T(8,128)(2,1)}), bf16[2,1024,5120]{2,1,0:T(8,128)(2,1)}) %all-gather.6.cloned.1.call-update) | async-done | bytes 20971536 | tf_op jit(solution)/shard_map/all_gather | solution.py:250
  199.0 3.3 fusion.3
  202.3 4.3 %fusion.2 = bf16[512,1280]{1,0:T(8,128)(2,1)} fusion(f32[512,1280]{1,0:T(8,128)S(1)} %fusion.3, bf16[512,1024]{1,0:T(8,128)(2,1)S(1)} %copy-done.9, bf16[2,1024,5120]{2,1,0:T(8,128)(2,1)} %all-gather.6.cloned.1.call-done), kind=kOutput, calls=%fused_computation.11 | convolution fusion | flops 1343488000 | bytes 7602176 | tf_op jit(solution)/shard_map/dot_general | solution.py:258
  206.7 3.7 all-to-all-start.6
  210.3 6.6 %fusion = f32[512,3840]{1,0:T(8,128)S(1)} fusion(bf16[512,1024]{1,0:T(8,128)(2,1)S(1)} %copy-done.9, bf16[2,1024,5120]{2,1,0:T(8,128)(2,1)} %all-gather.6.cloned.1.call-done), kind=kOutput, calls=%fused_computation.5 | convolution fusion | flops 4026531840 | bytes 16777216 | tf_op jit(solution)/shard_map/dot_general | solution.py:258
  216.9 9.2 %add_convert_fusion = bf16[512,3840]{1,0:T(8,128)(2,1)} fusion(f32[512,3840]{1,0:T(8,128)S(1)} %fusion, bf16[512,1024]{1,0:T(8,128)(2,1)S(1)} %copy-done.11, bf16[2,1024,5120]{2,1,0:T(8,128)(2,1)} %all-gather.6.cloned.1.call-done), kind=kOutput, calls=%fused_computation.9 | convolution fusion | flops 4030464000 | bytes 20709376 | tf_op jit(solution)/shard_map/dot_general | solution.py:256
  227.4 4.9 %all-to-all-start.7 = ((bf16[4,128,3840]{2,1,0:T(8,128)(2,1)}), bf16[4,128,3840]{2,1,0:T(8,128)(2,1)}, u32[]{:S(2)}, u32[]{:S(2)}) async-start(bf16[4,128,3840]{2,1,0:T(8,128)(2,1)} %bitcast.78), calls=%async_computation.7 | async-start | bytes 7864320 | tf_op jit(solution)/shard_map/all_to_all | solution.py:259
  232.9 43.9 %all-to-all-done.7 = bf16[4,128,3840]{2,1,0:T(8,128)(2,1)} async-done(((bf16[4,128,3840]{2,1,0:T(8,128)(2,1)}), bf16[4,128,3840]{2,1,0:T(8,128)(2,1)}, u32[]{:S(2)}, u32[]{:S(2)}) %all-to-all-start.7) | async-done | bytes 3932192 | tf_op jit(solution)/shard_map/all_to_all | solution.py:259
  276.7 2.9 convert_reduce_fusion.2
  282.4 18.4 %all_to_all.134 = bf16[128,8,256]{2,0,1:T(8,128)(2,1)} all-to-all(bf16[128,8,256]{2,0,1:T(8,128)(2,1)S(1)} %copy.63), channel_id=1, replica_groups=mesh['dp'=8,'tensor'=4] {'dp'}, dimensions={1} | all-to-all | bytes 1048576 | tf_op jit(solution)/shard_map/all_to_all | solution.py:280
  301.3 24.1 %all_to_all.135 = bf16[128,8,384]{2,0,1:T(8,128)(2,1)} all-to-all(bf16[128,8,384]{2,0,1:T(8,128)(2,1)S(1)} %copy.64), channel_id=1, replica_groups=mesh['dp'=8,'tensor'=4] {'dp'}, dimensions={1} | all-to-all | bytes 1572864 | tf_op jit(solution)/shard_map/all_to_all | solution.py:280
  325.4 8.8 %all-gather.8.cloned.1.call-done = bf16[512,8,256]{2,0,1:T(8,128)(2,1)} async-done(((bf16[128,8,256]{2,0,1:T(8,128)(2,1)}), bf16[512,8,256]{2,0,1:T(8,128)(2,1)}) %all-gather.8.cloned.1.call-update) | async-done | bytes 2097168 | tf_op jit(solution)/shard_map/all_gather | solution.py:283
  334.2 6.9 %convert_reduce_fusion.1 = f32[1024,256]{1,0:T(8,128)S(1)} fusion(bf16[8,512,1024]{2,1,0:T(8,128)(2,1)} %bitcast.84, bf16[512,8,256]{2,0,1:T(8,128)(2,1)} %all-gather.8.cloned.1.call-done), kind=kOutput, calls=%fused_computation.2 | convolution fusion | flops 2155610112 | bytes 11534336 | tf_op jit(solution)/shard_map/cis,scd->cid/dot_general | solution.py:284
  341.1 38.8 %all-gather.10.cloned.1.call-done = bf16[512,8,384]{2,0,1:T(8,128)(2,1)} async-done(((bf16[128,8,384]{2,0,1:T(8,128)(2,1)}), bf16[512,8,384]{2,0,1:T(8,128)(2,1)}) %all-gather.10.cloned.1.call-update) | async-done | bytes 3145744 | tf_op jit(solution)/shard_map/all_gather | solution.py:283
  379.9 8.9 %convert_reduce_fusion = f32[1024,384]{1,0:T(8,128)S(1)} fusion(bf16[8,512,1024]{2,1,0:T(8,128)(2,1)} %bitcast.85, bf16[512,8,384]{2,0,1:T(8,128)(2,1)} %all-gather.10.cloned.1.call-done), kind=kOutput, calls=%fused_computation | convolution fusion | flops 3233415168 | bytes 13107200 | tf_op jit(solution)/shard_map/cis,scd->cid/dot_general | solution.py:284
  (62 shorter events, 25.6 us)
Async XLA Ops:
  7.2 191.8 %all-gather.6.cloned.1.call-start = ((), (), s32[]{:S(2)}) async-start(), calls=%async_computation.10 | async-start | bytes 23592960 | tf_op jit(solution)/shard_map/all_gather | solution.py:250
  10.7 1.2 copy-start.7
  11.9 7.2 %copy-start.8 = (bf16[1,128,4096]{2,1,0:T(8,128)(2,1)S(1)}, bf16[1,128,4096]{2,1,0:T(8,128)(2,1)}, u32[]{:S(2)}) copy-start(bf16[1,128,4096]{2,1,0:T(8,128)(2,1)} %param.25) | copy-start | bytes 3145732
  14.0 18.8 %all-to-all-start.2 = ((bf16[128,4,1024]{2,0,1:T(8,128)(2,1)}), bf16[128,4,1024]{2,0,1:T(8,128)(2,1)S(1)}, u32[]{:S(2)}, u32[]{:S(2)}) async-start(bf16[128,4,1024]{2,0,1:T(8,128)(2,1)} %copy.52), calls=%async_computation.2 | async-start | bytes 2097152 | tf_op jit(solution)/shard_map/all_to_all | solution.py:222
  32.8 6.7 %copy-start = (bf16[128,4,1024]{2,0,1:T(8,128)(2,1)}, bf16[128,4,1024]{2,0,1:T(8,128)(2,1)S(1)}, u32[]{:S(2)}) copy-start(bf16[128,4,1024]{2,0,1:T(8,128)(2,1)S(1)} %all-to-all-done.2) | copy-start | bytes 3145732
  32.8 16.7 %all-to-all-start.3 = ((bf16[128,4,1024]{2,0,1:T(8,128)(2,1)}), bf16[128,4,1024]{2,0,1:T(8,128)(2,1)S(1)}, u32[]{:S(2)}, u32[]{:S(2)}) async-start(bf16[128,4,1024]{2,0,1:T(8,128)(2,1)} %copy.53), calls=%async_computation.3 | async-start | bytes 2097152 | tf_op jit(solution)/shard_map/all_to_all | solution.py:222
  49.5 6.8 %copy-start.1 = (bf16[128,4,1024]{2,0,1:T(8,128)(2,1)}, bf16[128,4,1024]{2,0,1:T(8,128)(2,1)S(1)}, u32[]{:S(2)}) copy-start(bf16[128,4,1024]{2,0,1:T(8,128)(2,1)S(1)} %all-to-all-done.3) | copy-start | bytes 3145732
  49.5 16.7 %all-to-all-start.4 = ((bf16[128,4,1024]{2,0,1:T(8,128)(2,1)}), bf16[128,4,1024]{2,0,1:T(8,128)(2,1)S(1)}, u32[]{:S(2)}, u32[]{:S(2)}) async-start(bf16[128,4,1024]{2,0,1:T(8,128)(2,1)} %copy.54), calls=%async_computation.4 | async-start | bytes 2097152 | tf_op jit(solution)/shard_map/all_to_all | solution.py:222
  66.2 6.7 %copy-start.2 = (bf16[128,4,1024]{2,0,1:T(8,128)(2,1)}, bf16[128,4,1024]{2,0,1:T(8,128)(2,1)S(1)}, u32[]{:S(2)}) copy-start(bf16[128,4,1024]{2,0,1:T(8,128)(2,1)S(1)} %all-to-all-done.4) | copy-start | bytes 3145732
  66.2 16.7 %all-to-all-start.5 = ((bf16[128,4,1024]{2,0,1:T(8,128)(2,1)}), bf16[128,4,1024]{2,0,1:T(8,128)(2,1)S(1)}, u32[]{:S(2)}, u32[]{:S(2)}) async-start(bf16[128,4,1024]{2,0,1:T(8,128)(2,1)} %copy.55), calls=%async_computation.5 | async-start | bytes 2097152 | tf_op jit(solution)/shard_map/all_to_all | solution.py:222
  82.8 7.6 %copy-start.3 = (bf16[128,4,1024]{2,0,1:T(8,128)(2,1)}, bf16[128,4,1024]{2,0,1:T(8,128)(2,1)S(1)}, u32[]{:S(2)}) copy-start(bf16[128,4,1024]{2,0,1:T(8,128)(2,1)S(1)} %all-to-all-done.5) | copy-start | bytes 3145732
  82.8 16.7 %all-to-all-start = ((bf16[128,4,1024]{2,0,1:T(8,128)(2,1)}), bf16[128,4,1024]{2,0,1:T(8,128)(2,1)S(1)}, u32[]{:S(2)}, u32[]{:S(2)}) async-start(bf16[128,4,1024]{2,0,1:T(8,128)(2,1)} %copy.50), calls=%async_computation | async-start | bytes 2097152 | tf_op jit(solution)/shard_map/all_to_all | solution.py:222
  89.0 14.9 %copy-start.10 = (s32[1,3,512]{2,0,1:T(1,128)S(1)}, s32[1,3,512]{2,0,1:T(1,128)}, u32[]{:S(2)}) copy-start(s32[1,3,512]{2,0,1:T(1,128)} %param.17) | copy-start | bytes 18436
  99.5 16.7 %copy-start.4 = (bf16[128,4,1024]{2,0,1:T(8,128)(2,1)}, bf16[128,4,1024]{2,0,1:T(8,128)(2,1)S(1)}, u32[]{:S(2)}) copy-start(bf16[128,4,1024]{2,0,1:T(8,128)(2,1)S(1)} %all-to-all-done) | copy-start | bytes 3145732
  99.5 16.7 %all-to-all-start.1 = ((bf16[128,4,1024]{2,0,1:T(8,128)(2,1)}), bf16[128,4,1024]{2,0,1:T(8,128)(2,1)S(1)}, u32[]{:S(2)}, u32[]{:S(2)}) async-start(bf16[128,4,1024]{2,0,1:T(8,128)(2,1)} %copy.51), calls=%async_computation.1 | async-start | bytes 2097152 | tf_op jit(solution)/shard_map/all_to_all | solution.py:222
  103.0 222.4 %all-gather.12.cloned.1.call-start = ((), (), s32[]{:S(2)}) async-start(), calls=%async_computation.13 | async-start | bytes 9437184 | tf_op jit(solution)/shard_map/all_gather | solution.py:273
  116.2 1.0 copy-start.5
  134.4 64.6 %copy-start.11 = (bf16[512,1024]{1,0:T(8,128)(2,1)S(1)}, bf16[512,1024]{1,0:T(8,128)(2,1)}, u32[]{:S(2)}) copy-start(bf16[512,1024]{1,0:T(8,128)(2,1)} %get-tuple-element.4) | copy-start | bytes 3145732
  199.0 3.4 copy-start.9
  206.7 20.7 %all-to-all-start.6 = ((bf16[4,128,1280]{2,1,0:T(8,128)(2,1)}), bf16[4,128,1280]{2,1,0:T(8,128)(2,1)S(1)}, u32[]{:S(2)}, u32[]{:S(2)}) async-start(bf16[4,128,1280]{2,1,0:T(8,128)(2,1)} %bitcast.24), calls=%async_computation.6 | async-start | bytes 2621440 | tf_op jit(solution)/shard_map/all_to_all | solution.py:259
  227.3 5.4 %copy-start.6 = (bf16[1,128,5120]{2,1,0:T(8,128)(2,1)S(1)}, bf16[1,128,5120]{2,1,0:T(8,128)(2,1)}, u32[]{:S(2)}) copy-start(bf16[1,128,5120]{2,1,0:T(8,128)(2,1)} %param.18) | copy-start | bytes 3932164
  227.4 49.4 %all-to-all-start.7 = ((bf16[4,128,3840]{2,1,0:T(8,128)(2,1)}), bf16[4,128,3840]{2,1,0:T(8,128)(2,1)}, u32[]{:S(2)}, u32[]{:S(2)}) async-start(bf16[4,128,3840]{2,1,0:T(8,128)(2,1)} %bitcast.78), calls=%async_computation.7 | async-start | bytes 7864320 | tf_op jit(solution)/shard_map/all_to_all | solution.py:259
  232.3 101.9 %all-gather.8.cloned.1.call-start = ((), (), s32[]{:S(2)}) async-start(), calls=%async_computation.11 | async-start | bytes 2621440 | tf_op jit(solution)/shard_map/all_gather | solution.py:283
  300.8 79.1 %all-gather.10.cloned.1.call-start = ((), (), s32[]{:S(2)}) async-start(), calls=%async_computation.12 | async-start | bytes 3932160 | tf_op jit(solution)/shard_map/all_gather | solution.py:283
Sparse Core Ops, SparseCore 0:
  10.8 188.0 all-gather.5
  200.6 80.2 all-gather.11
  301.0 33.2 all-gather.7
  335.9 43.9 all-gather.9
